TPU v7x, 256 devices: a whole 4x4x8 slice. The times are simulated.
256 devices in a mesh: dp: 64 (over z, x, core), mp: 4 (over y).
Axes of the slice: x: 4, y: 4, z: 8, core: 2. Of those that a mesh axis runs over, the one named last changes fastest.
Arguments:
- embed_table: float32 [16, 32768, 256], P('mp', 'dp'), may hold values from -5 to 5
- accum: float32 [16, 32768], P('mp', 'dp'), may hold values from 0.1 to 3
- stale_grad: bfloat16 [16, 32768, 256], P('mp', 'dp'), may hold values from -6 to 6
- grad_owner: int32 [16, 32768, 1], P('mp', 'dp'), may hold values from 0 to 63; in each aligned block of 512 rows (0 to 511, 512 to 1023, ..., all dimensions but the last counted through in order) at most 16 rows name the same one
- grad_row: int32 [16, 32768], P('mp', 'dp'), may hold values from 0 to 511
- lookup_owner: int32 [16, 32768, 1], P('mp', 'dp'), may hold values from 0 to 63; in each aligned block of 512 rows (0 to 511, 512 to 1023, ..., all dimensions but the last counted through in order) at most 16 rows name the same one
- lookup_row: int32 [16, 32768], P('mp', 'dp'), may hold values from 0 to 511
- bag_len: int32 [16, 16384], P('mp', 'dp'), may hold values from 1 to 2
- label: int32 [16384], P('dp'), may hold values 0 or 1
- up_factor_weight: bfloat16 [2, 512, 4096], P(None, None, 'mp'), may hold values from -0.25 to 0.25
- v_weight: bfloat16 [2, 512, 4096], P(None, None, 'mp'), may hold values from -0.09375 to 0.09375
- cross_bias: float32 [2, 4096], P(None, 'mp'), may hold values from -3 to 3
- head_weight: float32 [4096], P('mp'), may hold values from -0.09375 to 0.09375
Outputs:
- new_table: float32 [16, 32768, 256], P('mp', 'dp')
- new_accum: float32 [16, 32768], P('mp', 'dp')
- grad_u: float32 [2, 512, 4096], P(None, 'dp', 'mp')
- grad_v: float32 [2, 512, 4096], P(None, 'dp', 'mp')
- grad_small: float32 [3, 4096], P(None, 'mp')
- grad_pooled: bfloat16 [16384, 4096], P('dp', 'mp')
Inputs may be any that keep to these rules, and one draw needn't show every extreme that they name: `grad_owner`: among the 512 blocks of one feature held by one index of dp, at most 16 name the same owner, and in some such group exactly 16 do. `lookup_owner`: among the 512 id slots of one feature belonging to one index of dp, at most 16 name the same owner, and in some such group exactly 16 do; slots k >= bag_len are unused.
All inputs are finite; a program needn't handle non-finite values. No bound on the sum of `label` on one device may be relied on, other than what follows from the above.
Results may differ from a plain program's by a relative error of at most 0.009.
Values may be sent and summed in bfloat16 or wider, within the bound.
No kernel may reach another device: no remote copies, remote signals or barrier semaphores. Data moves between devices by JAX's collectives and lax.ppermute only.
A program may use at most 128 MiB of HBM per device.

v0:
```python
import jax
import jax.numpy as jnp
from jax import lax
from jax.sharding import PartitionSpec as P

learn_rate = 0.5


def in_blocks(array, dim, devices):
    shape = array.shape
    parts = array.reshape(*shape[:dim], devices, shape[dim] // devices, *shape[dim + 1 :])
    return jnp.moveaxis(parts, dim, 0)


def sum_at_owner(array, axis, dim):
    parts = in_blocks(array, dim, lax.axis_size(axis))
    arrived = lax.all_to_all(parts, axis, split_axis=0, concat_axis=0, tiled=True)
    return arrived.sum(axis=0)


def copy_for_each(array, axis):
    copies = jnp.broadcast_to(array, (lax.axis_size(axis), *array.shape))
    return lax.all_to_all(copies, axis, split_axis=0, concat_axis=0, tiled=True)


def over_copies(array, axis):
    return copy_for_each(array, axis).sum(axis=0)


def side_by_side(arrays, axis, dim, along):
    widths = [a.shape[along] for a in arrays]
    both = jnp.concatenate(arrays, axis=along)
    filled = lax.psum_scatter(both, axis, scatter_dimension=dim, tiled=True)
    return tuple(jnp.split(filled, [sum(widths[:k]) for k in range(1, len(widths))], axis=along))


def bucket_slots(owners, capacity, peers):
    count = owners.shape[1]
    onehot = (owners[:, None, :] == jnp.arange(peers)[None, :, None]).astype(jnp.bfloat16)
    earlier = (jnp.arange(count)[:, None] < jnp.arange(count)[None, :]).astype(jnp.bfloat16)
    before = jnp.einsum("fpi,ij->fpj", onehot, earlier, preferred_element_type=jnp.float32)
    order_in = jnp.sum(before * onehot.astype(jnp.float32), axis=1)
    return owners * capacity + order_in.astype(jnp.int32)


def selection_matrix(indices, length):
    return (indices[:, :, None] == jnp.arange(length)[None, None, :]).astype(jnp.bfloat16)


def contract_last(left, right):
    return lax.dot_general(
        left, right, (((1,), (1,)), ((), ())), preferred_element_type=jnp.float32
    )


def contract_first(left, right):
    return lax.dot_general(
        left, right, (((0,), (0,)), ((), ())), preferred_element_type=jnp.float32
    )


def cross_down(state, v_layer):
    share = sum_at_owner(contract_last(state, v_layer), "mp", 0)
    return lax.all_gather(share.astype(jnp.bfloat16), "mp", axis=0, tiled=True)


def local(
    embed_table,
    accum,
    stale_grad,
    grad_owner,
    grad_row,
    lookup_owner,
    lookup_row,
    bag_len,
    label,
    up_factor_weight,
    v_weight,
    cross_bias,
    head_weight,
):
    peers = lax.axis_size("dp")
    local_feats, grad_dev, width = stale_grad.shape
    rows_per_shard = embed_table.shape[1]
    which_feature = jnp.arange(local_feats)[:, None]
    grad_cap = max(2, 2 * grad_dev // peers)
    grad_total = peers * grad_cap
    grad_slot = bucket_slots(grad_owner[:, :, 0], grad_cap, peers)
    place = selection_matrix(grad_slot, grad_total)
    send_grads = jnp.einsum(
        "fns,fne->fse", place, stale_grad, preferred_element_type=jnp.float32
    ).astype(jnp.bfloat16)
    send_rows = (
        jnp.full((local_feats, grad_total), rows_per_shard, jnp.int32)
        .at[which_feature, grad_slot]
        .set(grad_row)
    )
    recv_grads = lax.all_to_all(
        send_grads.reshape(local_feats, peers, grad_cap, width),
        "dp",
        split_axis=1,
        concat_axis=1,
        tiled=True,
    )
    recv_rows = lax.all_to_all(
        send_rows.reshape(local_feats, peers, grad_cap),
        "dp",
        split_axis=1,
        concat_axis=1,
        tiled=True,
    )
    landing = selection_matrix(recv_rows.reshape(local_feats, grad_total), rows_per_shard)
    summed = jnp.einsum(
        "wjc,wjl->wcl",
        landing,
        recv_grads.reshape(local_feats, grad_total, width),
        preferred_element_type=jnp.float32,
    )
    new_accum = accum + jnp.mean(summed * summed, axis=2)
    new_table = embed_table - learn_rate * summed / jnp.sqrt(new_accum)[:, :, None]
    batch_dev = bag_len.shape[1]
    look_dev = lookup_row.shape[1]
    bag_size = look_dev // batch_dev
    look_cap = max(2, 2 * look_dev // peers)
    look_total = peers * look_cap
    look_slot = bucket_slots(lookup_owner[:, :, 0], look_cap, peers)
    wanted = (
        jnp.zeros((local_feats, look_total), jnp.int32).at[which_feature, look_slot].set(lookup_row)
    )
    requested_ids = lax.all_to_all(
        wanted.reshape(local_feats, peers, look_cap), "dp", split_axis=1, concat_axis=1, tiled=True
    ).reshape(local_feats, look_total)
    second_table = embed_table.astype(jnp.bfloat16)
    served = jnp.einsum(
        "adv,avm->adm",
        selection_matrix(requested_ids, rows_per_shard),
        second_table,
        preferred_element_type=jnp.float32,
    ).astype(jnp.bfloat16)
    returned = lax.all_to_all(
        served.reshape(local_feats, peers, look_cap, width),
        "dp",
        split_axis=1,
        concat_axis=1,
        tiled=True,
    ).reshape(local_feats, look_total, width)
    slots = look_slot.reshape(local_feats, batch_dev, bag_size)
    mixing = jnp.zeros((local_feats, batch_dev, look_total), jnp.bfloat16)
    for member in range(bag_size):
        used = (bag_len > member).astype(jnp.bfloat16)
        mixing = mixing + selection_matrix(slots[:, :, member], look_total) * used[:, :, None]
    pooled = jnp.einsum(
        "fbs,fse->fbe", mixing, returned, preferred_element_type=jnp.float32
    ).astype(jnp.bfloat16)
    start = jnp.transpose(pooled, (1, 0, 2)).reshape(batch_dev, local_feats * width)
    start_f = start.astype(jnp.float32)
    n_layers = up_factor_weight.shape[0]
    state = start
    states = []
    downs = []
    crosses = []
    for layer in range(n_layers):
        down_sum = cross_down(state, v_weight[layer])
        cross_out = (
            jnp.dot(down_sum, up_factor_weight[layer], preferred_element_type=jnp.float32)
            + cross_bias[layer]
        )
        states.append(state)
        downs.append(down_sum)
        crosses.append(cross_out)
        state = (start_f * cross_out + state.astype(jnp.float32)).astype(jnp.bfloat16)
    logit = lax.psum(jnp.sum(state.astype(jnp.float32) * head_weight[None, :], axis=1), "mp")
    slope = (jax.nn.sigmoid(logit) - label.astype(jnp.float32)) / jnp.sqrt(
        jnp.float32(batch_dev * peers)
    )
    upstream = slope[:, None] * head_weight[None, :]
    head_grad = jnp.sum(slope[:, None] * state.astype(jnp.float32), axis=0)
    to_start = jnp.zeros(start_f.shape, jnp.float32)
    grads_u = [None] * n_layers
    grads_v = [None] * n_layers
    bias_grads = [None] * n_layers
    for layer in reversed(range(n_layers)):
        direct = upstream * start_f
        bias_grads[layer] = jnp.sum(direct, axis=0)
        direct_bias_term = direct.astype(jnp.bfloat16)
        grad_u_layer = contract_first(downs[layer], direct_bias_term)
        back_sum = over_copies(
            contract_last(direct_bias_term, up_factor_weight[layer]), "mp"
        ).astype(jnp.bfloat16)
        down_factor_gradient = contract_first(back_sum, states[layer])
        to_start = to_start + upstream * crosses[layer]
        upstream = upstream + jnp.dot(back_sum, v_weight[layer], preferred_element_type=jnp.float32)
        grads_u[layer] = grad_u_layer
        grads_v[layer] = down_factor_gradient
    grad_u = jnp.stack(grads_u)
    grad_v = jnp.stack(grads_v)
    grad_u, grad_v = side_by_side((grad_u, grad_v), "dp", 1, 0)
    grad_small = over_copies(jnp.stack(bias_grads + [head_grad]), "dp")
    grad_pooled = (upstream + to_start).astype(jnp.bfloat16)
    return (new_table, new_accum, grad_u, grad_v, grad_small, grad_pooled)


def solution(mesh):
    return jax.shard_map(
        local,
        mesh=mesh,
        in_specs=(
            P("mp", "dp", None),
            P("mp", "dp"),
            P("mp", "dp", None),
            P("mp", "dp", None),
            P("mp", "dp"),
            P("mp", "dp", None),
            P("mp", "dp"),
            P("mp", "dp"),
            P("dp"),
            P(None, None, "mp"),
            P(None, None, "mp"),
            P(None, "mp"),
            P("mp"),
        ),
        out_specs=(
            P("mp", "dp", None),
            P("mp", "dp"),
            P(None, "dp", "mp"),
            P(None, "dp", "mp"),
            P(None, "mp"),
            P("dp", "mp"),
        ),
        check_vma=False,
    )
```

profile of v0, /device:TPU:8, one launch (start us, length us, event | category | flops | bytes accessed | tf_op | source)
XLA Modules:
  0.0 404.8 jit_solution(2929955920425047007)
XLA Ops:
  10.6 8.1 %scatter_custom_fusion.1 = s32[4096]{0:T(1024)S(1)} fusion(s32[2048]{0:T(1024)S(1)} %bitcast.115, s32[2048]{0:T(1024)S(1)} %bitcast.117, s32[]{:T(128)} %constant.5.clone.1), kind=kCustom, calls=%fused_computation.109 | custom fusion | bytes 16388
  18.9 22.8 %all_to_all.45 = s32[4,64,16]{2,0,1:T(4,128)S(1)} all-to-all(s32[4,64,16]{2,0,1:T(4,128)S(1)} %copy.81), channel_id=1, replica_groups=mesh['dp'=64,'mp'=4] {'dp'}, dimensions={1} | all-to-all | bytes 32768 | tf_op jit(solution)/shard_map/all_to_all | solution.py:130
  41.8 2.1 fusion.14
  43.9 1.6 copy.83
  45.5 4.7 %all-to-all-start.3 = ((bf16[4,64,16,256]{3,2,0,1:T(8,128)(2,1)}), bf16[4,64,16,256]{3,2,0,1:T(8,128)(2,1)S(1)}, u32[]{:S(2)}, u32[]{:S(2)}) async-start(bf16[4,64,16,256]{3,2,0,1:T(8,128)(2,1)} %copy.83), calls=%async_computation.3 | async-start | bytes 4194304 | tf_op jit(solution)/shard_map/all_to_all | solution.py:140
  52.7 48.8 %all-to-all-done.3 = bf16[4,64,16,256]{3,2,0,1:T(8,128)(2,1)S(1)} async-done(((bf16[4,64,16,256]{3,2,0,1:T(8,128)(2,1)}), bf16[4,64,16,256]{3,2,0,1:T(8,128)(2,1)S(1)}, u32[]{:S(2)}, u32[]{:S(2)}) %all-to-all-start.3) | async-done | bytes 2097184 | tf_op jit(solution)/shard_map/all_to_all | solution.py:140
  101.7 2.1 fusion.17
  104.5 2.5 fusion.39
  107.0 4.9 %all-to-all-start.4 = ((f32[4,64,512]{2,1,0:T(8,128)}), f32[4,64,512]{2,1,0:T(8,128)S(1)}, u32[]{:S(2)}, u32[]{:S(2)}) async-start(f32[4,64,512]{2,1,0:T(8,128)} %fusion.39), calls=%async_computation.4 | async-start | bytes 1048576 | tf_op jit(solution)/shard_map/all_to_all | solution.py:17
  112.1 6.4 %all-to-all-done.4 = f32[4,64,512]{2,1,0:T(8,128)S(1)} async-done(((f32[4,64,512]{2,1,0:T(8,128)}), f32[4,64,512]{2,1,0:T(8,128)S(1)}, u32[]{:S(2)}, u32[]{:S(2)}) %all-to-all-start.4) | async-done | bytes 524320 | tf_op jit(solution)/shard_map/all_to_all | solution.py:17
  118.6 11.8 %all_gather.6 = bf16[256,512]{1,0:T(8,128)(2,1)S(1)} all-gather(bf16[64,512]{1,0:T(8,128)(2,1)S(1)} %reduce_sum.111), channel_id=1, replica_groups=mesh['dp'=64,'mp'=4] {'mp'}, dimensions={0}, use_global_device_ids=true | all-gather | bytes 327680 | tf_op jit(solution)/shard_map/all_gather | solution.py:64
  130.4 2.8 fusion.26
  133.1 1.3 fusion.33
  134.4 5.5 %all-to-all-start.5 = ((f32[4,64,512]{2,1,0:T(8,128)}), f32[4,64,512]{2,1,0:T(8,128)S(1)}, u32[]{:S(2)}, u32[]{:S(2)}) async-start(f32[4,64,512]{2,1,0:T(8,128)} %fusion.33), calls=%async_computation.5 | async-start | bytes 1048576 | tf_op jit(solution)/shard_map/all_to_all | solution.py:17
  139.9 7.3 %all-to-all-done.5 = f32[4,64,512]{2,1,0:T(8,128)S(1)} async-done(((f32[4,64,512]{2,1,0:T(8,128)}), f32[4,64,512]{2,1,0:T(8,128)S(1)}, u32[]{:S(2)}, u32[]{:S(2)}) %all-to-all-start.5) | async-done | bytes 524320 | tf_op jit(solution)/shard_map/all_to_all | solution.py:17
  147.3 11.6 %all_gather.7 = bf16[256,512]{1,0:T(8,128)(2,1)S(1)} all-gather(bf16[64,512]{1,0:T(8,128)(2,1)S(1)} %reduce_sum.112), channel_id=1, replica_groups=mesh['dp'=64,'mp'=4] {'mp'}, dimensions={0}, use_global_device_ids=true | all-gather | bytes 327680 | tf_op jit(solution)/shard_map/all_gather | solution.py:64
  158.9 2.9 fusion.23
  161.8 9.3 %psum.7 = f32[256]{0:T(256)S(1)} all-reduce(f32[256]{0:T(256)S(1)} %get-tuple-element.40), channel_id=1, replica_groups=mesh['dp'=64,'mp'=4] {'mp'}, use_global_device_ids=true, to_apply=%region_8.0 | all-reduce | flops 256 | bytes 2048 | tf_op jit(solution)/shard_map/psum | solution.py:172
  171.6 1.7 fusion.30
  173.5 20.3 %all_to_all.46 = f32[4,256,512]{2,1,0:T(8,128)} all-to-all(f32[4,256,512]{2,1,0:T(8,128)S(1)} %broadcast_in_dim.18), channel_id=1, replica_groups=mesh['dp'=64,'mp'=4] {'mp'}, dimensions={0} | all-to-all | bytes 4194304 | tf_op jit(solution)/shard_map/all_to_all | solution.py:23
  193.9 2.6 reduce_sum.114
  196.5 1.9 fusion.59
  198.9 1.6 broadcast_in_dim.19
  200.5 5.9 %all-to-all-start.7 = ((f32[4,256,512]{2,1,0:T(8,128)}), f32[4,256,512]{2,1,0:T(8,128)}, u32[]{:S(2)}, u32[]{:S(2)}) async-start(f32[4,256,512]{2,1,0:T(8,128)} %broadcast_in_dim.19), calls=%async_computation.7 | async-start | bytes 4194304 | tf_op jit(solution)/shard_map/all_to_all | solution.py:23
  206.4 1.9 convolution_bitcast_fusion.2
  208.2 1.8 convolution_bitcast_fusion
  210.0 1.9 convolution_bitcast_fusion.3
  211.9 9.6 %all-to-all-done.7 = f32[4,256,512]{2,1,0:T(8,128)} async-done(((f32[4,256,512]{2,1,0:T(8,128)}), f32[4,256,512]{2,1,0:T(8,128)}, u32[]{:S(2)}, u32[]{:S(2)}) %all-to-all-start.7) | async-done | bytes 2097184 | tf_op jit(solution)/shard_map/all_to_all | solution.py:23
  221.5 1.8 reduce_sum.115
  225.0 5.2 %pad_maximum_fusion = f32[4,512,1024]{2,1,0:T(8,128)} fusion(f32[1,512,1024]{2,1,0:T(8,128)} %convolution_bitcast_fusion, f32[1,512,1024]{2,1,0:T(8,128)S(1)} %convolution_bitcast_fusion.1, f32[1,512,1024]{2,1,0:T(8,128)S(1)} %copy-done.2, f32[1,512,1024]{2,1,0:T(8,128)} %convolution_bitcast_fusion.3), kind=kLoop, calls=%fused_computation.2 | loop fusion | flops 6291456 | bytes 16777216 | tf_op jit(solution)/shard_map/concatenate | solution.py:32
  230.9 8.1 %scatter_custom_fusion = s32[4096]{0:T(1024)S(1)} fusion(s32[2048]{0:T(1024)S(1)} %bitcast.116, s32[2048]{0:T(1024)S(1)} %bitcast.118, s32[]{:T(128)} %constant.11.clone.1), kind=kCustom, calls=%fused_computation.111 | custom fusion | bytes 16388
  239.8 7.5 %all-to-all-start = ((s32[4,64,16]{2,0,1:T(4,128)}), s32[4,64,16]{2,0,1:T(4,128)S(1)}, u32[]{:S(2)}, u32[]{:S(2)}) async-start(s32[4,64,16]{2,0,1:T(4,128)} %copy.71), calls=%async_computation | async-start | bytes 262144 | tf_op jit(solution)/shard_map/all_to_all | solution.py:105
  247.3 1.5 fusion.15
  248.7 1.6 copy.73
  250.4 7.9 %all-to-all-done = s32[4,64,16]{2,0,1:T(4,128)S(1)} async-done(((s32[4,64,16]{2,0,1:T(4,128)}), s32[4,64,16]{2,0,1:T(4,128)S(1)}, u32[]{:S(2)}, u32[]{:S(2)}) %all-to-all-start) | async-done | bytes 16416 | tf_op jit(solution)/shard_map/all_to_all | solution.py:105
  258.3 5.6 %all-to-all-start.1 = ((bf16[4,64,16,256]{3,2,0,1:T(8,128)(2,1)}), bf16[4,64,16,256]{3,2,0,1:T(8,128)(2,1)}, u32[]{:S(2)}, u32[]{:S(2)}) async-start(bf16[4,64,16,256]{3,2,0,1:T(8,128)(2,1)} %copy.73), calls=%async_computation.1 | async-start | bytes 4194304 | tf_op jit(solution)/shard_map/all_to_all | solution.py:98
  264.1 51.6 %all-to-all-done.1 = bf16[4,64,16,256]{3,2,0,1:T(8,128)(2,1)} async-done(((bf16[4,64,16,256]{3,2,0,1:T(8,128)(2,1)}), bf16[4,64,16,256]{3,2,0,1:T(8,128)(2,1)}, u32[]{:S(2)}, u32[]{:S(2)}) %all-to-all-start.1) | async-done | bytes 2097184 | tf_op jit(solution)/shard_map/all_to_all | solution.py:98
  317.0 6.8 %all-to-all-start.8 = ((f32[64,3,1024]{2,1,0:T(4,128)}), f32[64,3,1024]{2,1,0:T(4,128)}, u32[]{:S(2)}, u32[]{:S(2)}) async-start(f32[64,3,1024]{2,1,0:T(4,128)} %broadcast_in_dim.20), calls=%async_computation.9 | async-start | bytes 2097152 | tf_op jit(solution)/shard_map/all_to_all | solution.py:23
  323.8 2.9 copy.76
  326.8 1.8 copy.74
  328.6 2.9 multiply_reduce_fusion
  332.1 1.9 divide_subtract_fusion
  334.0 3.0 copy.89
  337.0 24.2 %all-to-all-done.8 = f32[64,3,1024]{2,1,0:T(4,128)} async-done(((f32[64,3,1024]{2,1,0:T(4,128)}), f32[64,3,1024]{2,1,0:T(4,128)}, u32[]{:S(2)}, u32[]{:S(2)}) %all-to-all-start.8) | async-done | bytes 786464 | tf_op jit(solution)/shard_map/all_to_all | solution.py:23
  361.1 2.0 reduce_sum.119
  363.2 2.8 fusion.20
  366.0 30.5 %reduce-scatter.2.cloned.1.call-done = f32[4,8,1024]{2,1,0:T(8,128)} async-done(((f32[4,512,1024]{2,1,0:T(8,128)}), f32[4,8,1024]{2,1,0:T(8,128)}) %reduce-scatter.2.cloned.1.call-update) | async-done | bytes 131088 | tf_op jit(solution)/shard_map/reduce_scatter | solution.py:33
  396.5 1.5 fusion.83
  (98 shorter events, 13.7 us)
Async XLA Ops:
  7.2 240.1 %copy-start = (bf16[4,512,256]{2,1,0:T(8,128)(2,1)S(1)}, bf16[4,512,256]{2,1,0:T(8,128)(2,1)}, u32[]{:S(2)}) copy-start(bf16[4,512,256]{2,1,0:T(8,128)(2,1)} %param.15) | copy-start | bytes 3145732
  7.2 3.1 copy-start.22
  7.2 3.2 copy-start.21
  7.2 3.0 copy-start.14
  7.2 3.4 copy-start.15
  7.2 34.6 %copy-start.10 = (f32[4,512,256]{2,1,0:T(8,128)S(1)}, f32[4,512,256]{2,1,0:T(8,128)}, u32[]{:S(2)}) copy-start(f32[4,512,256]{2,1,0:T(8,128)} %param.13) | copy-start | bytes 6291460
  45.5 56.1 %all-to-all-start.3 = ((bf16[4,64,16,256]{3,2,0,1:T(8,128)(2,1)}), bf16[4,64,16,256]{3,2,0,1:T(8,128)(2,1)S(1)}, u32[]{:S(2)}, u32[]{:S(2)}) async-start(bf16[4,64,16,256]{3,2,0,1:T(8,128)(2,1)} %copy.83), calls=%async_computation.3 | async-start | bytes 4194304 | tf_op jit(solution)/shard_map/all_to_all | solution.py:140
  50.2 2.5 copy-start.19
  104.1 7.8 %copy-start.16 = (f32[2,1024]{1,0:T(2,128)S(1)}, f32[2,1024]{1,0:T(2,128)}, u32[]{:S(2)}) copy-start(f32[2,1024]{1,0:T(2,128)} %param.24) | copy-start | bytes 24580
  107.0 11.5 %all-to-all-start.4 = ((f32[4,64,512]{2,1,0:T(8,128)}), f32[4,64,512]{2,1,0:T(8,128)S(1)}, u32[]{:S(2)}, u32[]{:S(2)}) async-start(f32[4,64,512]{2,1,0:T(8,128)} %fusion.39), calls=%async_computation.4 | async-start | bytes 1048576 | tf_op jit(solution)/shard_map/all_to_all | solution.py:17
  118.6 14.6 %copy-start.12 = (bf16[2,512,1024]{2,1,0:T(8,128)(2,1)S(1)}, bf16[2,512,1024]{2,1,0:T(8,128)(2,1)}, u32[]{:S(2)}) copy-start(bf16[2,512,1024]{2,1,0:T(8,128)(2,1)} %param.23) | copy-start | bytes 6291460
  130.4 4.1 %copy-start.7 = (bf16[256,512]{1,0:T(8,128)(2,1)}, bf16[256,512]{1,0:T(8,128)(2,1)S(1)}, u32[]{:S(2)}) copy-start(bf16[256,512]{1,0:T(8,128)(2,1)S(1)} %all_gather.6) | copy-start | bytes 786436
  133.1 25.8 %copy-start.4 = (bf16[256,1024]{1,0:T(8,128)(2,1)}, bf16[256,1024]{1,0:T(8,128)(2,1)S(1)}, u32[]{:S(2)}) copy-start(bf16[256,1024]{1,0:T(8,128)(2,1)S(1)} %get-tuple-element.60) | copy-start | bytes 1572868
  133.1 6.8 %copy-start.13 = (f32[1024]{0:T(1024)S(1)}, f32[1024]{0:T(1024)}, u32[]{:S(2)}) copy-start(f32[1024]{0:T(1024)} %param.25) | copy-start | bytes 12292
  134.4 12.8 %all-to-all-start.5 = ((f32[4,64,512]{2,1,0:T(8,128)}), f32[4,64,512]{2,1,0:T(8,128)S(1)}, u32[]{:S(2)}, u32[]{:S(2)}) async-start(f32[4,64,512]{2,1,0:T(8,128)} %fusion.33), calls=%async_computation.5 | async-start | bytes 1048576 | tf_op jit(solution)/shard_map/all_to_all | solution.py:17
  147.3 23.9 %copy-start.20 = (s32[256]{0:T(256)S(1)}, s32[256]{0:T(256)}, u32[]{:S(2)}) copy-start(s32[256]{0:T(256)} %param.21) | copy-start | bytes 3076
  196.5 2.0 copy-start.3
  200.5 21.0 %all-to-all-start.7 = ((f32[4,256,512]{2,1,0:T(8,128)}), f32[4,256,512]{2,1,0:T(8,128)}, u32[]{:S(2)}, u32[]{:S(2)}) async-start(f32[4,256,512]{2,1,0:T(8,128)} %broadcast_in_dim.19), calls=%async_computation.7 | async-start | bytes 4194304 | tf_op jit(solution)/shard_map/all_to_all | solution.py:23
  206.4 190.1 %reduce-scatter.2.cloned.1.call-start = ((), (), s32[]{:S(2)}) async-start(), calls=%async_computation.10 | async-start | bytes 8519680 | tf_op jit(solution)/shard_map/reduce_scatter | solution.py:33
  206.4 1.9 copy-start.5
  206.4 1.9 copy-start.11
  208.2 1.8 copy-start.8
  223.4 1.6 copy-start.2
  230.2 0.7 copy-start.17
  239.8 18.5 %all-to-all-start = ((s32[4,64,16]{2,0,1:T(4,128)}), s32[4,64,16]{2,0,1:T(4,128)S(1)}, u32[]{:S(2)}, u32[]{:S(2)}) async-start(s32[4,64,16]{2,0,1:T(4,128)} %copy.71), calls=%async_computation | async-start | bytes 262144 | tf_op jit(solution)/shard_map/all_to_all | solution.py:105
  250.4 13.5 %copy-start.9 = (bf16[256,1024]{1,0:T(8,128)(2,1)S(1)}, bf16[256,1024]{1,0:T(8,128)(2,1)}, u32[]{:S(2)}) copy-start(bf16[256,1024]{1,0:T(8,128)(2,1)} %get-tuple-element.41) | copy-start | bytes 1572868
  258.3 57.4 %all-to-all-start.1 = ((bf16[4,64,16,256]{3,2,0,1:T(8,128)(2,1)}), bf16[4,64,16,256]{3,2,0,1:T(8,128)(2,1)}, u32[]{:S(2)}, u32[]{:S(2)}) async-start(bf16[4,64,16,256]{3,2,0,1:T(8,128)(2,1)} %copy.73), calls=%async_computation.1 | async-start | bytes 4194304 | tf_op jit(solution)/shard_map/all_to_all | solution.py:98
  317.0 44.2 %all-to-all-start.8 = ((f32[64,3,1024]{2,1,0:T(4,128)}), f32[64,3,1024]{2,1,0:T(4,128)}, u32[]{:S(2)}, u32[]{:S(2)}) async-start(f32[64,3,1024]{2,1,0:T(4,128)} %broadcast_in_dim.20), calls=%async_computation.9 | async-start | bytes 2097152 | tf_op jit(solution)/shard_map/all_to_all | solution.py:23
  328.6 2.9 copy-start.18
  328.6 3.5 copy-start.1
  334.0 29.1 %copy-start.6 = (f32[256,1024]{1,0:T(8,128)S(1)}, f32[256,1024]{1,0:T(8,128)}, u32[]{:S(2)}) copy-start(f32[256,1024]{1,0:T(8,128)} %get-tuple-element.62) | copy-start | bytes 3145732
Sparse Core Ops, SparseCore 0:
  230.3 166.1 reduce-scatter.1
where the time goes:
time: 406 us; the launch traced here: 405 us
  waiting for transfers between devices  186 us (46%)
  blocking collectives  75.8 us (19%)
  starting transfers between devices  40.8 us (10%)
  local copies, waits for them, and re-layouts  38.8 us (10%)
  matrix products  31.6 us (8%)
  other arithmetic  16.9 us (4%)
  between operations  14.5 us (4%)
    all_to_all x1, waiting for transfers between devices, local(): lax.all_to_all(send_grads.reshape(local_feats, peers, grad_cap, width), '...  51.6 us
    all_to_all x1, waiting for transfers between devices, local(): lax.all_to_all(served.reshape(local_feats, peers, look_cap, width), 'dp',...  48.8 us
    all_to_all x2, waiting for transfers between devices, copy_for_each(): return lax.all_to_all(copies, axis, split_axis=0, concat_axis=0, tiled=True)  33.8 us
    reduce_scatter x1, waiting for transfers between devices, side_by_side(): filled = lax.psum_scatter(both, axis, scatter_dimension=dim, tiled=True)  30.5 us
    unnamed x58, local copies, waits for them, and re-layouts  25.5 us
    all_gather x2, blocking collectives, cross_down(): return lax.all_gather(share.astype(jnp.bfloat16), 'mp', axis=0, tiled=True)  23.4 us
    all_to_all x1, blocking collectives, local(): lax.all_to_all(wanted.reshape(local_feats, peers, look_cap), 'dp', split_...  22.8 us
    all_to_all x1, blocking collectives, copy_for_each(): return lax.all_to_all(copies, axis, split_axis=0, concat_axis=0, tiled=True)  20.3 us
  transfers between devices with their start and end apart: 8, of which 8 were waited for; matrix products, arithmetic and copies ran while one was open for 10% of the time, Pallas kernels for 0%

commit v1 on v0

--- a/solution.py
+++ b/solution.py
@@ -59,9 +59,13 @@
     )
 
 
+def summed_rounded(partial, axis):
+    share = lax.psum_scatter(partial, axis, scatter_dimension=0, tiled=True)
+    return lax.all_gather(share.astype(jnp.bfloat16), axis, axis=0, tiled=True)
+
+
 def cross_down(state, v_layer):
-    share = sum_at_owner(contract_last(state, v_layer), "mp", 0)
-    return lax.all_gather(share.astype(jnp.bfloat16), "mp", axis=0, tiled=True)
+    return summed_rounded(contract_last(state, v_layer), "mp")
 
 
 def local(
@@ -184,9 +188,9 @@
         bias_grads[layer] = jnp.sum(direct, axis=0)
         direct_bias_term = direct.astype(jnp.bfloat16)
         grad_u_layer = contract_first(downs[layer], direct_bias_term)
-        back_sum = over_copies(
+        back_sum = summed_rounded(
             contract_last(direct_bias_term, up_factor_weight[layer]), "mp"
-        ).astype(jnp.bfloat16)
+        )
         down_factor_gradient = contract_first(back_sum, states[layer])
         to_start = to_start + upstream * crosses[layer]
         upstream = upstream + jnp.dot(back_sum, v_weight[layer], preferred_element_type=jnp.float32)
@@ -195,7 +199,7 @@
     grad_u = jnp.stack(grads_u)
     grad_v = jnp.stack(grads_v)
     grad_u, grad_v = side_by_side((grad_u, grad_v), "dp", 1, 0)
-    grad_small = over_copies(jnp.stack(bias_grads + [head_grad]), "dp")
+    grad_small = lax.psum(jnp.stack(bias_grads + [head_grad]), "dp")
     grad_pooled = (upstream + to_start).astype(jnp.bfloat16)
     return (new_table, new_accum, grad_u, grad_v, grad_small, grad_pooled)
 

time: 406 us -> 635 us (1.56)
  blocking collectives: 75.8 us -> 328 us
  starting transfers between devices: 40.8 us -> 21.1 us
    psum x0 -> x1, blocking collectives: none -> 246 us  [local(): grad_small = lax.psum(jnp.stack(bias_grads + [head_grad]), 'dp')]
    reduce_scatter x0 -> x4, waiting for transfers between devices: none -> 81.7 us  [summed_rounded(): share = lax.psum_scatter(partial, axis, scatter_dimension=0, tiled=True)]
    all_to_all x4 -> x0, waiting for transfers between devices: 47.5 us -> none  [the longest x2 33.8 us: copy_for_each(): return lax.all_to_all(copies, axis, split_axis=0, concat_axis=0, tiled=True)]
    reduce_scatter x1, waiting for transfers between devices: 30.5 us -> 0.01 us  [side_by_side(): filled = lax.psum_scatter(both, axis, scatter_dimension=dim, tiled=True)]
    all_gather x2 -> x4, blocking collectives: 23.4 us -> 49.2 us  [summed_rounded(): return lax.all_gather(share.astype(jnp.bfloat16), axis, axis=0, tiled=True)]
    all_to_all x4 -> x0, starting transfers between devices: 23.1 us -> none  [the longest x2 12.7 us: copy_for_each(): return lax.all_to_all(copies, axis, split_axis=0, concat_axis=0, tiled=True)]
    all_to_all x1 -> x0, blocking collectives: 20.3 us -> none  [copy_for_each(): return lax.all_to_all(copies, axis, split_axis=0, concat_axis=0, tiled=True)]
    reduce_sum x5 -> x0, other arithmetic: 6.53 us -> none  [the longest x3 6.45 us: over_copies(): return copy_for_each(array, axis).sum(axis=0)]
  transfers between devices with their start and end apart: 8 -> 8, of which waited for: 8 -> 7; matrix products, arithmetic and copies ran while one was open for 10% -> 6% of each run, Pallas kernels for 0% -> 0%
where the time goes in v1:
time: 635 us; the launch traced here: 633 us
  blocking collectives  328 us (52%)
  waiting for transfers between devices  187 us (29%)
  local copies, waits for them, and re-layouts  34.7 us (5%)
  matrix products  31.7 us (5%)
  starting transfers between devices  21.1 us (3%)
  other arithmetic  15.5 us (2%)
  between operations  14.3 us (2%)
    psum x1, blocking collectives, local(): grad_small = lax.psum(jnp.stack(bias_grads + [head_grad]), 'dp')  246 us
    reduce_scatter x4, waiting for transfers between devices, summed_rounded(): share = lax.psum_scatter(partial, axis, scatter_dimension=0, tiled=True)  81.7 us
    all_gather x4, blocking collectives, summed_rounded(): return lax.all_gather(share.astype(jnp.bfloat16), axis, axis=0, tiled=True)  49.2 us
    all_to_all x1, waiting for transfers between devices, local(): lax.all_to_all(served.reshape(local_feats, peers, look_cap, width), 'dp',...  48.8 us
    all_to_all x1, waiting for transfers between devices, local(): lax.all_to_all(send_grads.reshape(local_feats, peers, grad_cap, width), '...  48.3 us
    unnamed x60, local copies, waits for them, and re-layouts  25.1 us
    all_to_all x1, blocking collectives, local(): lax.all_to_all(wanted.reshape(local_feats, peers, look_cap), 'dp', split_...  22.8 us
  transfers between devices with their start and end apart: 8, of which 7 were waited for; matrix products, arithmetic and copies ran while one was open for 6% of the time, Pallas kernels for 0%

profile of v1, /device:TPU:8, one launch (start us, length us, event | category | flops | bytes accessed | tf_op | source)
XLA Modules:
  0.0 632.6 jit_solution(6955148603846393421)
XLA Ops:
  10.6 8.1 %scatter_custom_fusion.1 = s32[4096]{0:T(1024)S(1)} fusion(s32[2048]{0:T(1024)S(1)} %bitcast.111, s32[2048]{0:T(1024)S(1)} %bitcast.113, s32[]{:T(128)} %constant.5.clone.1), kind=kCustom, calls=%fused_computation.105 | custom fusion | bytes 16388
  18.9 22.8 %all_to_all.20 = s32[4,64,16]{2,0,1:T(4,128)S(1)} all-to-all(s32[4,64,16]{2,0,1:T(4,128)S(1)} %copy.43), channel_id=1, replica_groups=mesh['dp'=64,'mp'=4] {'dp'}, dimensions={1} | all-to-all | bytes 32768 | tf_op jit(solution)/shard_map/all_to_all | solution.py:134
  41.8 2.1 fusion.14
  43.9 1.6 copy.45
  45.5 4.7 all-to-all-start.3
  51.3 1.1 add.86
  52.8 48.8 %all-to-all-done.3 = bf16[4,64,16,256]{3,2,0,1:T(8,128)(2,1)S(1)} async-done(((bf16[4,64,16,256]{3,2,0,1:T(8,128)(2,1)}), bf16[4,64,16,256]{3,2,0,1:T(8,128)(2,1)S(1)}, u32[]{:S(2)}, u32[]{:S(2)}) %all-to-all-start.3) | async-done | bytes 2097184 | tf_op jit(solution)/shard_map/all_to_all | solution.py:144
  101.8 2.1 fusion.17
  103.8 1.3 fusion.40
  105.4 18.1 %reduce-scatter.6.cloned.1.call-done = f32[64,512]{1,0:T(8,128)} async-done(((f32[256,512]{1,0:T(8,128)}), f32[64,512]{1,0:T(8,128)}) %reduce-scatter.6.cloned.1.call-update) | async-done | bytes 131088 | tf_op jit(solution)/shard_map/reduce_scatter | solution.py:63
  123.5 1.1 convert_element_type.138
  124.6 12.3 %all_gather.12 = bf16[256,512]{1,0:T(8,128)(2,1)S(1)} all-gather(bf16[64,512]{1,0:T(8,128)(2,1)S(1)} %convert_element_type.138), channel_id=1, replica_groups=mesh['dp'=64,'mp'=4] {'mp'}, dimensions={0}, use_global_device_ids=true | all-gather | bytes 327680 | tf_op jit(solution)/shard_map/all_gather | solution.py:64
  136.9 2.8 fusion.26
  139.7 1.3 fusion.34
  141.1 23.8 %reduce-scatter.8.cloned.1.call-done = f32[64,512]{1,0:T(8,128)} async-done(((f32[256,512]{1,0:T(8,128)}), f32[64,512]{1,0:T(8,128)}) %reduce-scatter.8.cloned.1.call-update) | async-done | bytes 131088 | tf_op jit(solution)/shard_map/reduce_scatter | solution.py:63
  164.9 0.9 convert_element_type.141
  165.8 12.3 %all_gather.13 = bf16[256,512]{1,0:T(8,128)(2,1)S(1)} all-gather(bf16[64,512]{1,0:T(8,128)(2,1)S(1)} %convert_element_type.141), channel_id=1, replica_groups=mesh['dp'=64,'mp'=4] {'mp'}, dimensions={0}, use_global_device_ids=true | all-gather | bytes 327680 | tf_op jit(solution)/shard_map/all_gather | solution.py:64
  178.2 2.9 fusion.23
  181.0 10.2 %psum.14 = f32[256]{0:T(256)S(1)} all-reduce(f32[256]{0:T(256)S(1)} %get-tuple-element.28), channel_id=1, replica_groups=mesh['dp'=64,'mp'=4] {'mp'}, use_global_device_ids=true, to_apply=%region_8.0 | all-reduce | flops 256 | bytes 2048 | tf_op jit(solution)/shard_map/psum | solution.py:176
  191.7 2.5 fusion.30
  194.3 21.8 %reduce-scatter.10.cloned.1.call-done = f32[64,512]{1,0:T(8,128)} async-done(((f32[256,512]{1,0:T(8,128)}), f32[64,512]{1,0:T(8,128)}) %reduce-scatter.10.cloned.1.call-update) | async-done | bytes 131088 | tf_op jit(solution)/shard_map/reduce_scatter | solution.py:63
  216.1 1.1 convert_element_type.149
  217.1 12.3 %all_gather.14 = bf16[256,512]{1,0:T(8,128)(2,1)S(1)} all-gather(bf16[64,512]{1,0:T(8,128)(2,1)S(1)} %convert_element_type.149), channel_id=1, replica_groups=mesh['dp'=64,'mp'=4] {'mp'}, dimensions={0}, use_global_device_ids=true | all-gather | bytes 327680 | tf_op jit(solution)/shard_map/all_gather | solution.py:64
  230.1 1.7 fusion.59
  231.9 1.3 fusion.36
  233.4 1.9 convolution_bitcast_fusion.2
  235.3 1.8 convolution_bitcast_fusion
  237.1 1.8 convolution_bitcast_fusion.3
  238.9 18.1 %reduce-scatter.12.cloned.1.call-done = f32[64,512]{1,0:T(8,128)} async-done(((f32[256,512]{1,0:T(8,128)}), f32[64,512]{1,0:T(8,128)}) %reduce-scatter.12.cloned.1.call-update) | async-done | bytes 131088 | tf_op jit(solution)/shard_map/reduce_scatter | solution.py:63
  257.0 1.1 convert_element_type.152
  258.1 12.3 %all_gather.15 = bf16[256,512]{1,0:T(8,128)(2,1)S(1)} all-gather(bf16[64,512]{1,0:T(8,128)(2,1)S(1)} %convert_element_type.152), channel_id=1, replica_groups=mesh['dp'=64,'mp'=4] {'mp'}, dimensions={0}, use_global_device_ids=true | all-gather | bytes 327680 | tf_op jit(solution)/shard_map/all_gather | solution.py:64
  270.9 5.2 pad_maximum_fusion
  276.8 8.1 %scatter_custom_fusion = s32[4096]{0:T(1024)S(1)} fusion(s32[2048]{0:T(1024)S(1)} %bitcast.112, s32[2048]{0:T(1024)S(1)} %bitcast.114, s32[]{:T(128)} %constant.11.clone.1), kind=kCustom, calls=%fused_computation.107 | custom fusion | bytes 16388
  285.7 10.4 %all-to-all-start = ((s32[4,64,16]{2,0,1:T(4,128)}), s32[4,64,16]{2,0,1:T(4,128)S(1)}, u32[]{:S(2)}, u32[]{:S(2)}) async-start(s32[4,64,16]{2,0,1:T(4,128)} %copy.33), calls=%async_computation | async-start | bytes 262144 | tf_op jit(solution)/shard_map/all_to_all | solution.py:109
  296.1 1.5 fusion.15
  297.6 1.6 copy.35
  299.2 7.9 %all-to-all-done = s32[4,64,16]{2,0,1:T(4,128)S(1)} async-done(((s32[4,64,16]{2,0,1:T(4,128)}), s32[4,64,16]{2,0,1:T(4,128)S(1)}, u32[]{:S(2)}, u32[]{:S(2)}) %all-to-all-start) | async-done | bytes 16416 | tf_op jit(solution)/shard_map/all_to_all | solution.py:109
  307.1 5.6 all-to-all-start.1
  312.7 2.9 copy.38
  315.8 48.3 %all-to-all-done.1 = bf16[4,64,16,256]{3,2,0,1:T(8,128)(2,1)} async-done(((bf16[4,64,16,256]{3,2,0,1:T(8,128)(2,1)}), bf16[4,64,16,256]{3,2,0,1:T(8,128)(2,1)}, u32[]{:S(2)}, u32[]{:S(2)}) %all-to-all-start.1) | async-done | bytes 2097184 | tf_op jit(solution)/shard_map/all_to_all | solution.py:102
  364.1 1.8 copy.36
  366.0 2.9 multiply_reduce_fusion
  369.5 1.9 divide_subtract_fusion
  371.3 3.0 copy.49
  374.3 1.2 fusion.24
  375.6 246.2 %psum.15 = f32[3,1024]{1,0:T(4,128)} all-reduce(f32[3,1024]{1,0:T(4,128)S(1)} %pad_maximum_fusion.1), channel_id=1, replica_groups=mesh['dp'=64,'mp'=4] {'dp'}, use_global_device_ids=true, to_apply=%region_15.0 | all-reduce | flops 3072 | bytes 24576 | tf_op jit(solution)/shard_map/psum | solution.py:202
  621.8 2.8 fusion.20
  624.6 1.5 fusion.79
  (100 shorter events, 9.8 us)
Async XLA Ops:
  7.2 288.9 %copy-start = (bf16[4,512,256]{2,1,0:T(8,128)(2,1)S(1)}, bf16[4,512,256]{2,1,0:T(8,128)(2,1)}, u32[]{:S(2)}) copy-start(bf16[4,512,256]{2,1,0:T(8,128)(2,1)} %param.15) | copy-start | bytes 3145732
  7.2 3.1 copy-start.23
  7.2 3.2 copy-start.22
  7.2 3.0 copy-start.15
  7.2 3.4 copy-start.16
  7.2 34.6 %copy-start.9 = (f32[4,512,256]{2,1,0:T(8,128)S(1)}, f32[4,512,256]{2,1,0:T(8,128)}, u32[]{:S(2)}) copy-start(f32[4,512,256]{2,1,0:T(8,128)} %param.13) | copy-start | bytes 6291460
  45.5 56.1 %all-to-all-start.3 = ((bf16[4,64,16,256]{3,2,0,1:T(8,128)(2,1)}), bf16[4,64,16,256]{3,2,0,1:T(8,128)(2,1)S(1)}, u32[]{:S(2)}, u32[]{:S(2)}) async-start(bf16[4,64,16,256]{3,2,0,1:T(8,128)(2,1)} %copy.45), calls=%async_computation.3 | async-start | bytes 4194304 | tf_op jit(solution)/shard_map/all_to_all | solution.py:144
  50.2 2.5 copy-start.20
  50.2 73.3 %reduce-scatter.6.cloned.1.call-start = ((), (), s32[]{:S(2)}) async-start(), calls=%async_computation.9 | async-start | bytes 655360 | tf_op jit(solution)/shard_map/reduce_scatter | solution.py:63
  101.7 2.1 copy-start.12
  103.8 1.4 copy-start.17
  105.2 59.8 %reduce-scatter.8.cloned.1.call-start = ((), (), s32[]{:S(2)}) async-start(), calls=%async_computation.10 | async-start | bytes 655360 | tf_op jit(solution)/shard_map/reduce_scatter | solution.py:63
  123.5 16.2 %copy-start.13 = (bf16[2,512,1024]{2,1,0:T(8,128)(2,1)S(1)}, bf16[2,512,1024]{2,1,0:T(8,128)(2,1)}, u32[]{:S(2)}) copy-start(bf16[2,512,1024]{2,1,0:T(8,128)(2,1)} %param.23) | copy-start | bytes 6291460
  136.9 4.1 copy-start.7
  139.7 41.3 %copy-start.4 = (bf16[256,1024]{1,0:T(8,128)(2,1)}, bf16[256,1024]{1,0:T(8,128)(2,1)S(1)}, u32[]{:S(2)}) copy-start(bf16[256,1024]{1,0:T(8,128)(2,1)S(1)} %get-tuple-element.48) | copy-start | bytes 1572868
  139.7 1.4 copy-start.14
  141.0 75.0 %reduce-scatter.10.cloned.1.call-start = ((), (), s32[]{:S(2)}) async-start(), calls=%async_computation.11 | async-start | bytes 655360 | tf_op jit(solution)/shard_map/reduce_scatter | solution.py:63
  165.8 25.5 %copy-start.21 = (s32[256]{0:T(256)S(1)}, s32[256]{0:T(256)}, u32[]{:S(2)}) copy-start(s32[256]{0:T(256)} %param.21) | copy-start | bytes 3076
  194.2 62.8 %reduce-scatter.12.cloned.1.call-start = ((), (), s32[]{:S(2)}) async-start(), calls=%async_computation.12 | async-start | bytes 655360 | tf_op jit(solution)/shard_map/reduce_scatter | solution.py:63
  216.1 15.8 %copy-start.3 = (bf16[2,512,1024]{2,1,0:T(8,128)(2,1)S(1)}, bf16[2,512,1024]{2,1,0:T(8,128)(2,1)}, u32[]{:S(2)}) copy-start(bf16[2,512,1024]{2,1,0:T(8,128)(2,1)} %param.22) | copy-start | bytes 6291460
  229.4 0.7 copy-start.10
  233.2 391.4 %reduce-scatter.14.cloned.1.call-start = ((), (), s32[]{:S(2)}) async-start(), calls=%async_computation.13 | async-start | bytes 8519680 | tf_op jit(solution)/shard_map/reduce_scatter | solution.py:33
  233.4 1.9 copy-start.5
  233.4 1.9 copy-start.11
  235.3 1.8 copy-start.8
  257.0 13.9 %copy-start.2 = (f32[1,512,1024]{2,1,0:T(8,128)S(1)}, f32[1,512,1024]{2,1,0:T(8,128)}, u32[]{:S(2)}) copy-start(f32[1,512,1024]{2,1,0:T(8,128)} %convolution_bitcast_fusion.2) | copy-start | bytes 6291460
  276.1 0.7 copy-start.18
  285.7 21.5 %all-to-all-start = ((s32[4,64,16]{2,0,1:T(4,128)}), s32[4,64,16]{2,0,1:T(4,128)S(1)}, u32[]{:S(2)}, u32[]{:S(2)}) async-start(s32[4,64,16]{2,0,1:T(4,128)} %copy.33), calls=%async_computation | async-start | bytes 262144 | tf_op jit(solution)/shard_map/all_to_all | solution.py:109
  307.1 57.0 %all-to-all-start.1 = ((bf16[4,64,16,256]{3,2,0,1:T(8,128)(2,1)}), bf16[4,64,16,256]{3,2,0,1:T(8,128)(2,1)}, u32[]{:S(2)}, u32[]{:S(2)}) async-start(bf16[4,64,16,256]{3,2,0,1:T(8,128)(2,1)} %copy.35), calls=%async_computation.1 | async-start | bytes 4194304 | tf_op jit(solution)/shard_map/all_to_all | solution.py:102
  365.9 2.9 copy-start.19
  365.9 3.5 copy-start.1
  371.3 250.4 %copy-start.6 = (f32[256,1024]{1,0:T(8,128)S(1)}, f32[256,1024]{1,0:T(8,128)}, u32[]{:S(2)}) copy-start(f32[256,1024]{1,0:T(8,128)} %get-tuple-element.50) | copy-start | bytes 3145732
Sparse Core Ops, SparseCore 0:
  105.3 18.1 reduce-scatter.5
  141.1 23.7 reduce-scatter.7
  194.3 21.6 reduce-scatter.9
  233.3 23.6 reduce-scatter.11
  276.2 152.7 reduce-scatter.13

commit v2 on v1

--- a/solution.py
+++ b/solution.py
@@ -60,8 +60,7 @@
 
 
 def summed_rounded(partial, axis):
-    share = lax.psum_scatter(partial, axis, scatter_dimension=0, tiled=True)
-    return lax.all_gather(share.astype(jnp.bfloat16), axis, axis=0, tiled=True)
+    return lax.all_gather(partial, axis, axis=0).sum(axis=0).astype(jnp.bfloat16)
 
 
 def cross_down(state, v_layer):
@@ -99,29 +98,6 @@
         .at[which_feature, grad_slot]
         .set(grad_row)
     )
-    recv_grads = lax.all_to_all(
-        send_grads.reshape(local_feats, peers, grad_cap, width),
-        "dp",
-        split_axis=1,
-        concat_axis=1,
-        tiled=True,
-    )
-    recv_rows = lax.all_to_all(
-        send_rows.reshape(local_feats, peers, grad_cap),
-        "dp",
-        split_axis=1,
-        concat_axis=1,
-        tiled=True,
-    )
-    landing = selection_matrix(recv_rows.reshape(local_feats, grad_total), rows_per_shard)
-    summed = jnp.einsum(
-        "wjc,wjl->wcl",
-        landing,
-        recv_grads.reshape(local_feats, grad_total, width),
-        preferred_element_type=jnp.float32,
-    )
-    new_accum = accum + jnp.mean(summed * summed, axis=2)
-    new_table = embed_table - learn_rate * summed / jnp.sqrt(new_accum)[:, :, None]
     batch_dev = bag_len.shape[1]
     look_dev = lookup_row.shape[1]
     bag_size = look_dev // batch_dev
@@ -157,6 +133,21 @@
         "fbs,fse->fbe", mixing, returned, preferred_element_type=jnp.float32
     ).astype(jnp.bfloat16)
     start = jnp.transpose(pooled, (1, 0, 2)).reshape(batch_dev, local_feats * width)
+    send_grads, send_rows, start = lax.optimization_barrier((send_grads, send_rows, start))
+    recv_grads = lax.all_to_all(
+        send_grads.reshape(local_feats, peers, grad_cap, width),
+        "dp",
+        split_axis=1,
+        concat_axis=1,
+        tiled=True,
+    )
+    recv_rows = lax.all_to_all(
+        send_rows.reshape(local_feats, peers, grad_cap),
+        "dp",
+        split_axis=1,
+        concat_axis=1,
+        tiled=True,
+    )
     start_f = start.astype(jnp.float32)
     n_layers = up_factor_weight.shape[0]
     state = start
@@ -173,7 +164,11 @@
         downs.append(down_sum)
         crosses.append(cross_out)
         state = (start_f * cross_out + state.astype(jnp.float32)).astype(jnp.bfloat16)
-    logit = lax.psum(jnp.sum(state.astype(jnp.float32) * head_weight[None, :], axis=1), "mp")
+    local_logit = jnp.sum(state.astype(jnp.float32) * head_weight[None, :], axis=1)
+    recv_grads, recv_rows, local_logit = lax.optimization_barrier(
+        (recv_grads, recv_rows, local_logit)
+    )
+    logit = lax.psum(local_logit, "mp")
     slope = (jax.nn.sigmoid(logit) - label.astype(jnp.float32)) / jnp.sqrt(
         jnp.float32(batch_dev * peers)
     )
@@ -196,10 +191,29 @@
         upstream = upstream + jnp.dot(back_sum, v_weight[layer], preferred_element_type=jnp.float32)
         grads_u[layer] = grad_u_layer
         grads_v[layer] = down_factor_gradient
+    landing = selection_matrix(recv_rows.reshape(local_feats, grad_total), rows_per_shard)
+    summed = jnp.einsum(
+        "wjc,wjl->wcl",
+        landing,
+        recv_grads.reshape(local_feats, grad_total, width),
+        preferred_element_type=jnp.float32,
+    )
+    new_accum = accum + jnp.mean(summed * summed, axis=2)
+    new_table = embed_table - learn_rate * summed / jnp.sqrt(new_accum)[:, :, None]
     grad_u = jnp.stack(grads_u)
     grad_v = jnp.stack(grads_v)
-    grad_u, grad_v = side_by_side((grad_u, grad_v), "dp", 1, 0)
-    grad_small = lax.psum(jnp.stack(bias_grads + [head_grad]), "dp")
+    small = jnp.stack(bias_grads + [head_grad])
+    both = jnp.concatenate((grad_u, grad_v), axis=0)
+    lead, rows, cols = both.shape
+    block_rows = rows // peers
+    extra = -(-small.size // (lead * block_rows * 128)) * 128
+    small_block = jnp.pad(small.reshape(-1), (0, lead * block_rows * extra - small.size))
+    small_rep = jnp.tile(small_block.reshape(lead, block_rows, extra), (1, peers, 1))
+    filled = lax.psum_scatter(
+        jnp.concatenate((both, small_rep), axis=2), "dp", scatter_dimension=1, tiled=True
+    )
+    grad_u, grad_v = jnp.split(filled[:, :, :cols], 2, axis=0)
+    grad_small = filled[:, :, cols:].reshape(-1)[: small.size].reshape(small.shape)
     grad_pooled = (upstream + to_start).astype(jnp.bfloat16)
     return (new_table, new_accum, grad_u, grad_v, grad_small, grad_pooled)
 

time: 635 us -> 439 us (0.69)
  blocking collectives: 328 us -> 31.8 us
  waiting for transfers between devices: 187 us -> 288 us
    psum x2 -> x1, blocking collectives: 256 us -> 8.97 us  [local(): logit = lax.psum(local_logit, 'mp')]
    all_gather x0 -> x4, waiting for transfers between devices: none -> 100 us  [summed_rounded(): lax.all_gather(partial, axis, axis=0).sum(axis=0).astype(jnp.bfloat16)]
    reduce_scatter x5 -> x1, waiting for transfers between devices: 81.7 us -> 140 us  [local(): lax.psum_scatter(jnp.concatenate((both, small_rep), axis=2), 'dp', scatte...]
    all_gather x4 -> x0, blocking collectives: 49.2 us -> none  [summed_rounded(): return lax.all_gather(share.astype(jnp.bfloat16), axis, axis=0, tiled=True)]
    all_to_all x1, waiting for transfers between devices: 48.3 us -> 0.26 us  [local(): lax.all_to_all(send_grads.reshape(local_feats, peers, grad_cap, width), '...]
    all_to_all x1, waiting for transfers between devices: 48.8 us -> 37.9 us  [local(): lax.all_to_all(served.reshape(local_feats, peers, look_cap, width), 'dp',...]
    reduce_sum x2 -> x4, other arithmetic: 1.62 us -> 8.14 us  [summed_rounded(): lax.all_gather(partial, axis, axis=0).sum(axis=0).astype(jnp.bfloat16)]
    unnamed x60 -> x63, local copies, waits for them, and re-layouts: 25.1 us -> 26.8 us
  transfers between devices with their start and end apart: 8 -> 8, of which waited for: 7 -> 8; matrix products, arithmetic and copies ran while one was open for 6% -> 11% of each run, Pallas kernels for 0% -> 0%
where the time goes in v2:
time: 439 us; the launch traced here: 438 us
  waiting for transfers between devices  288 us (66%)
  local copies, waits for them, and re-layouts  36.5 us (8%)
  matrix products  33.7 us (8%)
  blocking collectives  31.8 us (7%)
  other arithmetic  18.3 us (4%)
  starting transfers between devices  15.2 us (3%)
  between operations  14.3 us (3%)
    reduce_scatter x1, waiting for transfers between devices, local(): lax.psum_scatter(jnp.concatenate((both, small_rep), axis=2), 'dp', scatte...  140 us
    all_gather x4, waiting for transfers between devices, summed_rounded(): lax.all_gather(partial, axis, axis=0).sum(axis=0).astype(jnp.bfloat16)  100 us
    all_to_all x1, waiting for transfers between devices, local(): lax.all_to_all(served.reshape(local_feats, peers, look_cap, width), 'dp',...  37.9 us
    unnamed x63, local copies, waits for them, and re-layouts  26.8 us
    all_to_all x1, blocking collectives, local(): lax.all_to_all(wanted.reshape(local_feats, peers, look_cap), 'dp', split_...  22.8 us
    all_to_all x1, waiting for transfers between devices, local(): lax.all_to_all(send_rows.reshape(local_feats, peers, grad_cap), 'dp', spl...  9.41 us
    psum x1, blocking collectives, local(): logit = lax.psum(local_logit, 'mp')  8.97 us
  transfers between devices with their start and end apart: 8, of which 8 were waited for; matrix products, arithmetic and copies ran while one was open for 11% of the time, Pallas kernels for 0%

profile of v2, /device:TPU:8, one launch (start us, length us, event | category | flops | bytes accessed | tf_op | source)
XLA Modules:
  0.0 437.6 jit_solution(6603476437160115323)
XLA Ops:
  7.2 0.9 copy.58
  8.1 0.7 copy.67
  10.7 8.1 %scatter_custom_fusion.1 = s32[4096]{0:T(1024)S(1)} fusion(s32[2048]{0:T(1024)S(1)} %bitcast.124, s32[2048]{0:T(1024)S(1)} %bitcast.121, s32[]{:T(128)} %constant.14.clone.1), kind=kCustom, calls=%fused_computation.113 | custom fusion | bytes 16388
  18.9 22.8 %all_to_all.20 = s32[4,64,16]{2,0,1:T(4,128)S(1)} all-to-all(s32[4,64,16]{2,0,1:T(4,128)S(1)} %copy.37), channel_id=1, replica_groups=mesh['dp'=64,'mp'=4] {'dp'}, dimensions={1} | all-to-all | bytes 32768 | tf_op jit(solution)/shard_map/all_to_all | solution.py:110
  41.8 2.1 fusion.14
  43.9 1.6 copy.39
  45.6 4.8 %all-to-all-start.1 = ((bf16[4,64,16,256]{3,2,0,1:T(8,128)(2,1)}), bf16[4,64,16,256]{3,2,0,1:T(8,128)(2,1)S(1)}, u32[]{:S(2)}, u32[]{:S(2)}) async-start(bf16[4,64,16,256]{3,2,0,1:T(8,128)(2,1)} %copy.39), calls=%async_computation.1 | async-start | bytes 4194304 | tf_op jit(solution)/shard_map/all_to_all | solution.py:120
  50.7 8.1 %scatter_custom_fusion = s32[4096]{0:T(1024)S(1)} fusion(s32[2048]{0:T(1024)S(1)} %bitcast.125, s32[2048]{0:T(1024)S(1)} %bitcast.123, s32[]{:T(128)} %constant.13.clone.1), kind=kCustom, calls=%fused_computation.115 | custom fusion | bytes 16388
  58.8 0.9 copy.33
  59.6 1.1 add.77
  61.1 2.8 fusion.15
  63.9 37.9 %all-to-all-done.1 = bf16[4,64,16,256]{3,2,0,1:T(8,128)(2,1)S(1)} async-done(((bf16[4,64,16,256]{3,2,0,1:T(8,128)(2,1)}), bf16[4,64,16,256]{3,2,0,1:T(8,128)(2,1)S(1)}, u32[]{:S(2)}, u32[]{:S(2)}) %all-to-all-start.1) | async-done | bytes 2097184 | tf_op jit(solution)/shard_map/all_to_all | solution.py:120
  102.0 2.1 fusion.17
  104.1 1.3 fusion.41
  105.5 0.7 copy.43
  106.2 5.3 %all-to-all-start.3 = ((s32[4,64,16]{2,0,1:T(4,128)}), s32[4,64,16]{2,0,1:T(4,128)S(1)}, u32[]{:S(2)}, u32[]{:S(2)}) async-start(s32[4,64,16]{2,0,1:T(4,128)} %copy.43), calls=%async_computation.3 | async-start | bytes 262144 | tf_op jit(solution)/shard_map/all_to_all | solution.py:144
  111.6 1.6 copy.42
  113.2 9.4 %all-to-all-done.3 = s32[4,64,16]{2,0,1:T(4,128)S(1)} async-done(((s32[4,64,16]{2,0,1:T(4,128)}), s32[4,64,16]{2,0,1:T(4,128)S(1)}, u32[]{:S(2)}, u32[]{:S(2)}) %all-to-all-start.3) | async-done | bytes 16416 | tf_op jit(solution)/shard_map/all_to_all | solution.py:144
  122.6 4.9 %all-to-all-start.2 = ((bf16[4,64,16,256]{3,2,0,1:T(8,128)(2,1)}), bf16[4,64,16,256]{3,2,0,1:T(8,128)(2,1)S(1)}, u32[]{:S(2)}, u32[]{:S(2)}) async-start(bf16[4,64,16,256]{3,2,0,1:T(8,128)(2,1)} %copy.42), calls=%async_computation.2 | async-start | bytes 4194304 | tf_op jit(solution)/shard_map/all_to_all | solution.py:137
  127.8 6.5 %all-gather.9.cloned.1.call-done = f32[1024,512]{1,0:T(8,128)} async-done(((f32[256,512]{1,0:T(8,128)}), f32[1024,512]{1,0:T(8,128)}) %all-gather.9.cloned.1.call-update) | async-done | bytes 2097168 | tf_op jit(solution)/shard_map/all_gather | solution.py:63
  134.2 1.8 reduce_sum.101
  136.1 2.8 fusion.28
  139.0 1.3 fusion.35
  140.3 33.5 %all-gather.11.cloned.1.call-done = f32[1024,512]{1,0:T(8,128)} async-done(((f32[256,512]{1,0:T(8,128)}), f32[1024,512]{1,0:T(8,128)}) %all-gather.11.cloned.1.call-update) | async-done | bytes 2097168 | tf_op jit(solution)/shard_map/all_gather | solution.py:63
  173.9 1.8 reduce_sum.102
  175.7 2.9 fusion.25
  178.9 9.0 %psum.7 = f32[256]{0:T(256)S(1)} all-reduce(f32[256]{0:T(256)S(1)} %get-tuple-element.17), channel_id=1, replica_groups=mesh['dp'=64,'mp'=4] {'mp'}, use_global_device_ids=true, to_apply=%region_8.0 | all-reduce | flops 256 | bytes 2048 | tf_op jit(solution)/shard_map/psum | solution.py:171
  188.5 2.5 fusion.31
  191.1 32.3 %all-gather.13.cloned.1.call-done = f32[1024,512]{1,0:T(8,128)} async-done(((f32[256,512]{1,0:T(8,128)}), f32[1024,512]{1,0:T(8,128)}) %all-gather.13.cloned.1.call-update) | async-done | bytes 2097168 | tf_op jit(solution)/shard_map/all_gather | solution.py:63
  223.4 2.6 reduce_sum.105
  226.0 2.1 fusion.58
  228.2 1.3 fusion.37
  229.5 1.9 convolution_bitcast_fusion.2
  231.5 1.8 convolution_bitcast_fusion
  233.2 1.9 convolution_bitcast_fusion.3
  235.2 27.9 %all-gather.15.cloned.1.call-done = f32[1024,512]{1,0:T(8,128)} async-done(((f32[256,512]{1,0:T(8,128)}), f32[1024,512]{1,0:T(8,128)}) %all-gather.15.cloned.1.call-update) | async-done | bytes 2097168 | tf_op jit(solution)/shard_map/all_gather | solution.py:63
  263.1 1.8 reduce_sum.106
  265.4 1.1 copy-done.2
  266.5 5.6 %pad_maximum_fusion = f32[4,512,1152]{2,1,0:T(8,128)} fusion(f32[4,512,128]{2,1,0:T(8,128)S(1)} %broadcast_bitcast_fusion, f32[1,512,1024]{2,1,0:T(8,128)} %convolution_bitcast_fusion, f32[1,512,1024]{2,1,0:T(8,128)S(1)} %convolution_bitcast_fusion.1, f32[1,512,1024]{2,1,0:T(8,128)S(1)} %copy-done.2, f32[1,512,1024]{2,1,0:T(8,128)} %convolution_bitcast_fusion.3), kind=kLoop, calls=%fused_computation.2 | loop fusion | flops 9437184 | bytes 18874368 | tf_op jit(solution)/shard_map/concatenate | solution.py:213
  272.2 2.9 copy.48
  275.2 1.8 copy.46
  277.0 2.9 multiply_reduce_fusion
  280.5 1.8 divide_subtract_fusion
  282.3 3.0 copy.49
  285.3 3.0 fusion.20
  288.3 140.0 %reduce-scatter.2.cloned.1.call-done = f32[4,8,1152]{2,1,0:T(8,128)} async-done(((f32[4,512,1152]{2,1,0:T(8,128)}), f32[4,8,1152]{2,1,0:T(8,128)}) %reduce-scatter.2.cloned.1.call-update) | async-done | bytes 147472 | tf_op jit(solution)/shard_map/reduce_scatter | solution.py:212
  428.2 0.7 slice_bitcast_fusion
  429.6 1.5 fusion.85
  (99 shorter events, 6.3 us)
Async XLA Ops:
  7.2 53.9 %copy-start = (bf16[4,512,256]{2,1,0:T(8,128)(2,1)S(1)}, bf16[4,512,256]{2,1,0:T(8,128)(2,1)}, u32[]{:S(2)}) copy-start(bf16[4,512,256]{2,1,0:T(8,128)(2,1)} %param.15) | copy-start | bytes 3145732
  7.2 3.2 copy-start.23
  7.2 3.3 copy-start.24
  7.2 3.1 copy-start.17
  7.2 3.1 copy-start.18
  7.2 34.6 %copy-start.9 = (f32[4,512,256]{2,1,0:T(8,128)S(1)}, f32[4,512,256]{2,1,0:T(8,128)}, u32[]{:S(2)}) copy-start(f32[4,512,256]{2,1,0:T(8,128)} %param.13) | copy-start | bytes 6291460
  45.6 5.0 %copy-start.19 = (s32[4,512]{1,0:T(4,128)S(1)}, s32[4,512]{1,0:T(4,128)}, u32[]{:S(2)}) copy-start(s32[4,512]{1,0:T(4,128)} %param.17) | copy-start | bytes 24580
  45.6 56.2 %all-to-all-start.1 = ((bf16[4,64,16,256]{3,2,0,1:T(8,128)(2,1)}), bf16[4,64,16,256]{3,2,0,1:T(8,128)(2,1)S(1)}, u32[]{:S(2)}, u32[]{:S(2)}) async-start(bf16[4,64,16,256]{3,2,0,1:T(8,128)(2,1)} %copy.39), calls=%async_computation.1 | async-start | bytes 4194304 | tf_op jit(solution)/shard_map/all_to_all | solution.py:120
  50.4 10.7 %copy-start.22 = (s32[4,256]{1,0:T(4,128)S(1)}, s32[4,256]{1,0:T(4,128)}, u32[]{:S(2)}) copy-start(s32[4,256]{1,0:T(4,128)} %param.20) | copy-start | bytes 12292
  50.4 83.8 %all-gather.9.cloned.1.call-start = ((), (), s32[]{:S(2)}) async-start(), calls=%async_computation.6 | async-start | bytes 2621440 | tf_op jit(solution)/shard_map/all_gather | solution.py:63
  101.9 2.1 copy-start.14
  104.0 23.5 %copy-start.11 = (bf16[4,256,256]{1,2,0:T(8,128)(2,1)}, bf16[4,256,256]{1,2,0:T(8,128)(2,1)S(1)}, u32[]{:S(2)}) copy-start(bf16[4,256,256]{1,2,0:T(8,128)(2,1)S(1)} %fusion.17) | copy-start | bytes 1572868
  104.0 7.5 %copy-start.10 = (bf16[4,1024,256]{2,1,0:T(8,128)(2,1)S(1)}, bf16[4,1024,256]{2,1,0:T(8,128)(2,1)}, u32[]{:S(2)}) copy-start(bf16[4,1024,256]{2,1,0:T(8,128)(2,1)} %fusion.15) | copy-start | bytes 6291460
  106.2 16.4 %all-to-all-start.3 = ((s32[4,64,16]{2,0,1:T(4,128)}), s32[4,64,16]{2,0,1:T(4,128)S(1)}, u32[]{:S(2)}, u32[]{:S(2)}) async-start(s32[4,64,16]{2,0,1:T(4,128)} %copy.43), calls=%async_computation.3 | async-start | bytes 262144 | tf_op jit(solution)/shard_map/all_to_all | solution.py:144
  113.2 14.4 %copy-start.20 = (f32[2,1024]{1,0:T(2,128)S(1)}, f32[2,1024]{1,0:T(2,128)}, u32[]{:S(2)}) copy-start(f32[2,1024]{1,0:T(2,128)} %param.24) | copy-start | bytes 24580
  122.6 56.2 %all-to-all-start.2 = ((bf16[4,64,16,256]{3,2,0,1:T(8,128)(2,1)}), bf16[4,64,16,256]{3,2,0,1:T(8,128)(2,1)S(1)}, u32[]{:S(2)}, u32[]{:S(2)}) async-start(bf16[4,64,16,256]{3,2,0,1:T(8,128)(2,1)} %copy.42), calls=%async_computation.2 | async-start | bytes 4194304 | tf_op jit(solution)/shard_map/all_to_all | solution.py:137
  127.5 46.4 %all-gather.11.cloned.1.call-start = ((), (), s32[]{:S(2)}) async-start(), calls=%async_computation.7 | async-start | bytes 2621440 | tf_op jit(solution)/shard_map/all_gather | solution.py:63
  136.1 4.1 copy-start.7
  136.1 2.8 copy-start.15
  139.0 36.8 %copy-start.16 = (f32[1024]{0:T(1024)S(1)}, f32[1024]{0:T(1024)}, u32[]{:S(2)}) copy-start(f32[1024]{0:T(1024)} %param.25) | copy-start | bytes 12292
  140.3 83.2 %all-gather.13.cloned.1.call-start = ((), (), s32[]{:S(2)}) async-start(), calls=%async_computation.8 | async-start | bytes 2621440 | tf_op jit(solution)/shard_map/all_gather | solution.py:63
  178.9 47.2 %copy-start.3 = (bf16[4,64,16,256]{3,2,0,1:T(8,128)(2,1)}, bf16[4,64,16,256]{3,2,0,1:T(8,128)(2,1)S(1)}, u32[]{:S(2)}) copy-start(bf16[4,64,16,256]{3,2,0,1:T(8,128)(2,1)S(1)} %all-to-all-done.2) | copy-start | bytes 6291460
  191.0 72.0 %all-gather.15.cloned.1.call-start = ((), (), s32[]{:S(2)}) async-start(), calls=%async_computation.9 | async-start | bytes 2621440 | tf_op jit(solution)/shard_map/all_gather | solution.py:63
  226.0 2.2 copy-start.5
  229.4 2.0 copy-start.13
  229.5 198.8 %reduce-scatter.2.cloned.1.call-start = ((), (), s32[]{:S(2)}) async-start(), calls=%async_computation.5 | async-start | bytes 9584640 | tf_op jit(solution)/shard_map/reduce_scatter | solution.py:212
  231.4 1.8 copy-start.8
  235.1 29.8 %copy-start.12 = (bf16[4,256,256]{1,2,0:T(8,128)(2,1)S(1)}, bf16[4,256,256]{1,2,0:T(8,128)(2,1)}, u32[]{:S(2)}) copy-start(bf16[4,256,256]{1,2,0:T(8,128)(2,1)} %copy-done.11) | copy-start | bytes 1572868
  264.9 1.6 copy-start.2
  277.0 2.9 copy-start.21
  277.0 3.5 copy-start.4
  282.3 3.0 copy-start.6
  285.3 145.8 %copy-start.1 = (bf16[4,512,256]{2,1,0:T(8,128)(2,1)S(1)}, bf16[4,512,256]{2,1,0:T(8,128)(2,1)}, u32[]{:S(2)}) copy-start(bf16[4,512,256]{2,1,0:T(8,128)(2,1)} %param.15) | copy-start | bytes 3145732
Sparse Core Ops, SparseCore 0:
  105.5 28.7 all-gather.8
  140.4 33.4 all-gather.10
  191.2 32.2 all-gather.12
  229.6 33.4 all-gather.14
  272.3 155.9 reduce-scatter.1

commit v3 on v0

--- a/solution.py
+++ b/solution.py
@@ -102,22 +102,6 @@
         concat_axis=1,
         tiled=True,
     )
-    recv_rows = lax.all_to_all(
-        send_rows.reshape(local_feats, peers, grad_cap),
-        "dp",
-        split_axis=1,
-        concat_axis=1,
-        tiled=True,
-    )
-    landing = selection_matrix(recv_rows.reshape(local_feats, grad_total), rows_per_shard)
-    summed = jnp.einsum(
-        "wjc,wjl->wcl",
-        landing,
-        recv_grads.reshape(local_feats, grad_total, width),
-        preferred_element_type=jnp.float32,
-    )
-    new_accum = accum + jnp.mean(summed * summed, axis=2)
-    new_table = embed_table - learn_rate * summed / jnp.sqrt(new_accum)[:, :, None]
     batch_dev = bag_len.shape[1]
     look_dev = lookup_row.shape[1]
     bag_size = look_dev // batch_dev
@@ -127,9 +111,22 @@
     wanted = (
         jnp.zeros((local_feats, look_total), jnp.int32).at[which_feature, look_slot].set(lookup_row)
     )
-    requested_ids = lax.all_to_all(
-        wanted.reshape(local_feats, peers, look_cap), "dp", split_axis=1, concat_axis=1, tiled=True
-    ).reshape(local_feats, look_total)
+    both_ids = jnp.concatenate(
+        (wanted.reshape(local_feats, peers, look_cap), send_rows.reshape(local_feats, peers, grad_cap)),
+        axis=2,
+    )
+    both_ids = lax.all_to_all(both_ids, "dp", split_axis=1, concat_axis=1, tiled=True)
+    requested_ids = both_ids[:, :, :look_cap].reshape(local_feats, look_total)
+    recv_rows = both_ids[:, :, look_cap:]
+    landing = selection_matrix(recv_rows.reshape(local_feats, grad_total), rows_per_shard)
+    summed = jnp.einsum(
+        "wjc,wjl->wcl",
+        landing,
+        recv_grads.reshape(local_feats, grad_total, width),
+        preferred_element_type=jnp.float32,
+    )
+    new_accum = accum + jnp.mean(summed * summed, axis=2)
+    new_table = embed_table - learn_rate * summed / jnp.sqrt(new_accum)[:, :, None]
     second_table = embed_table.astype(jnp.bfloat16)
     served = jnp.einsum(
         "adv,avm->adm",
@@ -192,10 +189,19 @@
         upstream = upstream + jnp.dot(back_sum, v_weight[layer], preferred_element_type=jnp.float32)
         grads_u[layer] = grad_u_layer
         grads_v[layer] = down_factor_gradient
-    grad_u = jnp.stack(grads_u)
-    grad_v = jnp.stack(grads_v)
-    grad_u, grad_v = side_by_side((grad_u, grad_v), "dp", 1, 0)
-    grad_small = over_copies(jnp.stack(bias_grads + [head_grad]), "dp")
+    small = jnp.stack(bias_grads + [head_grad])
+    rest = lax.psum_scatter(
+        jnp.stack((grads_u[1], grads_v[1], grads_v[0])), "dp", scatter_dimension=1, tiled=True
+    )
+    parts_u = in_blocks(grads_u[0], 0, peers)
+    block_rows, cols = parts_u.shape[1:]
+    small_rows = jnp.broadcast_to(small.reshape(block_rows, -1), (peers, block_rows, small.size // block_rows))
+    arrived = lax.all_to_all(
+        jnp.concatenate((parts_u, small_rows), axis=2), "dp", split_axis=0, concat_axis=0, tiled=True
+    ).sum(axis=0)
+    grad_u = jnp.stack((arrived[:, :cols], rest[0]))
+    grad_v = jnp.stack((rest[2], rest[1]))
+    grad_small = arrived[:, cols:].reshape(small.shape)
     grad_pooled = (upstream + to_start).astype(jnp.bfloat16)
     return (new_table, new_accum, grad_u, grad_v, grad_small, grad_pooled)
 

time: 406 us -> 428 us (1.054)
  waiting for transfers between devices: 186 us -> 210 us
  starting transfers between devices: 40.8 us -> 34.9 us
  other arithmetic: 16.9 us -> 22.4 us
    all_to_all x1, waiting for transfers between devices: 7.92 us -> 64.4 us  [local(): lax.all_to_all(jnp.concatenate((parts_u, small_rows), axis=2), 'dp', spli...]
    all_to_all x2 -> x1, waiting for transfers between devices: 33.8 us -> 12 us  [copy_for_each(): return lax.all_to_all(copies, axis, split_axis=0, concat_axis=0, tiled=True)]
    all_to_all x1, waiting for transfers between devices: 51.6 us -> 35.4 us  [local(): lax.all_to_all(send_grads.reshape(local_feats, peers, grad_cap, width), '...]
    all_to_all x2 -> x1, starting transfers between devices: 12.7 us -> 5.99 us  [copy_for_each(): return lax.all_to_all(copies, axis, split_axis=0, concat_axis=0, tiled=True)]
    another operation x1 -> x4, other arithmetic: 0.02 us -> 6.28 us  [the longest x1 4.99 us: local(): jnp.stack((grads_u[1], grads_v[1], grads_v[0]))]
    reduce_scatter x1, waiting for transfers between devices: 30.5 us -> 36.3 us  [local(): lax.psum_scatter(jnp.stack((grads_u[1], grads_v[1], grads_v[0])), 'dp', s...]
    unnamed x58 -> x62, local copies, waits for them, and re-layouts: 25.5 us -> 27.4 us
  transfers between devices with their start and end apart: 8 -> 7, of which waited for: 8 -> 7; matrix products, arithmetic and copies ran while one was open for 10% -> 9% of each run, Pallas kernels for 0% -> 0%
where the time goes in v3:
time: 428 us; the launch traced here: 427 us
  waiting for transfers between devices  210 us (49%)
  blocking collectives  74.8 us (17%)
  local copies, waits for them, and re-layouts  39.4 us (9%)
  starting transfers between devices  34.9 us (8%)
  matrix products  31.2 us (7%)
  other arithmetic  22.4 us (5%)
  between operations  14.5 us (3%)
    all_to_all x1, waiting for transfers between devices, local(): lax.all_to_all(jnp.concatenate((parts_u, small_rows), axis=2), 'dp', spli...  64.4 us
    all_to_all x1, waiting for transfers between devices, local(): lax.all_to_all(served.reshape(local_feats, peers, look_cap, width), 'dp',...  48.2 us
    reduce_scatter x1, waiting for transfers between devices, local(): lax.psum_scatter(jnp.stack((grads_u[1], grads_v[1], grads_v[0])), 'dp', s...  36.3 us
    all_to_all x1, waiting for transfers between devices, local(): lax.all_to_all(send_grads.reshape(local_feats, peers, grad_cap, width), '...  35.4 us
    unnamed x62, local copies, waits for them, and re-layouts  27.4 us
    all_gather x2, blocking collectives, cross_down(): return lax.all_gather(share.astype(jnp.bfloat16), 'mp', axis=0, tiled=True)  23.8 us
    all_to_all x1, blocking collectives, local(): lax.all_to_all(both_ids, 'dp', split_axis=1, concat_axis=1, tiled=True)  21.3 us
    all_to_all x1, blocking collectives, copy_for_each(): return lax.all_to_all(copies, axis, split_axis=0, concat_axis=0, tiled=True)  19.6 us
  transfers between devices with their start and end apart: 7, of which 7 were waited for; matrix products, arithmetic and copies ran while one was open for 9% of the time, Pallas kernels for 0%

profile of v3, /device:TPU:8, one launch (start us, length us, event | category | flops | bytes accessed | tf_op | source)
XLA Modules:
  0.0 427.0 jit_solution(17004265981673306412)
XLA Ops:
  12.0 8.1 %scatter_custom_fusion = s32[4096]{0:T(1024)S(1)} fusion(s32[2048]{0:T(1024)S(1)} %bitcast.128, s32[2048]{0:T(1024)S(1)} %bitcast.126, s32[]{:T(128)} %constant.11.clone.1), kind=kCustom, calls=%fused_computation.116 | custom fusion | bytes 16388
  20.1 8.1 %scatter_custom_fusion.1 = s32[4096]{0:T(1024)S(1)} fusion(s32[2048]{0:T(1024)S(1)} %bitcast.127, s32[2048]{0:T(1024)S(1)} %bitcast.125, s32[]{:T(128)} %constant.6.clone.1), kind=kCustom, calls=%fused_computation.114 | custom fusion | bytes 16388
  28.6 21.3 %all_to_all.40 = s32[64,1,128]{2,1,0:T(1,128)S(1)} all-to-all(s32[64,1,128]{2,1,0:T(1,128)S(1)} %reshape.139), channel_id=1, replica_groups=mesh['dp'=64,'mp'=4] {'dp'}, dimensions={0} | all-to-all | bytes 65536 | tf_op jit(solution)/shard_map/all_to_all | solution.py:118
  51.6 2.1 fusion.14
  53.7 1.6 copy.63
  55.3 4.7 %all-to-all-start.2 = ((bf16[4,64,16,256]{3,2,0,1:T(8,128)(2,1)}), bf16[4,64,16,256]{3,2,0,1:T(8,128)(2,1)S(1)}, u32[]{:S(2)}, u32[]{:S(2)}) async-start(bf16[4,64,16,256]{3,2,0,1:T(8,128)(2,1)} %copy.63), calls=%async_computation.2 | async-start | bytes 4194304 | tf_op jit(solution)/shard_map/all_to_all | solution.py:137
  61.1 1.1 add.78
  63.2 48.2 %all-to-all-done.2 = bf16[4,64,16,256]{3,2,0,1:T(8,128)(2,1)S(1)} async-done(((bf16[4,64,16,256]{3,2,0,1:T(8,128)(2,1)}), bf16[4,64,16,256]{3,2,0,1:T(8,128)(2,1)S(1)}, u32[]{:S(2)}, u32[]{:S(2)}) %all-to-all-start.2) | async-done | bytes 2097184 | tf_op jit(solution)/shard_map/all_to_all | solution.py:137
  111.6 2.1 fusion.17
  114.3 2.5 fusion.39
  116.8 4.9 %all-to-all-start.3 = ((f32[4,64,512]{2,1,0:T(8,128)}), f32[4,64,512]{2,1,0:T(8,128)S(1)}, u32[]{:S(2)}, u32[]{:S(2)}) async-start(f32[4,64,512]{2,1,0:T(8,128)} %fusion.39), calls=%async_computation.3 | async-start | bytes 1048576 | tf_op jit(solution)/shard_map/all_to_all | solution.py:17
  122.0 6.4 %all-to-all-done.3 = f32[4,64,512]{2,1,0:T(8,128)S(1)} async-done(((f32[4,64,512]{2,1,0:T(8,128)}), f32[4,64,512]{2,1,0:T(8,128)S(1)}, u32[]{:S(2)}, u32[]{:S(2)}) %all-to-all-start.3) | async-done | bytes 524320 | tf_op jit(solution)/shard_map/all_to_all | solution.py:17
  128.4 11.8 %all_gather.6 = bf16[256,512]{1,0:T(8,128)(2,1)S(1)} all-gather(bf16[64,512]{1,0:T(8,128)(2,1)S(1)} %reduce_sum.111), channel_id=1, replica_groups=mesh['dp'=64,'mp'=4] {'mp'}, dimensions={0}, use_global_device_ids=true | all-gather | bytes 327680 | tf_op jit(solution)/shard_map/all_gather | solution.py:64
  140.2 2.8 fusion.26
  143.0 1.3 fusion.33
  144.2 5.5 %all-to-all-start.4 = ((f32[4,64,512]{2,1,0:T(8,128)}), f32[4,64,512]{2,1,0:T(8,128)S(1)}, u32[]{:S(2)}, u32[]{:S(2)}) async-start(f32[4,64,512]{2,1,0:T(8,128)} %fusion.33), calls=%async_computation.4 | async-start | bytes 1048576 | tf_op jit(solution)/shard_map/all_to_all | solution.py:17
  149.8 7.0 %all-to-all-done.4 = f32[4,64,512]{2,1,0:T(8,128)S(1)} async-done(((f32[4,64,512]{2,1,0:T(8,128)}), f32[4,64,512]{2,1,0:T(8,128)S(1)}, u32[]{:S(2)}, u32[]{:S(2)}) %all-to-all-start.4) | async-done | bytes 524320 | tf_op jit(solution)/shard_map/all_to_all | solution.py:17
  157.4 12.0 %all_gather.7 = bf16[256,512]{1,0:T(8,128)(2,1)S(1)} all-gather(bf16[64,512]{1,0:T(8,128)(2,1)} %reduce_sum.112), channel_id=1, replica_groups=mesh['dp'=64,'mp'=4] {'mp'}, dimensions={0}, use_global_device_ids=true | all-gather | bytes 327680 | tf_op jit(solution)/shard_map/all_gather | solution.py:64
  169.4 2.9 fusion.23
  172.3 10.1 %psum.7 = f32[256]{0:T(256)S(1)} all-reduce(f32[256]{0:T(256)S(1)} %get-tuple-element.34), channel_id=1, replica_groups=mesh['dp'=64,'mp'=4] {'mp'}, use_global_device_ids=true, to_apply=%region_8.0 | all-reduce | flops 256 | bytes 2048 | tf_op jit(solution)/shard_map/psum | solution.py:169
  182.4 1.0 fusion.42
  183.4 1.7 fusion.30
  185.3 19.6 %all_to_all.41 = f32[4,256,512]{2,1,0:T(8,128)} all-to-all(f32[4,256,512]{2,1,0:T(8,128)S(1)} %broadcast_in_dim.18), channel_id=1, replica_groups=mesh['dp'=64,'mp'=4] {'mp'}, dimensions={0} | all-to-all | bytes 4194304 | tf_op jit(solution)/shard_map/all_to_all | solution.py:23
  204.9 2.6 reduce_sum.114
  207.5 2.5 fusion.59
  210.5 1.6 broadcast_in_dim.20
  212.1 6.0 %all-to-all-start.7 = ((f32[4,256,512]{2,1,0:T(8,128)}), f32[4,256,512]{2,1,0:T(8,128)}, u32[]{:S(2)}, u32[]{:S(2)}) async-start(f32[4,256,512]{2,1,0:T(8,128)} %broadcast_in_dim.20), calls=%async_computation.7 | async-start | bytes 4194304 | tf_op jit(solution)/shard_map/all_to_all | solution.py:23
  218.1 1.5 fusion.15
  219.6 1.6 copy.54
  221.2 12.0 %all-to-all-done.7 = f32[4,256,512]{2,1,0:T(8,128)} async-done(((f32[4,256,512]{2,1,0:T(8,128)}), f32[4,256,512]{2,1,0:T(8,128)}, u32[]{:S(2)}, u32[]{:S(2)}) %all-to-all-start.7) | async-done | bytes 2097184 | tf_op jit(solution)/shard_map/all_to_all | solution.py:23
  233.2 8.2 %all-to-all-start.1 = ((bf16[4,64,16,256]{3,2,0,1:T(8,128)(2,1)}), bf16[4,64,16,256]{3,2,0,1:T(8,128)(2,1)}, u32[]{:S(2)}, u32[]{:S(2)}) async-start(bf16[4,64,16,256]{3,2,0,1:T(8,128)(2,1)} %copy.54), calls=%async_computation.1 | async-start | bytes 4194304 | tf_op jit(solution)/shard_map/all_to_all | solution.py:98
  241.5 1.8 convolution_bitcast_fusion.2
  243.3 1.8 convolution_bitcast_fusion.1
  245.1 1.8 reduce_sum.119
  247.5 1.1 copy-done.3
  248.6 5.0 %pad_maximum_fusion = f32[3,512,1024]{2,1,0:T(8,128)} fusion(f32[1,512,1024]{2,1,0:T(8,128)S(1)} %convolution_bitcast_fusion, f32[1,512,1024]{2,1,0:T(8,128)} %convolution_bitcast_fusion.1, f32[1,512,1024]{2,1,0:T(8,128)S(1)} %copy-done.3), kind=kLoop, calls=%fused_computation.8 | loop fusion | flops 3145728 | bytes 12582912 | tf_op jit(solution)/shard_map/stack | solution.py:194
  255.4 1.8 pad_maximum_fusion.1
  257.2 35.4 %all-to-all-done.1 = bf16[4,64,16,256]{3,2,0,1:T(8,128)(2,1)} async-done(((bf16[4,64,16,256]{3,2,0,1:T(8,128)(2,1)}), bf16[4,64,16,256]{3,2,0,1:T(8,128)(2,1)}, u32[]{:S(2)}, u32[]{:S(2)}) %all-to-all-start.1) | async-done | bytes 2097184 | tf_op jit(solution)/shard_map/all_to_all | solution.py:98
  292.6 5.6 %all-to-all-start.6 = ((f32[64,8,1408]{2,1,0:T(8,128)}), f32[64,8,1408]{2,1,0:T(8,128)}, u32[]{:S(2)}, u32[]{:S(2)}) async-start(f32[64,8,1408]{2,1,0:T(8,128)} %pad_maximum_fusion.1), calls=%async_computation.6 | async-start | bytes 5767168 | tf_op jit(solution)/shard_map/all_to_all | solution.py:199
  298.2 2.9 copy.57
  301.3 1.8 copy.55
  303.1 2.9 multiply_reduce_fusion
  306.6 1.9 divide_subtract_fusion
  308.5 2.9 copy.68
  311.4 3.3 fusion.20
  314.7 64.4 %all-to-all-done.6 = f32[64,8,1408]{2,1,0:T(8,128)} async-done(((f32[64,8,1408]{2,1,0:T(8,128)}), f32[64,8,1408]{2,1,0:T(8,128)}, u32[]{:S(2)}, u32[]{:S(2)}) %all-to-all-start.6) | async-done | bytes 2883616 | tf_op jit(solution)/shard_map/all_to_all | solution.py:199
  379.1 2.0 reduce_sum.118
  381.7 36.3 %reduce-scatter.2.cloned.1.call-done = f32[3,8,1024]{2,1,0:T(8,128)} async-done(((f32[3,512,1024]{2,1,0:T(8,128)}), f32[3,8,1024]{2,1,0:T(8,128)}) %reduce-scatter.2.cloned.1.call-update) | async-done | bytes 98320 | tf_op jit(solution)/shard_map/reduce_scatter | solution.py:193
  (110 shorter events, 17.1 us)
Async XLA Ops:
  7.2 210.9 %copy-start = (bf16[4,512,256]{2,1,0:T(8,128)(2,1)S(1)}, bf16[4,512,256]{2,1,0:T(8,128)(2,1)}, u32[]{:S(2)}) copy-start(bf16[4,512,256]{2,1,0:T(8,128)(2,1)} %param.15) | copy-start | bytes 3145732
  7.2 4.5 %copy-start.22 = (s32[2]{0:T(128)S(1)}, s32[2]{0:T(128)}, u32[]{:S(2)}) copy-start(s32[2]{0:T(128)} %constant.33) | copy-start | bytes 28
  7.2 4.6 %copy-start.23 = (s32[2]{0:T(128)S(1)}, s32[2]{0:T(128)}, u32[]{:S(2)}) copy-start(s32[2]{0:T(128)} %constant.30) | copy-start | bytes 28
  7.2 3.8 copy-start.14
  7.2 4.4 %copy-start.15 = (s32[4,512,1]{1,2,0:T(1,128)S(1)}, s32[4,512,1]{1,2,0:T(1,128)}, u32[]{:S(2)}) copy-start(s32[4,512,1]{1,2,0:T(1,128)} %param.18) | copy-start | bytes 24580
  9.8 41.9 %copy-start.10 = (f32[4,512,256]{2,1,0:T(8,128)S(1)}, f32[4,512,256]{2,1,0:T(8,128)}, u32[]{:S(2)}) copy-start(f32[4,512,256]{2,1,0:T(8,128)} %param.13) | copy-start | bytes 6291460
  55.3 56.1 %all-to-all-start.2 = ((bf16[4,64,16,256]{3,2,0,1:T(8,128)(2,1)}), bf16[4,64,16,256]{3,2,0,1:T(8,128)(2,1)S(1)}, u32[]{:S(2)}, u32[]{:S(2)}) async-start(bf16[4,64,16,256]{3,2,0,1:T(8,128)(2,1)} %copy.63), calls=%async_computation.2 | async-start | bytes 4194304 | tf_op jit(solution)/shard_map/all_to_all | solution.py:137
  113.9 7.8 %copy-start.18 = (f32[2,1024]{1,0:T(2,128)S(1)}, f32[2,1024]{1,0:T(2,128)}, u32[]{:S(2)}) copy-start(f32[2,1024]{1,0:T(2,128)} %param.24) | copy-start | bytes 24580
  116.8 11.5 %all-to-all-start.3 = ((f32[4,64,512]{2,1,0:T(8,128)}), f32[4,64,512]{2,1,0:T(8,128)S(1)}, u32[]{:S(2)}, u32[]{:S(2)}) async-start(f32[4,64,512]{2,1,0:T(8,128)} %fusion.39), calls=%async_computation.3 | async-start | bytes 1048576 | tf_op jit(solution)/shard_map/all_to_all | solution.py:17
  128.4 14.6 %copy-start.12 = (bf16[2,512,1024]{2,1,0:T(8,128)(2,1)S(1)}, bf16[2,512,1024]{2,1,0:T(8,128)(2,1)}, u32[]{:S(2)}) copy-start(bf16[2,512,1024]{2,1,0:T(8,128)(2,1)} %param.23) | copy-start | bytes 6291460
  140.2 4.1 copy-start.7
  143.0 26.4 %copy-start.5 = (bf16[256,1024]{1,0:T(8,128)(2,1)}, bf16[256,1024]{1,0:T(8,128)(2,1)S(1)}, u32[]{:S(2)}) copy-start(bf16[256,1024]{1,0:T(8,128)(2,1)S(1)} %get-tuple-element.57) | copy-start | bytes 1572868
  143.0 6.8 %copy-start.13 = (f32[1024]{0:T(1024)S(1)}, f32[1024]{0:T(1024)}, u32[]{:S(2)}) copy-start(f32[1024]{0:T(1024)} %param.25) | copy-start | bytes 12292
  144.2 12.5 %all-to-all-start.4 = ((f32[4,64,512]{2,1,0:T(8,128)}), f32[4,64,512]{2,1,0:T(8,128)S(1)}, u32[]{:S(2)}, u32[]{:S(2)}) async-start(f32[4,64,512]{2,1,0:T(8,128)} %fusion.33), calls=%async_computation.4 | async-start | bytes 1048576 | tf_op jit(solution)/shard_map/all_to_all | solution.py:17
  157.4 25.0 %copy-start.21 = (s32[256]{0:T(256)S(1)}, s32[256]{0:T(256)}, u32[]{:S(2)}) copy-start(s32[256]{0:T(256)} %param.21) | copy-start | bytes 3076
  207.5 2.5 copy-start.4
  212.1 6.0 %copy-start.16 = (s32[4,512,1]{1,2,0:T(1,128)S(1)}, s32[4,512,1]{1,2,0:T(1,128)}, u32[]{:S(2)}) copy-start(s32[4,512,1]{1,2,0:T(1,128)} %get-tuple-element.39) | copy-start | bytes 24580
  212.1 21.1 %all-to-all-start.7 = ((f32[4,256,512]{2,1,0:T(8,128)}), f32[4,256,512]{2,1,0:T(8,128)}, u32[]{:S(2)}, u32[]{:S(2)}) async-start(f32[4,256,512]{2,1,0:T(8,128)} %broadcast_in_dim.20), calls=%async_computation.7 | async-start | bytes 4194304 | tf_op jit(solution)/shard_map/all_to_all | solution.py:23
  233.2 59.4 %all-to-all-start.1 = ((bf16[4,64,16,256]{3,2,0,1:T(8,128)(2,1)}), bf16[4,64,16,256]{3,2,0,1:T(8,128)(2,1)}, u32[]{:S(2)}, u32[]{:S(2)}) async-start(bf16[4,64,16,256]{3,2,0,1:T(8,128)(2,1)} %copy.54), calls=%async_computation.1 | async-start | bytes 4194304 | tf_op jit(solution)/shard_map/all_to_all | solution.py:98
  241.4 1.9 copy-start.6
  241.4 1.9 copy-start.11
  241.4 176.6 %reduce-scatter.2.cloned.1.call-start = ((), (), s32[]{:S(2)}) async-start(), calls=%async_computation.9 | async-start | bytes 6389760 | tf_op jit(solution)/shard_map/reduce_scatter | solution.py:193
  247.0 1.6 copy-start.3
  253.6 0.7 copy-start.17
  253.6 1.1 copy-start.9
  253.6 1.2 copy-start.20
  253.6 1.3 copy-start.8
  292.6 86.5 %all-to-all-start.6 = ((f32[64,8,1408]{2,1,0:T(8,128)}), f32[64,8,1408]{2,1,0:T(8,128)}, u32[]{:S(2)}, u32[]{:S(2)}) async-start(f32[64,8,1408]{2,1,0:T(8,128)} %pad_maximum_fusion.1), calls=%async_computation.6 | async-start | bytes 5767168 | tf_op jit(solution)/shard_map/all_to_all | solution.py:199
  303.1 2.9 copy-start.19
  303.1 3.5 copy-start.2
  311.4 108.7 %copy-start.1 = (bf16[4,512,256]{2,1,0:T(8,128)(2,1)S(1)}, bf16[4,512,256]{2,1,0:T(8,128)(2,1)}, u32[]{:S(2)}) copy-start(bf16[4,512,256]{2,1,0:T(8,128)(2,1)} %param.15) | copy-start | bytes 3145732
Sparse Core Ops, SparseCore 0:
  253.7 164.3 reduce-scatter.1

commit v4 on v2

--- a/solution.py
+++ b/solution.py
@@ -25,6 +25,15 @@
 
 def over_copies(array, axis):
     return copy_for_each(array, axis).sum(axis=0)
+
+
+def butterfly_sum(array, axis):
+    peers = lax.axis_size(axis)
+    step = 1
+    while step < peers:
+        array = array + lax.ppermute(array, axis, [(i, i ^ step) for i in range(peers)])
+        step *= 2
+    return array
 
 
 def side_by_side(arrays, axis, dim, along):
@@ -59,12 +68,9 @@
     )
 
 
-def summed_rounded(partial, axis):
-    return lax.all_gather(partial, axis, axis=0).sum(axis=0).astype(jnp.bfloat16)
-
-
 def cross_down(state, v_layer):
-    return summed_rounded(contract_last(state, v_layer), "mp")
+    share = sum_at_owner(contract_last(state, v_layer), "mp", 0)
+    return lax.all_gather(share.astype(jnp.bfloat16), "mp", axis=0, tiled=True)
 
 
 def local(
@@ -107,9 +113,13 @@
     wanted = (
         jnp.zeros((local_feats, look_total), jnp.int32).at[which_feature, look_slot].set(lookup_row)
     )
-    requested_ids = lax.all_to_all(
-        wanted.reshape(local_feats, peers, look_cap), "dp", split_axis=1, concat_axis=1, tiled=True
-    ).reshape(local_feats, look_total)
+    both_ids = jnp.concatenate(
+        (wanted.reshape(local_feats, peers, look_cap), send_rows.reshape(local_feats, peers, grad_cap)),
+        axis=2,
+    )
+    both_ids = lax.all_to_all(both_ids, "dp", split_axis=1, concat_axis=1, tiled=True)
+    requested_ids = both_ids[:, :, :look_cap].reshape(local_feats, look_total)
+    recv_rows = both_ids[:, :, look_cap:]
     second_table = embed_table.astype(jnp.bfloat16)
     served = jnp.einsum(
         "adv,avm->adm",
@@ -133,16 +143,9 @@
         "fbs,fse->fbe", mixing, returned, preferred_element_type=jnp.float32
     ).astype(jnp.bfloat16)
     start = jnp.transpose(pooled, (1, 0, 2)).reshape(batch_dev, local_feats * width)
-    send_grads, send_rows, start = lax.optimization_barrier((send_grads, send_rows, start))
+    send_grads, start = lax.optimization_barrier((send_grads, start))
     recv_grads = lax.all_to_all(
         send_grads.reshape(local_feats, peers, grad_cap, width),
-        "dp",
-        split_axis=1,
-        concat_axis=1,
-        tiled=True,
-    )
-    recv_rows = lax.all_to_all(
-        send_rows.reshape(local_feats, peers, grad_cap),
         "dp",
         split_axis=1,
         concat_axis=1,
@@ -165,9 +168,7 @@
         crosses.append(cross_out)
         state = (start_f * cross_out + state.astype(jnp.float32)).astype(jnp.bfloat16)
     local_logit = jnp.sum(state.astype(jnp.float32) * head_weight[None, :], axis=1)
-    recv_grads, recv_rows, local_logit = lax.optimization_barrier(
-        (recv_grads, recv_rows, local_logit)
-    )
+    recv_grads, local_logit = lax.optimization_barrier((recv_grads, local_logit))
     logit = lax.psum(local_logit, "mp")
     slope = (jax.nn.sigmoid(logit) - label.astype(jnp.float32)) / jnp.sqrt(
         jnp.float32(batch_dev * peers)
@@ -183,9 +184,9 @@
         bias_grads[layer] = jnp.sum(direct, axis=0)
         direct_bias_term = direct.astype(jnp.bfloat16)
         grad_u_layer = contract_first(downs[layer], direct_bias_term)
-        back_sum = summed_rounded(
+        back_sum = over_copies(
             contract_last(direct_bias_term, up_factor_weight[layer]), "mp"
-        )
+        ).astype(jnp.bfloat16)
         down_factor_gradient = contract_first(back_sum, states[layer])
         to_start = to_start + upstream * crosses[layer]
         upstream = upstream + jnp.dot(back_sum, v_weight[layer], preferred_element_type=jnp.float32)
@@ -202,18 +203,8 @@
     new_table = embed_table - learn_rate * summed / jnp.sqrt(new_accum)[:, :, None]
     grad_u = jnp.stack(grads_u)
     grad_v = jnp.stack(grads_v)
-    small = jnp.stack(bias_grads + [head_grad])
-    both = jnp.concatenate((grad_u, grad_v), axis=0)
-    lead, rows, cols = both.shape
-    block_rows = rows // peers
-    extra = -(-small.size // (lead * block_rows * 128)) * 128
-    small_block = jnp.pad(small.reshape(-1), (0, lead * block_rows * extra - small.size))
-    small_rep = jnp.tile(small_block.reshape(lead, block_rows, extra), (1, peers, 1))
-    filled = lax.psum_scatter(
-        jnp.concatenate((both, small_rep), axis=2), "dp", scatter_dimension=1, tiled=True
-    )
-    grad_u, grad_v = jnp.split(filled[:, :, :cols], 2, axis=0)
-    grad_small = filled[:, :, cols:].reshape(-1)[: small.size].reshape(small.shape)
+    grad_u, grad_v = side_by_side((grad_u, grad_v), "dp", 1, 0)
+    grad_small = butterfly_sum(jnp.stack(bias_grads + [head_grad]), "dp")
     grad_pooled = (upstream + to_start).astype(jnp.bfloat16)
     return (new_table, new_accum, grad_u, grad_v, grad_small, grad_pooled)
 

time: 439 us -> 452 us (1.030)
  waiting for transfers between devices: 288 us -> 229 us
  blocking collectives: 31.8 us -> 79.4 us
  starting transfers between devices: 15.2 us -> 40 us
    all_gather x4 -> x0, waiting for transfers between devices: 100 us -> none  [summed_rounded(): lax.all_gather(partial, axis, axis=0).sum(axis=0).astype(jnp.bfloat16)]
    all_to_all x1, waiting for transfers between devices: 0.26 us -> 34.9 us  [local(): lax.all_to_all(send_grads.reshape(local_feats, peers, grad_cap, width), '...]
    reduce_scatter x1, waiting for transfers between devices: 140 us -> 115 us  [side_by_side(): filled = lax.psum_scatter(both, axis, scatter_dimension=dim, tiled=True)]
    all_to_all x1 -> x2, blocking collectives: 22.8 us -> 46.6 us  [the longest x1 25.3 us: copy_for_each(): return lax.all_to_all(copies, axis, split_axis=0, concat_axis=0, tiled=True)]
    all_gather x0 -> x2, blocking collectives: none -> 23.6 us  [cross_down(): return lax.all_gather(share.astype(jnp.bfloat16), 'mp', axis=0, tiled=True)]
    all_to_all x1 -> x3, waiting for transfers between devices: 9.41 us -> 26.9 us  [the longest x1 15.1 us: copy_for_each(): return lax.all_to_all(copies, axis, split_axis=0, concat_axis=0, tiled=True)]
    all_to_all x1 -> x3, starting transfers between devices: 5.33 us -> 16.9 us  [the longest x2 11.1 us: sum_at_owner(): lax.all_to_all(parts, axis, split_axis=0, concat_axis=0, tiled=True)]
    ppermute x0 -> x6, starting transfers between devices: none -> 11.3 us  [butterfly_sum(): lax.ppermute(array, axis, [(i, i ^ step) for i in range(peers)])]
  transfers between devices with their start and end apart: 8 -> 12, of which waited for: 8 -> 10; matrix products, arithmetic and copies ran while one was open for 11% -> 8% of each run, Pallas kernels for 0% -> 0%
where the time goes in v4:
time: 452 us; the launch traced here: 450 us
  waiting for transfers between devices  229 us (51%)
  blocking collectives  79.4 us (18%)
  starting transfers between devices  40 us (9%)
  local copies, waits for them, and re-layouts  38.6 us (9%)
  matrix products  32 us (7%)
  other arithmetic  17.1 us (4%)
  between operations  14.5 us (3%)
    reduce_scatter x1, waiting for transfers between devices, side_by_side(): filled = lax.psum_scatter(both, axis, scatter_dimension=dim, tiled=True)  115 us
    all_to_all x1, waiting for transfers between devices, local(): lax.all_to_all(served.reshape(local_feats, peers, look_cap, width), 'dp',...  44.7 us
    all_to_all x1, waiting for transfers between devices, local(): lax.all_to_all(send_grads.reshape(local_feats, peers, grad_cap, width), '...  34.9 us
    unnamed x59, local copies, waits for them, and re-layouts  27.2 us
    all_to_all x1, blocking collectives, copy_for_each(): return lax.all_to_all(copies, axis, split_axis=0, concat_axis=0, tiled=True)  25.3 us
    all_gather x2, blocking collectives, cross_down(): return lax.all_gather(share.astype(jnp.bfloat16), 'mp', axis=0, tiled=True)  23.6 us
    all_to_all x1, blocking collectives, local(): lax.all_to_all(both_ids, 'dp', split_axis=1, concat_axis=1, tiled=True)  21.3 us
    all_to_all x1, waiting for transfers between devices, copy_for_each(): return lax.all_to_all(copies, axis, split_axis=0, concat_axis=0, tiled=True)  15.1 us
  transfers between devices with their start and end apart: 12, of which 10 were waited for; matrix products, arithmetic and copies ran while one was open for 8% of the time, Pallas kernels for 0%

profile of v4, /device:TPU:8, one launch (start us, length us, event | category | flops | bytes accessed | tf_op | source)
XLA Modules:
  0.0 450.4 jit_solution(9479145776542777172)
XLA Ops:
  12.0 8.1 %scatter_custom_fusion = s32[4096]{0:T(1024)S(1)} fusion(s32[2048]{0:T(1024)S(1)} %bitcast.127, s32[2048]{0:T(1024)S(1)} %bitcast.124, s32[]{:T(128)} %constant.11.clone.1), kind=kCustom, calls=%fused_computation.108 | custom fusion | bytes 16388
  20.1 8.1 %scatter_custom_fusion.1 = s32[4096]{0:T(1024)S(1)} fusion(s32[2048]{0:T(1024)S(1)} %bitcast.126, s32[2048]{0:T(1024)S(1)} %bitcast.123, s32[]{:T(128)} %constant.6.clone.1), kind=kCustom, calls=%fused_computation.106 | custom fusion | bytes 16388
  28.6 21.3 %all_to_all.35 = s32[64,1,128]{2,1,0:T(1,128)S(1)} all-to-all(s32[64,1,128]{2,1,0:T(1,128)S(1)} %reshape.107), channel_id=1, replica_groups=mesh['dp'=64,'mp'=4] {'dp'}, dimensions={0} | all-to-all | bytes 65536 | tf_op jit(solution)/shard_map/all_to_all | solution.py:120
  51.6 2.1 fusion.14
  53.7 1.7 copy.59
  55.4 4.7 %all-to-all-start.1 = ((bf16[4,64,16,256]{3,2,0,1:T(8,128)(2,1)}), bf16[4,64,16,256]{3,2,0,1:T(8,128)(2,1)S(1)}, u32[]{:S(2)}, u32[]{:S(2)}) async-start(bf16[4,64,16,256]{3,2,0,1:T(8,128)(2,1)} %copy.59), calls=%async_computation.1 | async-start | bytes 4194304 | tf_op jit(solution)/shard_map/all_to_all | solution.py:130
  64.0 2.8 fusion.15
  66.8 44.7 %all-to-all-done.1 = bf16[4,64,16,256]{3,2,0,1:T(8,128)(2,1)S(1)} async-done(((bf16[4,64,16,256]{3,2,0,1:T(8,128)(2,1)}), bf16[4,64,16,256]{3,2,0,1:T(8,128)(2,1)S(1)}, u32[]{:S(2)}, u32[]{:S(2)}) %all-to-all-start.1) | async-done | bytes 2097184 | tf_op jit(solution)/shard_map/all_to_all | solution.py:130
  111.6 2.1 fusion.17
  113.9 2.6 fusion.40
  116.6 4.9 %all-to-all-start.3 = ((f32[4,64,512]{2,1,0:T(8,128)}), f32[4,64,512]{2,1,0:T(8,128)S(1)}, u32[]{:S(2)}, u32[]{:S(2)}) async-start(f32[4,64,512]{2,1,0:T(8,128)} %fusion.40), calls=%async_computation.3 | async-start | bytes 1048576 | tf_op jit(solution)/shard_map/all_to_all | solution.py:17
  121.5 6.6 %all-to-all-done.3 = f32[4,64,512]{2,1,0:T(8,128)S(1)} async-done(((f32[4,64,512]{2,1,0:T(8,128)}), f32[4,64,512]{2,1,0:T(8,128)S(1)}, u32[]{:S(2)}, u32[]{:S(2)}) %all-to-all-start.3) | async-done | bytes 524320 | tf_op jit(solution)/shard_map/all_to_all | solution.py:17
  128.2 11.8 %all_gather.6 = bf16[256,512]{1,0:T(8,128)(2,1)S(1)} all-gather(bf16[64,512]{1,0:T(8,128)(2,1)S(1)} %reduce_sum.101), channel_id=1, replica_groups=mesh['dp'=64,'mp'=4] {'mp'}, dimensions={0}, use_global_device_ids=true | all-gather | bytes 327680 | tf_op jit(solution)/shard_map/all_gather | solution.py:73
  139.9 1.5 fusion.28
  142.7 6.2 %all-to-all-start.4 = ((f32[4,64,512]{2,1,0:T(8,128)}), f32[4,64,512]{2,1,0:T(8,128)}, u32[]{:S(2)}, u32[]{:S(2)}) async-start(f32[4,64,512]{2,1,0:T(8,128)} %fusion.34), calls=%async_computation.4 | async-start | bytes 1048576 | tf_op jit(solution)/shard_map/all_to_all | solution.py:17
  148.9 1.6 copy.62
  150.5 5.1 %all-to-all-done.4 = f32[4,64,512]{2,1,0:T(8,128)} async-done(((f32[4,64,512]{2,1,0:T(8,128)}), f32[4,64,512]{2,1,0:T(8,128)}, u32[]{:S(2)}, u32[]{:S(2)}) %all-to-all-start.4) | async-done | bytes 524320 | tf_op jit(solution)/shard_map/all_to_all | solution.py:17
  155.6 7.0 %all-to-all-start.2 = ((bf16[4,64,16,256]{3,2,0,1:T(8,128)(2,1)}), bf16[4,64,16,256]{3,2,0,1:T(8,128)(2,1)S(1)}, u32[]{:S(2)}, u32[]{:S(2)}) async-start(bf16[4,64,16,256]{3,2,0,1:T(8,128)(2,1)} %copy.62), calls=%async_computation.2 | async-start | bytes 4194304 | tf_op jit(solution)/shard_map/all_to_all | solution.py:147
  162.7 1.7 reduce_sum.102
  164.4 11.8 %all_gather.7 = bf16[256,512]{1,0:T(8,128)(2,1)S(1)} all-gather(bf16[64,512]{1,0:T(8,128)(2,1)} %reduce_sum.102), channel_id=1, replica_groups=mesh['dp'=64,'mp'=4] {'mp'}, dimensions={0}, use_global_device_ids=true | all-gather | bytes 327680 | tf_op jit(solution)/shard_map/all_gather | solution.py:73
  176.3 2.9 fusion.25
  179.1 34.9 %all-to-all-done.2 = bf16[4,64,16,256]{3,2,0,1:T(8,128)(2,1)S(1)} async-done(((bf16[4,64,16,256]{3,2,0,1:T(8,128)(2,1)}), bf16[4,64,16,256]{3,2,0,1:T(8,128)(2,1)S(1)}, u32[]{:S(2)}, u32[]{:S(2)}) %all-to-all-start.2) | async-done | bytes 2097184 | tf_op jit(solution)/shard_map/all_to_all | solution.py:147
  214.0 9.2 %psum.7 = f32[256]{0:T(256)S(1)} all-reduce(f32[256]{0:T(256)S(1)} %get-tuple-element.13), channel_id=1, replica_groups=mesh['dp'=64,'mp'=4] {'mp'}, use_global_device_ids=true, to_apply=%region_8.0 | all-reduce | flops 256 | bytes 2048 | tf_op jit(solution)/shard_map/psum | solution.py:172
  223.9 1.7 fusion.31
  225.9 25.3 %all_to_all.36 = f32[4,256,512]{2,1,0:T(8,128)S(1)} all-to-all(f32[4,256,512]{2,1,0:T(8,128)S(1)} %broadcast_in_dim.16), channel_id=1, replica_groups=mesh['dp'=64,'mp'=4] {'mp'}, dimensions={0} | all-to-all | bytes 4194304 | tf_op jit(solution)/shard_map/all_to_all | solution.py:23
  252.1 2.1 fusion.58
  254.8 1.6 broadcast_in_dim.17
  256.4 5.9 %all-to-all-start.6 = ((f32[4,256,512]{2,1,0:T(8,128)}), f32[4,256,512]{2,1,0:T(8,128)}, u32[]{:S(2)}, u32[]{:S(2)}) async-start(f32[4,256,512]{2,1,0:T(8,128)} %broadcast_in_dim.17), calls=%async_computation.6 | async-start | bytes 4194304 | tf_op jit(solution)/shard_map/all_to_all | solution.py:23
  262.2 1.8 convolution_bitcast_fusion.2
  264.1 1.8 convolution_bitcast_fusion
  265.8 1.8 convolution_bitcast_fusion.3
  267.6 15.1 %all-to-all-done.6 = f32[4,256,512]{2,1,0:T(8,128)} async-done(((f32[4,256,512]{2,1,0:T(8,128)}), f32[4,256,512]{2,1,0:T(8,128)}, u32[]{:S(2)}, u32[]{:S(2)}) %all-to-all-start.6) | async-done | bytes 2097184 | tf_op jit(solution)/shard_map/all_to_all | solution.py:23
  282.8 1.8 reduce_sum.106
  286.2 5.2 %pad_maximum_fusion = f32[4,512,1024]{2,1,0:T(8,128)} fusion(f32[1,512,1024]{2,1,0:T(8,128)} %convolution_bitcast_fusion, f32[1,512,1024]{2,1,0:T(8,128)S(1)} %convolution_bitcast_fusion.1, f32[1,512,1024]{2,1,0:T(8,128)} %convolution_bitcast_fusion.2, f32[1,512,1024]{2,1,0:T(8,128)S(1)} %copy-done.4), kind=kLoop, calls=%fused_computation.2 | loop fusion | flops 6291456 | bytes 16777216 | tf_op jit(solution)/shard_map/concatenate | solution.py:41
  292.8 1.7 collective-permute-start.1
  294.4 2.2 collective-permute-done.1
  296.6 4.3 collective-permute-start.2
  300.9 2.9 copy.67
  303.9 1.8 copy.65
  305.8 2.4 collective-permute-start.3
  308.2 2.9 multiply_reduce_fusion
  312.5 3.3 collective-permute-done.4
  315.8 2.1 collective-permute-start.5
  317.9 1.9 divide_subtract_fusion
  319.8 3.0 copy.68
  324.1 3.0 fusion.20
  327.0 115.0 %reduce-scatter.2.cloned.1.call-done = f32[4,8,1024]{2,1,0:T(8,128)} async-done(((f32[4,512,1024]{2,1,0:T(8,128)}), f32[4,8,1024]{2,1,0:T(8,128)}) %reduce-scatter.2.cloned.1.call-update) | async-done | bytes 131088 | tf_op jit(solution)/shard_map/reduce_scatter | solution.py:42
  442.0 1.5 fusion.82
  (109 shorter events, 20.6 us)
Async XLA Ops:
  7.2 56.8 %copy-start = (bf16[4,512,256]{2,1,0:T(8,128)(2,1)S(1)}, bf16[4,512,256]{2,1,0:T(8,128)(2,1)}, u32[]{:S(2)}) copy-start(bf16[4,512,256]{2,1,0:T(8,128)(2,1)} %param.15) | copy-start | bytes 3145732
  7.2 4.5 copy-start.21
  7.2 4.6 %copy-start.22 = (s32[2]{0:T(128)S(1)}, s32[2]{0:T(128)}, u32[]{:S(2)}) copy-start(s32[2]{0:T(128)} %constant.30) | copy-start | bytes 28
  7.2 3.8 copy-start.17
  7.2 4.4 copy-start.18
  9.8 41.9 %copy-start.10 = (f32[4,512,256]{2,1,0:T(8,128)S(1)}, f32[4,512,256]{2,1,0:T(8,128)}, u32[]{:S(2)}) copy-start(f32[4,512,256]{2,1,0:T(8,128)} %param.13) | copy-start | bytes 6291460
  55.4 56.1 %all-to-all-start.1 = ((bf16[4,64,16,256]{3,2,0,1:T(8,128)(2,1)}), bf16[4,64,16,256]{3,2,0,1:T(8,128)(2,1)S(1)}, u32[]{:S(2)}, u32[]{:S(2)}) async-start(bf16[4,64,16,256]{3,2,0,1:T(8,128)(2,1)} %copy.59), calls=%async_computation.1 | async-start | bytes 4194304 | tf_op jit(solution)/shard_map/all_to_all | solution.py:130
  113.7 2.9 copy-start.12
  113.7 7.8 %copy-start.19 = (f32[2,1024]{1,0:T(2,128)S(1)}, f32[2,1024]{1,0:T(2,128)}, u32[]{:S(2)}) copy-start(f32[2,1024]{1,0:T(2,128)} %param.24) | copy-start | bytes 24580
  113.9 26.0 %copy-start.5 = (bf16[2,512,1024]{2,1,0:T(8,128)(2,1)S(1)}, bf16[2,512,1024]{2,1,0:T(8,128)(2,1)}, u32[]{:S(2)}) copy-start(bf16[2,512,1024]{2,1,0:T(8,128)(2,1)} %param.22) | copy-start | bytes 6291460
  116.6 11.5 %all-to-all-start.3 = ((f32[4,64,512]{2,1,0:T(8,128)}), f32[4,64,512]{2,1,0:T(8,128)S(1)}, u32[]{:S(2)}, u32[]{:S(2)}) async-start(f32[4,64,512]{2,1,0:T(8,128)} %fusion.40), calls=%async_computation.3 | async-start | bytes 1048576 | tf_op jit(solution)/shard_map/all_to_all | solution.py:17
  128.1 13.3 %copy-start.15 = (bf16[2,512,1024]{2,1,0:T(8,128)(2,1)S(1)}, bf16[2,512,1024]{2,1,0:T(8,128)(2,1)}, u32[]{:S(2)}) copy-start(bf16[2,512,1024]{2,1,0:T(8,128)(2,1)} %param.23) | copy-start | bytes 6291460
  139.9 1.5 copy-start.8
  141.5 7.4 %copy-start.11 = (bf16[4,1024,256]{2,1,0:T(8,128)(2,1)S(1)}, bf16[4,1024,256]{2,1,0:T(8,128)(2,1)}, u32[]{:S(2)}) copy-start(bf16[4,1024,256]{2,1,0:T(8,128)(2,1)} %fusion.15) | copy-start | bytes 6291460
  142.7 12.9 %all-to-all-start.4 = ((f32[4,64,512]{2,1,0:T(8,128)}), f32[4,64,512]{2,1,0:T(8,128)}, u32[]{:S(2)}, u32[]{:S(2)}) async-start(f32[4,64,512]{2,1,0:T(8,128)} %fusion.34), calls=%async_computation.4 | async-start | bytes 1048576 | tf_op jit(solution)/shard_map/all_to_all | solution.py:17
  150.5 25.7 %copy-start.16 = (f32[1024]{0:T(1024)S(1)}, f32[1024]{0:T(1024)}, u32[]{:S(2)}) copy-start(f32[1024]{0:T(1024)} %param.25) | copy-start | bytes 12292
  155.6 58.4 %all-to-all-start.2 = ((bf16[4,64,16,256]{3,2,0,1:T(8,128)(2,1)}), bf16[4,64,16,256]{3,2,0,1:T(8,128)(2,1)S(1)}, u32[]{:S(2)}, u32[]{:S(2)}) async-start(bf16[4,64,16,256]{3,2,0,1:T(8,128)(2,1)} %copy.62), calls=%async_computation.2 | async-start | bytes 4194304 | tf_op jit(solution)/shard_map/all_to_all | solution.py:147
  214.0 11.6 %copy-start.2 = (bf16[4,64,16,256]{3,2,0,1:T(8,128)(2,1)}, bf16[4,64,16,256]{3,2,0,1:T(8,128)(2,1)S(1)}, u32[]{:S(2)}) copy-start(bf16[4,64,16,256]{3,2,0,1:T(8,128)(2,1)S(1)} %all-to-all-done.2) | copy-start | bytes 6291460
  252.1 2.2 copy-start.6
  256.4 26.4 %all-to-all-start.6 = ((f32[4,256,512]{2,1,0:T(8,128)}), f32[4,256,512]{2,1,0:T(8,128)}, u32[]{:S(2)}, u32[]{:S(2)}) async-start(f32[4,256,512]{2,1,0:T(8,128)} %broadcast_in_dim.17), calls=%async_computation.6 | async-start | bytes 4194304 | tf_op jit(solution)/shard_map/all_to_all | solution.py:23
  262.2 1.8 copy-start.14
  262.2 179.8 %reduce-scatter.2.cloned.1.call-start = ((), (), s32[]{:S(2)}) async-start(), calls=%async_computation.8 | async-start | bytes 8519680 | tf_op jit(solution)/shard_map/reduce_scatter | solution.py:42
  264.1 1.8 copy-start.9
  267.6 17.0 %copy-start.13 = (bf16[4,256,256]{1,2,0:T(8,128)(2,1)S(1)}, bf16[4,256,256]{1,2,0:T(8,128)(2,1)}, u32[]{:S(2)}) copy-start(bf16[4,256,256]{1,2,0:T(8,128)(2,1)} %copy-done.12) | copy-start | bytes 1572868
  284.6 1.6 copy-start.4
  291.5 1.3 collective-permute-start
  292.8 3.8 collective-permute-start.1
  296.6 9.1 %collective-permute-start.2 = (f32[3,1024]{1,0:T(4,128)S(1)}, f32[3,1024]{1,0:T(4,128)S(1)}, u32[]{:S(2)}, u32[]{:S(2)}) collective-permute-start(f32[3,1024]{1,0:T(4,128)S(1)} %fusion.100), channel_id=1, source_target_pairs={{0,16},{4,20},{8,24},{12,28},{16,0},{20,4},{24,8},{28,12},{32,48},... | collective-permute-start | bytes 36872 | tf_op jit(solution)/shard_map/ppermute | solution.py:34
  305.8 5.3 %collective-permute-start.3 = (f32[3,1024]{1,0:T(4,128)S(1)}, f32[3,1024]{1,0:T(4,128)S(1)}, u32[]{:S(2)}, u32[]{:S(2)}) collective-permute-start(f32[3,1024]{1,0:T(4,128)S(1)} %add.110), channel_id=1, source_target_pairs={{0,32},{4,36},{8,40},{12,44},{16,48},{20,52},{24,56},{28,60},{32,0... | collective-permute-start | bytes 36872 | tf_op jit(solution)/shard_map/ppermute | solution.py:34
  308.2 3.7 copy-start.20
  308.2 9.7 %copy-start.3 = (f32[4,512,256]{1,2,0:T(8,128)S(1)}, f32[4,512,256]{1,2,0:T(8,128)}, u32[]{:S(2)}) copy-start(f32[4,512,256]{1,2,0:T(8,128)} %copy.67) | copy-start | bytes 6291460
  311.1 4.7 %collective-permute-start.4 = (f32[3,1024]{1,0:T(4,128)S(1)}, f32[3,1024]{1,0:T(4,128)S(1)}, u32[]{:S(2)}, u32[]{:S(2)}) collective-permute-start(f32[3,1024]{1,0:T(4,128)S(1)} %add.111), channel_id=1, source_target_pairs={{0,64},{4,68},{8,72},{12,76},{16,80},{20,84},{24,88},{28,92},{32,9... | collective-permute-start | bytes 36872 | tf_op jit(solution)/shard_map/ppermute | solution.py:34
  315.8 7.6 %collective-permute-start.5 = (f32[3,1024]{1,0:T(4,128)S(1)}, f32[3,1024]{1,0:T(4,128)S(1)}, u32[]{:S(2)}, u32[]{:S(2)}) collective-permute-start(f32[3,1024]{1,0:T(4,128)S(1)} %add.112), channel_id=1, source_target_pairs={{0,128},{4,132},{8,136},{12,140},{16,144},{20,148},{24,152},{28,15... | collective-permute-start | bytes 36872 | tf_op jit(solution)/shard_map/ppermute | solution.py:34
  319.8 4.3 copy-start.7
  324.1 119.5 %copy-start.1 = (bf16[4,512,256]{2,1,0:T(8,128)(2,1)S(1)}, bf16[4,512,256]{2,1,0:T(8,128)(2,1)}, u32[]{:S(2)}) copy-start(bf16[4,512,256]{2,1,0:T(8,128)(2,1)} %param.15) | copy-start | bytes 3145732
Sparse Core Ops, SparseCore 0:
  291.6 150.4 reduce-scatter.1

commit v5 on v0

--- a/solution.py
+++ b/solution.py
@@ -25,6 +25,15 @@
 
 def over_copies(array, axis):
     return copy_for_each(array, axis).sum(axis=0)
+
+
+def butterfly_sum(array, axis):
+    peers = lax.axis_size(axis)
+    step = 1
+    while step < peers:
+        array = array + lax.ppermute(array, axis, [(i, i ^ step) for i in range(peers)])
+        step *= 2
+    return array
 
 
 def side_by_side(arrays, axis, dim, along):
@@ -60,8 +69,7 @@
 
 
 def cross_down(state, v_layer):
-    share = sum_at_owner(contract_last(state, v_layer), "mp", 0)
-    return lax.all_gather(share.astype(jnp.bfloat16), "mp", axis=0, tiled=True)
+    return over_copies(contract_last(state, v_layer), "mp").astype(jnp.bfloat16)
 
 
 def local(
@@ -195,7 +203,7 @@
     grad_u = jnp.stack(grads_u)
     grad_v = jnp.stack(grads_v)
     grad_u, grad_v = side_by_side((grad_u, grad_v), "dp", 1, 0)
-    grad_small = over_copies(jnp.stack(bias_grads + [head_grad]), "dp")
+    grad_small = butterfly_sum(jnp.stack(bias_grads + [head_grad]), "dp")
     grad_pooled = (upstream + to_start).astype(jnp.bfloat16)
     return (new_table, new_accum, grad_u, grad_v, grad_small, grad_pooled)
 

time: 406 us -> 417 us (1.027)
  waiting for transfers between devices: 186 us -> 207 us
  blocking collectives: 75.8 us -> 56 us
  starting transfers between devices: 40.8 us -> 49.8 us
    all_to_all x2 -> x3, waiting for transfers between devices: 33.8 us -> 59.3 us  [copy_for_each(): return lax.all_to_all(copies, axis, split_axis=0, concat_axis=0, tiled=True)]
    all_gather x2 -> x0, blocking collectives: 23.4 us -> none  [cross_down(): return lax.all_gather(share.astype(jnp.bfloat16), 'mp', axis=0, tiled=True)]
    all_to_all x2 -> x0, waiting for transfers between devices: 13.7 us -> none  [sum_at_owner(): lax.all_to_all(parts, axis, split_axis=0, concat_axis=0, tiled=True)]
    all_to_all x1, waiting for transfers between devices: 51.6 us -> 39.8 us  [local(): lax.all_to_all(send_grads.reshape(local_feats, peers, grad_cap, width), '...]
    ppermute x0 -> x6, waiting for transfers between devices: none -> 10.8 us  [butterfly_sum(): lax.ppermute(array, axis, [(i, i ^ step) for i in range(peers)])]
    all_to_all x2 -> x0, starting transfers between devices: 10.4 us -> none  [sum_at_owner(): lax.all_to_all(parts, axis, split_axis=0, concat_axis=0, tiled=True)]
    reduce_scatter x1, waiting for transfers between devices: 30.5 us -> 40.5 us  [side_by_side(): filled = lax.psum_scatter(both, axis, scatter_dimension=dim, tiled=True)]
    all_to_all x1, starting transfers between devices: 7.47 us -> 15.5 us  [local(): lax.all_to_all(send_rows.reshape(local_feats, peers, grad_cap), 'dp', spl...]
  transfers between devices with their start and end apart: 8 -> 13, of which waited for: 8 -> 11; matrix products, arithmetic and copies ran while one was open for 10% -> 9% of each run, Pallas kernels for 0% -> 0%
where the time goes in v5:
time: 417 us; the launch traced here: 416 us
  waiting for transfers between devices  207 us (50%)
  blocking collectives  56 us (13%)
  starting transfers between devices  49.8 us (12%)
  local copies, waits for them, and re-layouts  40.1 us (10%)
  matrix products  28.8 us (7%)
  other arithmetic  19.2 us (5%)
  between operations  14.6 us (4%)
    all_to_all x3, waiting for transfers between devices, copy_for_each(): return lax.all_to_all(copies, axis, split_axis=0, concat_axis=0, tiled=True)  59.3 us
    all_to_all x1, waiting for transfers between devices, local(): lax.all_to_all(served.reshape(local_feats, peers, look_cap, width), 'dp',...  48.8 us
    reduce_scatter x1, waiting for transfers between devices, side_by_side(): filled = lax.psum_scatter(both, axis, scatter_dimension=dim, tiled=True)  40.5 us
    all_to_all x1, waiting for transfers between devices, local(): lax.all_to_all(send_grads.reshape(local_feats, peers, grad_cap, width), '...  39.8 us
    unnamed x60, local copies, waits for them, and re-layouts  25.5 us
    all_to_all x1, blocking collectives, copy_for_each(): return lax.all_to_all(copies, axis, split_axis=0, concat_axis=0, tiled=True)  24.1 us
    all_to_all x1, blocking collectives, local(): lax.all_to_all(wanted.reshape(local_feats, peers, look_cap), 'dp', split_...  22.8 us
    all_to_all x3, starting transfers between devices, copy_for_each(): return lax.all_to_all(copies, axis, split_axis=0, concat_axis=0, tiled=True)  16.8 us
  transfers between devices with their start and end apart: 13, of which 11 were waited for; matrix products, arithmetic and copies ran while one was open for 9% of the time, Pallas kernels for 0%

profile of v5, /device:TPU:8, one launch (start us, length us, event | category | flops | bytes accessed | tf_op | source)
XLA Modules:
  0.0 415.7 jit_solution(2378748861931140014)
XLA Ops:
  10.6 8.1 %scatter_custom_fusion.1 = s32[4096]{0:T(1024)S(1)} fusion(s32[2048]{0:T(1024)S(1)} %bitcast.118, s32[2048]{0:T(1024)S(1)} %bitcast.120, s32[]{:T(128)} %constant.5.clone.1), kind=kCustom, calls=%fused_computation.113 | custom fusion | bytes 16388
  18.9 22.8 %all_to_all.40 = s32[4,64,16]{2,0,1:T(4,128)S(1)} all-to-all(s32[4,64,16]{2,0,1:T(4,128)S(1)} %copy.60), channel_id=1, replica_groups=mesh['dp'=64,'mp'=4] {'dp'}, dimensions={1} | all-to-all | bytes 32768 | tf_op jit(solution)/shard_map/all_to_all | solution.py:138
  41.8 2.1 fusion.14
  43.9 1.6 copy.62
  45.5 4.7 %all-to-all-start.3 = ((bf16[4,64,16,256]{3,2,0,1:T(8,128)(2,1)}), bf16[4,64,16,256]{3,2,0,1:T(8,128)(2,1)S(1)}, u32[]{:S(2)}, u32[]{:S(2)}) async-start(bf16[4,64,16,256]{3,2,0,1:T(8,128)(2,1)} %copy.62), calls=%async_computation.3 | async-start | bytes 4194304 | tf_op jit(solution)/shard_map/all_to_all | solution.py:148
  52.7 48.8 %all-to-all-done.3 = bf16[4,64,16,256]{3,2,0,1:T(8,128)(2,1)S(1)} async-done(((bf16[4,64,16,256]{3,2,0,1:T(8,128)(2,1)}), bf16[4,64,16,256]{3,2,0,1:T(8,128)(2,1)S(1)}, u32[]{:S(2)}, u32[]{:S(2)}) %all-to-all-start.3) | async-done | bytes 2097184 | tf_op jit(solution)/shard_map/all_to_all | solution.py:148
  101.8 2.1 fusion.17
  104.3 1.6 broadcast_in_dim.20
  105.9 5.0 %all-to-all-start.4 = ((f32[4,256,512]{2,1,0:T(8,128)}), f32[4,256,512]{2,1,0:T(8,128)}, u32[]{:S(2)}, u32[]{:S(2)}) async-start(f32[4,256,512]{2,1,0:T(8,128)} %broadcast_in_dim.20), calls=%async_computation.4 | async-start | bytes 4194304 | tf_op jit(solution)/shard_map/all_to_all | solution.py:23
  111.2 23.5 %all-to-all-done.4 = f32[4,256,512]{2,1,0:T(8,128)} async-done(((f32[4,256,512]{2,1,0:T(8,128)}), f32[4,256,512]{2,1,0:T(8,128)}, u32[]{:S(2)}, u32[]{:S(2)}) %all-to-all-start.4) | async-done | bytes 2097184 | tf_op jit(solution)/shard_map/all_to_all | solution.py:23
  134.7 1.8 reduce_sum.102
  136.6 2.9 fusion.26
  139.9 1.6 broadcast_in_dim.21
  141.5 5.9 %all-to-all-start.5 = ((f32[4,256,512]{2,1,0:T(8,128)}), f32[4,256,512]{2,1,0:T(8,128)}, u32[]{:S(2)}, u32[]{:S(2)}) async-start(f32[4,256,512]{2,1,0:T(8,128)} %broadcast_in_dim.21), calls=%async_computation.5 | async-start | bytes 4194304 | tf_op jit(solution)/shard_map/all_to_all | solution.py:23
  147.4 22.7 %all-to-all-done.5 = f32[4,256,512]{2,1,0:T(8,128)} async-done(((f32[4,256,512]{2,1,0:T(8,128)}), f32[4,256,512]{2,1,0:T(8,128)}, u32[]{:S(2)}, u32[]{:S(2)}) %all-to-all-start.5) | async-done | bytes 2097184 | tf_op jit(solution)/shard_map/all_to_all | solution.py:23
  170.1 1.8 reduce_sum.103
  172.0 2.9 fusion.23
  174.9 9.2 %psum.7 = f32[256]{0:T(256)S(1)} all-reduce(f32[256]{0:T(256)S(1)} %get-tuple-element.34), channel_id=1, replica_groups=mesh['dp'=64,'mp'=4] {'mp'}, use_global_device_ids=true, to_apply=%region_8.0 | all-reduce | flops 256 | bytes 2048 | tf_op jit(solution)/shard_map/psum | solution.py:180
  184.5 1.7 fusion.30
  186.5 24.1 %all_to_all.41 = f32[4,256,512]{2,1,0:T(8,128)} all-to-all(f32[4,256,512]{2,1,0:T(8,128)S(1)} %broadcast_in_dim.22), channel_id=1, replica_groups=mesh['dp'=64,'mp'=4] {'mp'}, dimensions={0} | all-to-all | bytes 4194304 | tf_op jit(solution)/shard_map/all_to_all | solution.py:23
  210.5 2.6 reduce_sum.105
  213.1 1.9 fusion.59
  215.6 1.6 broadcast_in_dim.23
  217.1 5.9 %all-to-all-start.7 = ((f32[4,256,512]{2,1,0:T(8,128)}), f32[4,256,512]{2,1,0:T(8,128)}, u32[]{:S(2)}, u32[]{:S(2)}) async-start(f32[4,256,512]{2,1,0:T(8,128)} %broadcast_in_dim.23), calls=%async_computation.7 | async-start | bytes 4194304 | tf_op jit(solution)/shard_map/all_to_all | solution.py:23
  223.0 1.9 convolution_bitcast_fusion.2
  224.9 1.8 convolution_bitcast_fusion
  226.7 1.8 convolution_bitcast_fusion.3
  228.5 13.1 %all-to-all-done.7 = f32[4,256,512]{2,1,0:T(8,128)} async-done(((f32[4,256,512]{2,1,0:T(8,128)}), f32[4,256,512]{2,1,0:T(8,128)}, u32[]{:S(2)}, u32[]{:S(2)}) %all-to-all-start.7) | async-done | bytes 2097184 | tf_op jit(solution)/shard_map/all_to_all | solution.py:23
  241.6 1.8 reduce_sum.106
  245.0 5.2 %pad_maximum_fusion = f32[4,512,1024]{2,1,0:T(8,128)} fusion(f32[1,512,1024]{2,1,0:T(8,128)} %convolution_bitcast_fusion, f32[1,512,1024]{2,1,0:T(8,128)S(1)} %convolution_bitcast_fusion.1, f32[1,512,1024]{2,1,0:T(8,128)S(1)} %copy-done.2, f32[1,512,1024]{2,1,0:T(8,128)} %convolution_bitcast_fusion.3), kind=kLoop, calls=%fused_computation.2 | loop fusion | flops 6291456 | bytes 16777216 | tf_op jit(solution)/shard_map/concatenate | solution.py:41
  250.9 8.1 %scatter_custom_fusion = s32[4096]{0:T(1024)S(1)} fusion(s32[2048]{0:T(1024)S(1)} %bitcast.119, s32[2048]{0:T(1024)S(1)} %bitcast.121, s32[]{:T(128)} %constant.11.clone.1), kind=kCustom, calls=%fused_computation.115 | custom fusion | bytes 16388
  259.8 15.5 %all-to-all-start = ((s32[4,64,16]{2,0,1:T(4,128)}), s32[4,64,16]{2,0,1:T(4,128)S(1)}, u32[]{:S(2)}, u32[]{:S(2)}) async-start(s32[4,64,16]{2,0,1:T(4,128)} %copy.50), calls=%async_computation | async-start | bytes 262144 | tf_op jit(solution)/shard_map/all_to_all | solution.py:113
  276.8 1.6 copy.52
  278.4 7.9 %all-to-all-done = s32[4,64,16]{2,0,1:T(4,128)S(1)} async-done(((s32[4,64,16]{2,0,1:T(4,128)}), s32[4,64,16]{2,0,1:T(4,128)S(1)}, u32[]{:S(2)}, u32[]{:S(2)}) %all-to-all-start) | async-done | bytes 16416 | tf_op jit(solution)/shard_map/all_to_all | solution.py:113
  286.3 5.6 %all-to-all-start.1 = ((bf16[4,64,16,256]{3,2,0,1:T(8,128)(2,1)}), bf16[4,64,16,256]{3,2,0,1:T(8,128)(2,1)}, u32[]{:S(2)}, u32[]{:S(2)}) async-start(bf16[4,64,16,256]{3,2,0,1:T(8,128)(2,1)} %copy.52), calls=%async_computation.1 | async-start | bytes 4194304 | tf_op jit(solution)/shard_map/all_to_all | solution.py:106
  294.9 4.1 collective-permute-done.1
  299.0 2.0 collective-permute-start.2
  301.0 2.9 copy.55
  304.0 39.8 %all-to-all-done.1 = bf16[4,64,16,256]{3,2,0,1:T(8,128)(2,1)} async-done(((bf16[4,64,16,256]{3,2,0,1:T(8,128)(2,1)}), bf16[4,64,16,256]{3,2,0,1:T(8,128)(2,1)}, u32[]{:S(2)}, u32[]{:S(2)}) %all-to-all-start.1) | async-done | bytes 2097184 | tf_op jit(solution)/shard_map/all_to_all | solution.py:106
  343.8 1.8 copy.53
  345.6 1.9 collective-permute-start.3
  347.6 2.9 multiply_reduce_fusion
  351.2 4.2 %collective-permute-done.4 = f32[3,1024]{1,0:T(4,128)S(1)} collective-permute-done((f32[3,1024]{1,0:T(4,128)S(1)}, f32[3,1024]{1,0:T(4,128)S(1)}, u32[]{:S(2)}, u32[]{:S(2)}) %collective-permute-start.4) | collective-permute-done | bytes 12320 | tf_op jit(solution)/shard_map/ppermute | solution.py:34
  355.4 1.7 collective-permute-start.5
  357.1 1.9 divide_subtract_fusion
  359.0 3.0 copy.66
  363.9 2.9 fusion.20
  366.8 40.5 %reduce-scatter.2.cloned.1.call-done = f32[4,8,1024]{2,1,0:T(8,128)} async-done(((f32[4,512,1024]{2,1,0:T(8,128)}), f32[4,8,1024]{2,1,0:T(8,128)}) %reduce-scatter.2.cloned.1.call-update) | async-done | bytes 131088 | tf_op jit(solution)/shard_map/reduce_scatter | solution.py:42
  (112 shorter events, 20.6 us)
Async XLA Ops:
  7.2 268.1 %copy-start = (bf16[4,512,256]{2,1,0:T(8,128)(2,1)S(1)}, bf16[4,512,256]{2,1,0:T(8,128)(2,1)}, u32[]{:S(2)}) copy-start(bf16[4,512,256]{2,1,0:T(8,128)(2,1)} %param.15) | copy-start | bytes 3145732
  7.2 3.1 copy-start.23
  7.2 3.2 copy-start.22
  7.2 3.0 copy-start.15
  7.2 3.4 copy-start.16
  7.2 34.6 %copy-start.10 = (f32[4,512,256]{2,1,0:T(8,128)S(1)}, f32[4,512,256]{2,1,0:T(8,128)}, u32[]{:S(2)}) copy-start(f32[4,512,256]{2,1,0:T(8,128)} %param.13) | copy-start | bytes 6291460
  45.5 56.1 %all-to-all-start.3 = ((bf16[4,64,16,256]{3,2,0,1:T(8,128)(2,1)}), bf16[4,64,16,256]{3,2,0,1:T(8,128)(2,1)S(1)}, u32[]{:S(2)}, u32[]{:S(2)}) async-start(bf16[4,64,16,256]{3,2,0,1:T(8,128)(2,1)} %copy.62), calls=%async_computation.3 | async-start | bytes 4194304 | tf_op jit(solution)/shard_map/all_to_all | solution.py:148
  50.2 2.5 copy-start.20
  101.7 2.1 copy-start.12
  105.9 5.1 %copy-start.17 = (f32[2,1024]{1,0:T(2,128)S(1)}, f32[2,1024]{1,0:T(2,128)}, u32[]{:S(2)}) copy-start(f32[2,1024]{1,0:T(2,128)} %param.24) | copy-start | bytes 24580
  105.9 28.8 %all-to-all-start.4 = ((f32[4,256,512]{2,1,0:T(8,128)}), f32[4,256,512]{2,1,0:T(8,128)}, u32[]{:S(2)}, u32[]{:S(2)}) async-start(f32[4,256,512]{2,1,0:T(8,128)} %broadcast_in_dim.20), calls=%async_computation.4 | async-start | bytes 4194304 | tf_op jit(solution)/shard_map/all_to_all | solution.py:23
  136.5 3.4 copy-start.7
  136.5 2.9 copy-start.13
  139.4 32.6 %copy-start.4 = (bf16[256,1024]{1,0:T(8,128)(2,1)}, bf16[256,1024]{1,0:T(8,128)(2,1)S(1)}, u32[]{:S(2)}) copy-start(bf16[256,1024]{1,0:T(8,128)(2,1)S(1)} %get-tuple-element.54) | copy-start | bytes 1572868
  141.5 5.9 %copy-start.14 = (f32[1024]{0:T(1024)S(1)}, f32[1024]{0:T(1024)}, u32[]{:S(2)}) copy-start(f32[1024]{0:T(1024)} %param.25) | copy-start | bytes 12292
  141.5 28.6 %all-to-all-start.5 = ((f32[4,256,512]{2,1,0:T(8,128)}), f32[4,256,512]{2,1,0:T(8,128)}, u32[]{:S(2)}, u32[]{:S(2)}) async-start(f32[4,256,512]{2,1,0:T(8,128)} %broadcast_in_dim.21), calls=%async_computation.5 | async-start | bytes 4194304 | tf_op jit(solution)/shard_map/all_to_all | solution.py:23
  172.0 12.1 %copy-start.21 = (s32[256]{0:T(256)S(1)}, s32[256]{0:T(256)}, u32[]{:S(2)}) copy-start(s32[256]{0:T(256)} %param.21) | copy-start | bytes 3076
  213.1 2.0 copy-start.3
  217.1 24.4 %all-to-all-start.7 = ((f32[4,256,512]{2,1,0:T(8,128)}), f32[4,256,512]{2,1,0:T(8,128)}, u32[]{:S(2)}, u32[]{:S(2)}) async-start(f32[4,256,512]{2,1,0:T(8,128)} %broadcast_in_dim.23), calls=%async_computation.7 | async-start | bytes 4194304 | tf_op jit(solution)/shard_map/all_to_all | solution.py:23
  223.0 184.3 %reduce-scatter.2.cloned.1.call-start = ((), (), s32[]{:S(2)}) async-start(), calls=%async_computation.9 | async-start | bytes 8519680 | tf_op jit(solution)/shard_map/reduce_scatter | solution.py:42
  223.0 1.9 copy-start.5
  223.0 1.9 copy-start.11
  224.9 1.8 copy-start.8
  243.4 1.6 copy-start.2
  250.2 0.7 copy-start.18
  259.8 26.5 %all-to-all-start = ((s32[4,64,16]{2,0,1:T(4,128)}), s32[4,64,16]{2,0,1:T(4,128)S(1)}, u32[]{:S(2)}, u32[]{:S(2)}) async-start(s32[4,64,16]{2,0,1:T(4,128)} %copy.50), calls=%async_computation | async-start | bytes 262144 | tf_op jit(solution)/shard_map/all_to_all | solution.py:113
  278.4 13.5 %copy-start.9 = (bf16[256,1024]{1,0:T(8,128)(2,1)S(1)}, bf16[256,1024]{1,0:T(8,128)(2,1)}, u32[]{:S(2)}) copy-start(bf16[256,1024]{1,0:T(8,128)(2,1)} %get-tuple-element.35) | copy-start | bytes 1572868
  286.3 57.4 %all-to-all-start.1 = ((bf16[4,64,16,256]{3,2,0,1:T(8,128)(2,1)}), bf16[4,64,16,256]{3,2,0,1:T(8,128)(2,1)}, u32[]{:S(2)}, u32[]{:S(2)}) async-start(bf16[4,64,16,256]{3,2,0,1:T(8,128)(2,1)} %copy.52), calls=%async_computation.1 | async-start | bytes 4194304 | tf_op jit(solution)/shard_map/all_to_all | solution.py:106
  292.1 1.3 collective-permute-start
  293.4 5.6 %collective-permute-start.1 = (f32[3,1024]{1,0:T(4,128)S(1)}, f32[3,1024]{1,0:T(4,128)S(1)}, u32[]{:S(2)}, u32[]{:S(2)}) collective-permute-start(f32[3,1024]{1,0:T(4,128)S(1)} %fusion.82), channel_id=1, source_target_pairs={{0,8},{4,12},{8,0},{12,4},{16,24},{20,28},{24,16},{28,20},{32,40},... | collective-permute-start | bytes 36872 | tf_op jit(solution)/shard_map/ppermute | solution.py:34
  299.0 46.6 %collective-permute-start.2 = (f32[3,1024]{1,0:T(4,128)S(1)}, f32[3,1024]{1,0:T(4,128)S(1)}, u32[]{:S(2)}, u32[]{:S(2)}) collective-permute-start(f32[3,1024]{1,0:T(4,128)S(1)} %fusion.106), channel_id=1, source_target_pairs={{0,16},{4,20},{8,24},{12,28},{16,0},{20,4},{24,8},{28,12},{32,48},... | collective-permute-start | bytes 36872 | tf_op jit(solution)/shard_map/ppermute | solution.py:34
  345.6 4.8 %collective-permute-start.3 = (f32[3,1024]{1,0:T(4,128)S(1)}, f32[3,1024]{1,0:T(4,128)S(1)}, u32[]{:S(2)}, u32[]{:S(2)}) collective-permute-start(f32[3,1024]{1,0:T(4,128)S(1)} %add.110), channel_id=1, source_target_pairs={{0,32},{4,36},{8,40},{12,44},{16,48},{20,52},{24,56},{28,60},{32,0... | collective-permute-start | bytes 36872 | tf_op jit(solution)/shard_map/ppermute | solution.py:34
  347.6 3.0 copy-start.19
  347.6 9.5 %copy-start.1 = (f32[4,512,256]{1,2,0:T(8,128)S(1)}, f32[4,512,256]{1,2,0:T(8,128)}, u32[]{:S(2)}) copy-start(f32[4,512,256]{1,2,0:T(8,128)} %copy.55) | copy-start | bytes 6291460
  350.5 4.9 %collective-permute-start.4 = (f32[3,1024]{1,0:T(4,128)S(1)}, f32[3,1024]{1,0:T(4,128)S(1)}, u32[]{:S(2)}, u32[]{:S(2)}) collective-permute-start(f32[3,1024]{1,0:T(4,128)S(1)} %add.111), channel_id=1, source_target_pairs={{0,64},{4,68},{8,72},{12,76},{16,80},{20,84},{24,88},{28,92},{32,9... | collective-permute-start | bytes 36872 | tf_op jit(solution)/shard_map/ppermute | solution.py:34
  355.4 7.9 %collective-permute-start.5 = (f32[3,1024]{1,0:T(4,128)S(1)}, f32[3,1024]{1,0:T(4,128)S(1)}, u32[]{:S(2)}, u32[]{:S(2)}) collective-permute-start(f32[3,1024]{1,0:T(4,128)S(1)} %add.112), channel_id=1, source_target_pairs={{0,128},{4,132},{8,136},{12,140},{16,144},{20,148},{24,152},{28,15... | collective-permute-start | bytes 36872 | tf_op jit(solution)/shard_map/ppermute | solution.py:34
  359.0 4.9 %copy-start.6 = (f32[256,1024]{1,0:T(8,128)S(1)}, f32[256,1024]{1,0:T(8,128)}, u32[]{:S(2)}) copy-start(f32[256,1024]{1,0:T(8,128)} %get-tuple-element.56) | copy-start | bytes 3145732
Sparse Core Ops, SparseCore 0:
  250.4 156.9 reduce-scatter.1

commit v6 on v5

--- a/solution.py
+++ b/solution.py
@@ -69,7 +69,8 @@
 
 
 def cross_down(state, v_layer):
-    return over_copies(contract_last(state, v_layer), "mp").astype(jnp.bfloat16)
+    share = sum_at_owner(contract_last(state, v_layer), "mp", 0)
+    return lax.all_gather(share.astype(jnp.bfloat16), "mp", axis=0, tiled=True)
 
 
 def local(
@@ -195,14 +196,22 @@
         back_sum = over_copies(
             contract_last(direct_bias_term, up_factor_weight[layer]), "mp"
         ).astype(jnp.bfloat16)
+        if layer == n_layers - 1:
+            halves = jnp.swapaxes(grad_u_layer.reshape(grad_u_layer.shape[0], 2, -1), 0, 1)
+            early_u = lax.psum_scatter(halves, "dp", scatter_dimension=1, tiled=True)
+        else:
+            early_u, back_sum = lax.optimization_barrier((early_u, back_sum))
         down_factor_gradient = contract_first(back_sum, states[layer])
         to_start = to_start + upstream * crosses[layer]
         upstream = upstream + jnp.dot(back_sum, v_weight[layer], preferred_element_type=jnp.float32)
         grads_u[layer] = grad_u_layer
         grads_v[layer] = down_factor_gradient
-    grad_u = jnp.stack(grads_u)
-    grad_v = jnp.stack(grads_v)
-    grad_u, grad_v = side_by_side((grad_u, grad_v), "dp", 1, 0)
+    rest = lax.psum_scatter(
+        jnp.stack((grads_u[0], grads_v[0], grads_v[1])), "dp", scatter_dimension=1, tiled=True
+    )
+    early_u = jnp.swapaxes(early_u, 0, 1).reshape(1, early_u.shape[1], -1)
+    grad_u = jnp.concatenate((rest[0:1], early_u), axis=0)
+    grad_v = rest[1:3]
     grad_small = butterfly_sum(jnp.stack(bias_grads + [head_grad]), "dp")
     grad_pooled = (upstream + to_start).astype(jnp.bfloat16)
     return (new_table, new_accum, grad_u, grad_v, grad_small, grad_pooled)

time: 417 us -> 506 us (1.21)
  waiting for transfers between devices: 207 us -> 281 us
  blocking collectives: 56 us -> 75.8 us
  starting transfers between devices: 49.8 us -> 41.4 us
  matrix products: 28.8 us -> 34.7 us
    reduce_scatter x1 -> x2, waiting for transfers between devices: 40.5 us -> 149 us  [the longest x1 111 us: local(): early_u = lax.psum_scatter(halves, 'dp', scatter_dimension=1, tiled=True)]
    all_to_all x3 -> x1, waiting for transfers between devices: 59.3 us -> 10.4 us  [copy_for_each(): return lax.all_to_all(copies, axis, split_axis=0, concat_axis=0, tiled=True)]
    all_gather x0 -> x2, blocking collectives: none -> 23.4 us  [cross_down(): return lax.all_gather(share.astype(jnp.bfloat16), 'mp', axis=0, tiled=True)]
    all_to_all x0 -> x2, waiting for transfers between devices: none -> 13.7 us  [sum_at_owner(): lax.all_to_all(parts, axis, split_axis=0, concat_axis=0, tiled=True)]
    all_to_all x3 -> x1, starting transfers between devices: 16.8 us -> 5.84 us  [copy_for_each(): return lax.all_to_all(copies, axis, split_axis=0, concat_axis=0, tiled=True)]
    all_to_all x0 -> x2, starting transfers between devices: none -> 10.4 us  [sum_at_owner(): lax.all_to_all(parts, axis, split_axis=0, concat_axis=0, tiled=True)]
    all_to_all x1, starting transfers between devices: 15.5 us -> 7.52 us  [local(): lax.all_to_all(send_rows.reshape(local_feats, peers, grad_cap), 'dp', spl...]
    unnamed x60 -> x54, local copies, waits for them, and re-layouts: 25.5 us -> 25.4 us
  transfers between devices with their start and end apart: 13 -> 14, of which waited for: 11 -> 12; matrix products, arithmetic and copies ran while one was open for 9% -> 8% of each run, Pallas kernels for 0% -> 0%
where the time goes in v6:
time: 506 us; the launch traced here: 505 us
  waiting for transfers between devices  281 us (56%)
  blocking collectives  75.8 us (15%)
  starting transfers between devices  41.4 us (8%)
  local copies, waits for them, and re-layouts  40.4 us (8%)
  matrix products  34.7 us (7%)
  other arithmetic  16.9 us (3%)
  between operations  14.5 us (3%)
    reduce_scatter x1, waiting for transfers between devices, local(): early_u = lax.psum_scatter(halves, 'dp', scatter_dimension=1, tiled=True)  111 us
    all_to_all x1, waiting for transfers between devices, local(): lax.all_to_all(served.reshape(local_feats, peers, look_cap, width), 'dp',...  48.8 us
    all_to_all x1, waiting for transfers between devices, local(): lax.all_to_all(send_grads.reshape(local_feats, peers, grad_cap, width), '...  39.8 us
    reduce_scatter x1, waiting for transfers between devices, local(): lax.psum_scatter(jnp.stack((grads_u[0], grads_v[0], grads_v[1])), 'dp', s...  38 us
    unnamed x54, local copies, waits for them, and re-layouts  25.4 us
    all_gather x2, blocking collectives, cross_down(): return lax.all_gather(share.astype(jnp.bfloat16), 'mp', axis=0, tiled=True)  23.4 us
    all_to_all x1, blocking collectives, local(): lax.all_to_all(wanted.reshape(local_feats, peers, look_cap), 'dp', split_...  22.8 us
    all_to_all x1, blocking collectives, copy_for_each(): return lax.all_to_all(copies, axis, split_axis=0, concat_axis=0, tiled=True)  20.3 us
  transfers between devices with their start and end apart: 14, of which 12 were waited for; matrix products, arithmetic and copies ran while one was open for 8% of the time, Pallas kernels for 0%

profile of v6, /device:TPU:8, one launch (start us, length us, event | category | flops | bytes accessed | tf_op | source)
XLA Modules:
  0.0 504.6 jit_solution(43356603869337143)
XLA Ops:
  10.6 8.1 %scatter_custom_fusion.1 = s32[4096]{0:T(1024)S(1)} fusion(s32[2048]{0:T(1024)S(1)} %bitcast.131, s32[2048]{0:T(1024)S(1)} %bitcast.133, s32[]{:T(128)} %constant.5.clone.1), kind=kCustom, calls=%fused_computation.108 | custom fusion | bytes 16388
  18.9 22.8 %all_to_all.40 = s32[4,64,16]{2,0,1:T(4,128)S(1)} all-to-all(s32[4,64,16]{2,0,1:T(4,128)S(1)} %copy.66), channel_id=1, replica_groups=mesh['dp'=64,'mp'=4] {'dp'}, dimensions={1} | all-to-all | bytes 32768 | tf_op jit(solution)/shard_map/all_to_all | solution.py:139
  41.8 2.1 fusion.14
  45.5 4.7 all-to-all-start.3
  52.7 48.8 %all-to-all-done.3 = bf16[4,64,16,256]{3,2,0,1:T(8,128)(2,1)S(1)} async-done(((bf16[4,64,16,256]{3,2,0,1:T(8,128)(2,1)}), bf16[4,64,16,256]{3,2,0,1:T(8,128)(2,1)S(1)}, u32[]{:S(2)}, u32[]{:S(2)}) %all-to-all-start.3) | async-done | bytes 2097184 | tf_op jit(solution)/shard_map/all_to_all | solution.py:149
  101.7 2.1 fusion.17
  104.5 2.5 fusion.39
  107.0 4.9 all-to-all-start.4
  112.1 6.4 %all-to-all-done.4 = f32[4,64,512]{2,1,0:T(8,128)S(1)} async-done(((f32[4,64,512]{2,1,0:T(8,128)}), f32[4,64,512]{2,1,0:T(8,128)S(1)}, u32[]{:S(2)}, u32[]{:S(2)}) %all-to-all-start.4) | async-done | bytes 524320 | tf_op jit(solution)/shard_map/all_to_all | solution.py:17
  118.6 11.8 %all_gather.6 = bf16[256,512]{1,0:T(8,128)(2,1)S(1)} all-gather(bf16[64,512]{1,0:T(8,128)(2,1)S(1)} %reduce_sum.102), channel_id=1, replica_groups=mesh['dp'=64,'mp'=4] {'mp'}, dimensions={0}, use_global_device_ids=true | all-gather | bytes 327680 | tf_op jit(solution)/shard_map/all_gather | solution.py:73
  130.4 2.8 fusion.26
  134.4 5.5 %all-to-all-start.5 = ((f32[4,64,512]{2,1,0:T(8,128)}), f32[4,64,512]{2,1,0:T(8,128)S(1)}, u32[]{:S(2)}, u32[]{:S(2)}) async-start(f32[4,64,512]{2,1,0:T(8,128)} %fusion.33), calls=%async_computation.5 | async-start | bytes 1048576 | tf_op jit(solution)/shard_map/all_to_all | solution.py:17
  139.9 7.3 %all-to-all-done.5 = f32[4,64,512]{2,1,0:T(8,128)S(1)} async-done(((f32[4,64,512]{2,1,0:T(8,128)}), f32[4,64,512]{2,1,0:T(8,128)S(1)}, u32[]{:S(2)}, u32[]{:S(2)}) %all-to-all-start.5) | async-done | bytes 524320 | tf_op jit(solution)/shard_map/all_to_all | solution.py:17
  147.3 11.6 %all_gather.7 = bf16[256,512]{1,0:T(8,128)(2,1)S(1)} all-gather(bf16[64,512]{1,0:T(8,128)(2,1)S(1)} %reduce_sum.103), channel_id=1, replica_groups=mesh['dp'=64,'mp'=4] {'mp'}, dimensions={0}, use_global_device_ids=true | all-gather | bytes 327680 | tf_op jit(solution)/shard_map/all_gather | solution.py:73
  158.9 2.9 fusion.23
  161.8 9.3 %psum.7 = f32[256]{0:T(256)S(1)} all-reduce(f32[256]{0:T(256)S(1)} %get-tuple-element.38), channel_id=1, replica_groups=mesh['dp'=64,'mp'=4] {'mp'}, use_global_device_ids=true, to_apply=%region_8.0 | all-reduce | flops 256 | bytes 2048 | tf_op jit(solution)/shard_map/psum | solution.py:181
  171.5 1.7 fusion.30
  173.5 20.3 %all_to_all.41 = f32[4,256,512]{2,1,0:T(8,128)} all-to-all(f32[4,256,512]{2,1,0:T(8,128)S(1)} %broadcast_in_dim.16), channel_id=1, replica_groups=mesh['dp'=64,'mp'=4] {'mp'}, dimensions={0} | all-to-all | bytes 4194304 | tf_op jit(solution)/shard_map/all_to_all | solution.py:23
  193.8 2.6 reduce_sum.105
  196.4 1.8 multiply_add_fusion
  199.4 2.1 copy.77
  201.4 2.8 convolution_bitcast_fusion.2
  204.3 1.7 fusion.36
  207.6 5.8 %all-to-all-start.7 = ((f32[4,256,512]{2,1,0:T(8,128)}), f32[4,256,512]{2,1,0:T(8,128)}, u32[]{:S(2)}, u32[]{:S(2)}) async-start(f32[4,256,512]{2,1,0:T(8,128)} %broadcast_in_dim.17), calls=%async_computation.8 | async-start | bytes 4194304 | tf_op jit(solution)/shard_map/all_to_all | solution.py:23
  213.5 2.9 convolution_bitcast_fusion
  216.4 1.8 convolution_bitcast_fusion.3
  218.2 10.4 %all-to-all-done.7 = f32[4,256,512]{2,1,0:T(8,128)} async-done(((f32[4,256,512]{2,1,0:T(8,128)}), f32[4,256,512]{2,1,0:T(8,128)}, u32[]{:S(2)}, u32[]{:S(2)}) %all-to-all-start.7) | async-done | bytes 2097184 | tf_op jit(solution)/shard_map/all_to_all | solution.py:23
  228.6 1.9 reduce_sum.106
  230.5 111.5 %reduce-scatter.3.cloned.1.call-done = f32[2,8,512]{2,1,0:T(8,128)} async-done(((f32[2,512,512]{2,1,0:T(8,128)}), f32[2,8,512]{2,1,0:T(8,128)}) %reduce-scatter.3.cloned.1.call-update) | async-done | bytes 32784 | tf_op jit(solution)/shard_map/reduce_scatter | solution.py:201
  343.6 5.0 pad_maximum_fusion
  349.3 8.1 %scatter_custom_fusion = s32[4096]{0:T(1024)S(1)} fusion(s32[2048]{0:T(1024)S(1)} %bitcast.132, s32[2048]{0:T(1024)S(1)} %bitcast.134, s32[]{:T(128)} %constant.11.clone.1), kind=kCustom, calls=%fused_computation.110 | custom fusion | bytes 16388
  358.2 7.5 %all-to-all-start = ((s32[4,64,16]{2,0,1:T(4,128)}), s32[4,64,16]{2,0,1:T(4,128)S(1)}, u32[]{:S(2)}, u32[]{:S(2)}) async-start(s32[4,64,16]{2,0,1:T(4,128)} %copy.56), calls=%async_computation | async-start | bytes 262144 | tf_op jit(solution)/shard_map/all_to_all | solution.py:114
  367.2 1.7 copy.58
  368.9 7.9 %all-to-all-done = s32[4,64,16]{2,0,1:T(4,128)S(1)} async-done(((s32[4,64,16]{2,0,1:T(4,128)}), s32[4,64,16]{2,0,1:T(4,128)S(1)}, u32[]{:S(2)}, u32[]{:S(2)}) %all-to-all-start) | async-done | bytes 16416 | tf_op jit(solution)/shard_map/all_to_all | solution.py:114
  376.7 5.6 %all-to-all-start.1 = ((bf16[4,64,16,256]{3,2,0,1:T(8,128)(2,1)}), bf16[4,64,16,256]{3,2,0,1:T(8,128)(2,1)}, u32[]{:S(2)}, u32[]{:S(2)}) async-start(bf16[4,64,16,256]{3,2,0,1:T(8,128)(2,1)} %copy.58), calls=%async_computation.1 | async-start | bytes 4194304 | tf_op jit(solution)/shard_map/all_to_all | solution.py:107
  385.1 4.3 collective-permute-done.1
  389.4 2.0 collective-permute-start.2
  391.4 2.9 copy.61
  394.4 39.8 %all-to-all-done.1 = bf16[4,64,16,256]{3,2,0,1:T(8,128)(2,1)} async-done(((bf16[4,64,16,256]{3,2,0,1:T(8,128)(2,1)}), bf16[4,64,16,256]{3,2,0,1:T(8,128)(2,1)}, u32[]{:S(2)}, u32[]{:S(2)}) %all-to-all-start.1) | async-done | bytes 2097184 | tf_op jit(solution)/shard_map/all_to_all | solution.py:107
  434.3 1.8 copy.59
  436.1 1.9 collective-permute-start.3
  438.0 2.9 multiply_reduce_fusion
  441.6 4.0 collective-permute-done.4
  445.7 1.8 collective-permute-start.5
  447.5 1.8 divide_subtract_fusion
  449.3 3.0 copy.74
  454.1 2.9 fusion.20
  456.9 38.0 %reduce-scatter.5.cloned.1.call-done = f32[3,8,1024]{2,1,0:T(8,128)} async-done(((f32[3,512,1024]{2,1,0:T(8,128)}), f32[3,8,1024]{2,1,0:T(8,128)}) %reduce-scatter.5.cloned.1.call-update) | async-done | bytes 98320 | tf_op jit(solution)/shard_map/reduce_scatter | solution.py:209
  (114 shorter events, 26.5 us)
Async XLA Ops:
  7.2 358.5 %copy-start = (bf16[4,512,256]{2,1,0:T(8,128)(2,1)S(1)}, bf16[4,512,256]{2,1,0:T(8,128)(2,1)}, u32[]{:S(2)}) copy-start(bf16[4,512,256]{2,1,0:T(8,128)(2,1)} %param.15) | copy-start | bytes 3145732
  7.2 3.1 copy-start.20
  7.2 3.2 copy-start.19
  7.2 3.0 copy-start.11
  7.2 3.4 copy-start.13
  7.2 34.6 %copy-start.8 = (f32[4,512,256]{2,1,0:T(8,128)S(1)}, f32[4,512,256]{2,1,0:T(8,128)}, u32[]{:S(2)}) copy-start(f32[4,512,256]{2,1,0:T(8,128)} %param.13) | copy-start | bytes 6291460
  45.5 56.1 %all-to-all-start.3 = ((bf16[4,64,16,256]{3,2,0,1:T(8,128)(2,1)}), bf16[4,64,16,256]{3,2,0,1:T(8,128)(2,1)S(1)}, u32[]{:S(2)}, u32[]{:S(2)}) async-start(bf16[4,64,16,256]{3,2,0,1:T(8,128)(2,1)} %copy.68), calls=%async_computation.3 | async-start | bytes 4194304 | tf_op jit(solution)/shard_map/all_to_all | solution.py:149
  50.2 2.5 copy-start.17
  104.1 7.8 %copy-start.14 = (f32[2,1024]{1,0:T(2,128)S(1)}, f32[2,1024]{1,0:T(2,128)}, u32[]{:S(2)}) copy-start(f32[2,1024]{1,0:T(2,128)} %param.24) | copy-start | bytes 24580
  107.0 11.5 %all-to-all-start.4 = ((f32[4,64,512]{2,1,0:T(8,128)}), f32[4,64,512]{2,1,0:T(8,128)S(1)}, u32[]{:S(2)}, u32[]{:S(2)}) async-start(f32[4,64,512]{2,1,0:T(8,128)} %fusion.39), calls=%async_computation.4 | async-start | bytes 1048576 | tf_op jit(solution)/shard_map/all_to_all | solution.py:17
  118.6 14.6 %copy-start.9 = (bf16[2,512,1024]{2,1,0:T(8,128)(2,1)S(1)}, bf16[2,512,1024]{2,1,0:T(8,128)(2,1)}, u32[]{:S(2)}) copy-start(bf16[2,512,1024]{2,1,0:T(8,128)(2,1)} %param.23) | copy-start | bytes 6291460
  130.4 4.0 copy-start.5
  133.1 25.8 %copy-start.3 = (bf16[256,1024]{1,0:T(8,128)(2,1)}, bf16[256,1024]{1,0:T(8,128)(2,1)S(1)}, u32[]{:S(2)}) copy-start(bf16[256,1024]{1,0:T(8,128)(2,1)S(1)} %get-tuple-element.59) | copy-start | bytes 1572868
  133.1 6.8 %copy-start.10 = (f32[1024]{0:T(1024)S(1)}, f32[1024]{0:T(1024)}, u32[]{:S(2)}) copy-start(f32[1024]{0:T(1024)} %param.25) | copy-start | bytes 12292
  134.4 12.8 %all-to-all-start.5 = ((f32[4,64,512]{2,1,0:T(8,128)}), f32[4,64,512]{2,1,0:T(8,128)S(1)}, u32[]{:S(2)}, u32[]{:S(2)}) async-start(f32[4,64,512]{2,1,0:T(8,128)} %fusion.33), calls=%async_computation.5 | async-start | bytes 1048576 | tf_op jit(solution)/shard_map/all_to_all | solution.py:17
  139.9 202.1 %reduce-scatter.3.cloned.1.call-start = ((), (), s32[]{:S(2)}) async-start(), calls=%async_computation.10 | async-start | bytes 2129920 | tf_op jit(solution)/shard_map/reduce_scatter | solution.py:201
  147.3 23.8 %copy-start.18 = (s32[256]{0:T(256)S(1)}, s32[256]{0:T(256)}, u32[]{:S(2)}) copy-start(s32[256]{0:T(256)} %param.21) | copy-start | bytes 3076
  196.4 1.8 copy-start.7
  207.6 21.0 %all-to-all-start.7 = ((f32[4,256,512]{2,1,0:T(8,128)}), f32[4,256,512]{2,1,0:T(8,128)}, u32[]{:S(2)}, u32[]{:S(2)}) async-start(f32[4,256,512]{2,1,0:T(8,128)} %broadcast_in_dim.17), calls=%async_computation.8 | async-start | bytes 4194304 | tf_op jit(solution)/shard_map/all_to_all | solution.py:23
  213.5 2.9 copy-start.6
  213.5 281.4 %reduce-scatter.5.cloned.1.call-start = ((), (), s32[]{:S(2)}) async-start(), calls=%async_computation.11 | async-start | bytes 6389760 | tf_op jit(solution)/shard_map/reduce_scatter | solution.py:209
  342.0 1.6 copy-start.2
  348.6 0.7 copy-start.15
  358.2 18.6 %all-to-all-start = ((s32[4,64,16]{2,0,1:T(4,128)}), s32[4,64,16]{2,0,1:T(4,128)S(1)}, u32[]{:S(2)}, u32[]{:S(2)}) async-start(s32[4,64,16]{2,0,1:T(4,128)} %copy.56), calls=%async_computation | async-start | bytes 262144 | tf_op jit(solution)/shard_map/all_to_all | solution.py:114
  376.7 57.5 %all-to-all-start.1 = ((bf16[4,64,16,256]{3,2,0,1:T(8,128)(2,1)}), bf16[4,64,16,256]{3,2,0,1:T(8,128)(2,1)}, u32[]{:S(2)}, u32[]{:S(2)}) async-start(bf16[4,64,16,256]{3,2,0,1:T(8,128)(2,1)} %copy.58), calls=%async_computation.1 | async-start | bytes 4194304 | tf_op jit(solution)/shard_map/all_to_all | solution.py:107
  382.4 1.3 collective-permute-start
  383.6 5.7 %collective-permute-start.1 = (f32[3,1024]{1,0:T(4,128)S(1)}, f32[3,1024]{1,0:T(4,128)S(1)}, u32[]{:S(2)}, u32[]{:S(2)}) collective-permute-start(f32[3,1024]{1,0:T(4,128)S(1)} %fusion.75), channel_id=1, source_target_pairs={{0,8},{4,12},{8,0},{12,4},{16,24},{20,28},{24,16},{28,20},{32,40},... | collective-permute-start | bytes 36872 | tf_op jit(solution)/shard_map/ppermute | solution.py:34
  389.4 46.7 %collective-permute-start.2 = (f32[3,1024]{1,0:T(4,128)S(1)}, f32[3,1024]{1,0:T(4,128)S(1)}, u32[]{:S(2)}, u32[]{:S(2)}) collective-permute-start(f32[3,1024]{1,0:T(4,128)S(1)} %fusion.98), channel_id=1, source_target_pairs={{0,16},{4,20},{8,24},{12,28},{16,0},{20,4},{24,8},{28,12},{32,48},... | collective-permute-start | bytes 36872 | tf_op jit(solution)/shard_map/ppermute | solution.py:34
  436.1 4.8 collective-permute-start.3
  438.0 3.0 copy-start.16
  438.0 9.4 %copy-start.1 = (f32[4,512,256]{1,2,0:T(8,128)S(1)}, f32[4,512,256]{1,2,0:T(8,128)}, u32[]{:S(2)}) copy-start(f32[4,512,256]{1,2,0:T(8,128)} %copy.61) | copy-start | bytes 6291460
  440.9 4.7 collective-permute-start.4
  445.7 7.8 %collective-permute-start.5 = (f32[3,1024]{1,0:T(4,128)S(1)}, f32[3,1024]{1,0:T(4,128)S(1)}, u32[]{:S(2)}, u32[]{:S(2)}) collective-permute-start(f32[3,1024]{1,0:T(4,128)S(1)} %add.114), channel_id=1, source_target_pairs={{0,128},{4,132},{8,136},{12,140},{16,144},{20,148},{24,152},{28,15... | collective-permute-start | bytes 36872 | tf_op jit(solution)/shard_map/ppermute | solution.py:34
  449.3 4.8 copy-start.4
  454.1 41.6 %copy-start.12 = (f32[2,8,512]{2,1,0:T(8,128)S(1)}, f32[2,8,512]{2,1,0:T(8,128)}, u32[]{:S(2)}) copy-start(f32[2,8,512]{2,1,0:T(8,128)} %reduce-scatter.3.cloned.1.call-done) | copy-start | bytes 98308
Sparse Core Ops, SparseCore 0:
  204.4 137.5 reduce-scatter.2
  348.7 146.1 reduce-scatter.4

commit v7 on v0

--- a/solution.py
+++ b/solution.py
@@ -1,5 +1,8 @@
+import functools
+
 import jax
 import jax.numpy as jnp
+import numpy as np
 from jax import lax
 from jax.sharding import PartitionSpec as P
 
@@ -26,6 +29,29 @@
 def over_copies(array, axis):
     return copy_for_each(array, axis).sum(axis=0)
 
+
+def ring_sum_scatter(blocks, axis, stride):
+    size = blocks.shape[0]
+    peers = lax.axis_size(axis)
+    pos = (lax.axis_index(axis) // stride) % size
+    ahead = [
+        (i, i + (((i // stride) % size + 1) % size - (i // stride) % size) * stride)
+        for i in range(peers)
+    ]
+    carry = blocks[(pos + size - 1) % size]
+    for step in range(size - 1):
+        carry = lax.ppermute(carry, axis, ahead) + blocks[(pos + 2 * size - step - 2) % size]
+    return carry
+
+def tree_sum_scatter(array, axis, dim, splits):
+    lead = array.shape[:dim]
+    parts = array.reshape(*lead, *splits, array.shape[dim] // np.prod(splits), *array.shape[dim + 1:])
+    stride = 1
+    for level in reversed(range(len(splits))):
+        parts = jnp.moveaxis(parts, dim + level, 0)
+        parts = ring_sum_scatter(parts, axis, stride)
+        stride *= splits[level]
+    return parts
 
 def side_by_side(arrays, axis, dim, along):
     widths = [a.shape[along] for a in arrays]
@@ -64,7 +90,20 @@
     return lax.all_gather(share.astype(jnp.bfloat16), "mp", axis=0, tiled=True)
 
 
+def dp_factors(mesh):
+    column = mesh.devices[:, 0]
+    try:
+        keys = [(d.coords[2], d.coords[0], d.core_on_chip) for d in column]
+    except AttributeError:
+        return (len(column),)
+    factors = tuple(len(set(k[level] for k in keys)) for level in range(3))
+    if int(np.prod(factors)) != len(column) or keys != sorted(keys):
+        return (len(column),)
+    return factors
+
+
 def local(
+    splits,
     embed_table,
     accum,
     stale_grad,
@@ -192,9 +231,8 @@
         upstream = upstream + jnp.dot(back_sum, v_weight[layer], preferred_element_type=jnp.float32)
         grads_u[layer] = grad_u_layer
         grads_v[layer] = down_factor_gradient
-    grad_u = jnp.stack(grads_u)
-    grad_v = jnp.stack(grads_v)
-    grad_u, grad_v = side_by_side((grad_u, grad_v), "dp", 1, 0)
+    both = jnp.concatenate((jnp.stack(grads_u), jnp.stack(grads_v)), axis=0)
+    grad_u, grad_v = jnp.split(tree_sum_scatter(both, "dp", 1, splits), 2, axis=0)
     grad_small = over_copies(jnp.stack(bias_grads + [head_grad]), "dp")
     grad_pooled = (upstream + to_start).astype(jnp.bfloat16)
     return (new_table, new_accum, grad_u, grad_v, grad_small, grad_pooled)
@@ -202,7 +240,7 @@
 
 def solution(mesh):
     return jax.shard_map(
-        local,
+        functools.partial(local, dp_factors(mesh)),
         mesh=mesh,
         in_specs=(
             P("mp", "dp", None),

time: 406 us -> 440 us (1.084)
  between operations: 14.5 us -> 1.33 us
  starting transfers between devices: 40.8 us -> 53 us
  local copies, waits for them, and re-layouts: 38.8 us -> 50.4 us
  other arithmetic: 16.9 us -> 28.4 us
  waiting for transfers between devices: 186 us -> 192 us
  matrix products: 31.6 us -> 36.9 us
    ppermute x0 -> x11, waiting for transfers between devices: none -> 113 us  [ring_sum_scatter(): lax.ppermute(carry, axis, ahead)]
    all_to_all x1, waiting for transfers between devices: 51.6 us -> 0.01 us  [local(): lax.all_to_all(send_grads.reshape(local_feats, peers, grad_cap, width), '...]
    reduce_scatter x1 -> x0, waiting for transfers between devices: 30.5 us -> none  [side_by_side(): filled = lax.psum_scatter(both, axis, scatter_dimension=dim, tiled=True)]
    all_to_all x2, waiting for transfers between devices: 33.8 us -> 7.71 us  [copy_for_each(): return lax.all_to_all(copies, axis, split_axis=0, concat_axis=0, tiled=True)]
    add x0 -> x11, other arithmetic: none -> 13.8 us  [ring_sum_scatter(): lax.ppermute(carry, axis, ahead)]
    ppermute x0 -> x11, starting transfers between devices: none -> 8.86 us  [ring_sum_scatter(): lax.ppermute(carry, axis, ahead)]
    unnamed x58 -> x70, local copies, waits for them, and re-layouts: 25.5 us -> 29.3 us
  transfers between devices with their start and end apart: 8 -> 18, of which waited for: 8 -> 12; matrix products, arithmetic and copies ran while one was open for 10% -> 12% of each run, Pallas kernels for 0% -> 0%
where the time goes in v7:
time: 440 us; the launch traced here: 437 us
  waiting for transfers between devices  192 us (44%)
  blocking collectives  75.6 us (17%)
  starting transfers between devices  53 us (12%)
  local copies, waits for them, and re-layouts  50.4 us (11%)
  matrix products  36.9 us (8%)
  other arithmetic  28.4 us (6%)
    ppermute x11, waiting for transfers between devices, ring_sum_scatter(): lax.ppermute(carry, axis, ahead)  113 us
    all_to_all x1, waiting for transfers between devices, local(): lax.all_to_all(served.reshape(local_feats, peers, look_cap, width), 'dp',...  50.3 us
    unnamed x70, local copies, waits for them, and re-layouts  29.3 us
    all_gather x2, blocking collectives, cross_down(): return lax.all_gather(share.astype(jnp.bfloat16), 'mp', axis=0, tiled=True)  23.4 us
    all_to_all x1, blocking collectives, local(): lax.all_to_all(wanted.reshape(local_feats, peers, look_cap), 'dp', split_...  22.8 us
    all_to_all x1, blocking collectives, copy_for_each(): return lax.all_to_all(copies, axis, split_axis=0, concat_axis=0, tiled=True)  20.1 us
    all_to_all x2, starting transfers between devices, copy_for_each(): return lax.all_to_all(copies, axis, split_axis=0, concat_axis=0, tiled=True)  14.3 us
    add x11, other arithmetic, ring_sum_scatter(): lax.ppermute(carry, axis, ahead)  13.8 us
  transfers between devices with their start and end apart: 18, of which 12 were waited for; matrix products, arithmetic and copies ran while one was open for 12% of the time, Pallas kernels for 0%

profile of v7, /device:TPU:8, one launch (start us, length us, event | category | flops | bytes accessed | tf_op | source)
XLA Modules:
  0.0 437.3 jit_solution(2505857900949818380)
XLA Ops:
  4.6 8.1 %scatter_custom_fusion.1 = s32[4096]{0:T(1024)S(1)} fusion(s32[2048]{0:T(1024)S(1)} %bitcast.160, s32[2048]{0:T(1024)S(1)} %bitcast.162, s32[]{:T(128)} %constant.180.clone.1), kind=kCustom, calls=%fused_computation.118 | custom fusion | bytes 16388
  12.8 22.8 %all_to_all.45 = s32[4,64,16]{2,0,1:T(4,128)S(1)} all-to-all(s32[4,64,16]{2,0,1:T(4,128)S(1)} %copy.126), channel_id=1, replica_groups=mesh['dp'=64,'mp'=4] {'dp'}, dimensions={1} | all-to-all | bytes 32768 | tf_op jit(solution)/shard_map/all_to_all | solution.py:169
  35.7 3.7 fusion.14
  41.1 5.6 %all-to-all-start.3 = ((bf16[4,64,16,256]{3,2,0,1:T(8,128)(2,1)}), bf16[4,64,16,256]{3,2,0,1:T(8,128)(2,1)}, u32[]{:S(2)}, u32[]{:S(2)}) async-start(bf16[4,64,16,256]{3,2,0,1:T(8,128)(2,1)} %copy.128), calls=%async_computation.3 | async-start | bytes 4194304 | tf_op jit(solution)/shard_map/all_to_all | solution.py:179
  47.5 50.3 %all-to-all-done.3 = bf16[4,64,16,256]{3,2,0,1:T(8,128)(2,1)} async-done(((bf16[4,64,16,256]{3,2,0,1:T(8,128)(2,1)}), bf16[4,64,16,256]{3,2,0,1:T(8,128)(2,1)}, u32[]{:S(2)}, u32[]{:S(2)}) %all-to-all-start.3) | async-done | bytes 2097184 | tf_op jit(solution)/shard_map/all_to_all | solution.py:179
  99.6 2.1 fusion.17
  102.3 2.5 fusion.38
  104.8 4.9 %all-to-all-start.4 = ((f32[4,64,512]{2,1,0:T(8,128)}), f32[4,64,512]{2,1,0:T(8,128)S(1)}, u32[]{:S(2)}, u32[]{:S(2)}) async-start(f32[4,64,512]{2,1,0:T(8,128)} %fusion.38), calls=%async_computation.4 | async-start | bytes 1048576 | tf_op jit(solution)/shard_map/all_to_all | solution.py:20
  110.0 6.4 %all-to-all-done.4 = f32[4,64,512]{2,1,0:T(8,128)S(1)} async-done(((f32[4,64,512]{2,1,0:T(8,128)}), f32[4,64,512]{2,1,0:T(8,128)S(1)}, u32[]{:S(2)}, u32[]{:S(2)}) %all-to-all-start.4) | async-done | bytes 524320 | tf_op jit(solution)/shard_map/all_to_all | solution.py:20
  116.4 11.8 %all_gather.6 = bf16[256,512]{1,0:T(8,128)(2,1)S(1)} all-gather(bf16[64,512]{1,0:T(8,128)(2,1)S(1)} %reduce_sum.111), channel_id=1, replica_groups=mesh['dp'=64,'mp'=4] {'mp'}, dimensions={0}, use_global_device_ids=true | all-gather | bytes 327680 | tf_op jit(solution)/shard_map/all_gather | solution.py:90
  128.2 2.8 fusion.26
  132.3 5.5 %all-to-all-start.5 = ((f32[4,64,512]{2,1,0:T(8,128)}), f32[4,64,512]{2,1,0:T(8,128)S(1)}, u32[]{:S(2)}, u32[]{:S(2)}) async-start(f32[4,64,512]{2,1,0:T(8,128)} %fusion.32), calls=%async_computation.5 | async-start | bytes 1048576 | tf_op jit(solution)/shard_map/all_to_all | solution.py:20
  137.8 7.3 %all-to-all-done.5 = f32[4,64,512]{2,1,0:T(8,128)S(1)} async-done(((f32[4,64,512]{2,1,0:T(8,128)}), f32[4,64,512]{2,1,0:T(8,128)S(1)}, u32[]{:S(2)}, u32[]{:S(2)}) %all-to-all-start.5) | async-done | bytes 524320 | tf_op jit(solution)/shard_map/all_to_all | solution.py:20
  145.2 11.6 %all_gather.7 = bf16[256,512]{1,0:T(8,128)(2,1)S(1)} all-gather(bf16[64,512]{1,0:T(8,128)(2,1)S(1)} %reduce_sum.112), channel_id=1, replica_groups=mesh['dp'=64,'mp'=4] {'mp'}, dimensions={0}, use_global_device_ids=true | all-gather | bytes 327680 | tf_op jit(solution)/shard_map/all_gather | solution.py:90
  156.7 2.9 fusion.23
  159.6 9.3 %psum.7 = f32[256]{0:T(256)S(1)} all-reduce(f32[256]{0:T(256)S(1)} %get-tuple-element.52), channel_id=1, replica_groups=mesh['dp'=64,'mp'=4] {'mp'}, use_global_device_ids=true, to_apply=%region_8.0 | all-reduce | flops 256 | bytes 2048 | tf_op jit(solution)/shard_map/psum | solution.py:211
  170.0 1.9 fusion.29
  172.1 20.1 %all_to_all.46 = f32[4,256,512]{2,1,0:T(8,128)} all-to-all(f32[4,256,512]{2,1,0:T(8,128)S(1)} %broadcast_in_dim.18), channel_id=1, replica_groups=mesh['dp'=64,'mp'=4] {'mp'}, dimensions={0} | all-to-all | bytes 4194304 | tf_op jit(solution)/shard_map/all_to_all | solution.py:26
  192.2 2.6 reduce_sum.114
  194.9 2.5 fusion.58
  199.4 5.9 %all-to-all-start.7 = ((f32[4,256,512]{2,1,0:T(8,128)}), f32[4,256,512]{2,1,0:T(8,128)}, u32[]{:S(2)}, u32[]{:S(2)}) async-start(f32[4,256,512]{2,1,0:T(8,128)} %broadcast_in_dim.19), calls=%async_computation.7 | async-start | bytes 4194304 | tf_op jit(solution)/shard_map/all_to_all | solution.py:26
  206.2 3.0 convolution_bitcast_fusion.1
  212.8 7.7 %all-to-all-done.7 = f32[4,256,512]{2,1,0:T(8,128)} async-done(((f32[4,256,512]{2,1,0:T(8,128)}), f32[4,256,512]{2,1,0:T(8,128)}, u32[]{:S(2)}, u32[]{:S(2)}) %all-to-all-start.7) | async-done | bytes 2097184 | tf_op jit(solution)/shard_map/all_to_all | solution.py:26
  220.5 1.8 reduce_sum.115
  224.1 2.6 pad_maximum_fusion
  226.7 2.5 dynamic-slice_bitcast_fusion
  229.2 2.0 copy-done.1
  231.2 7.5 %collective-permute-done = f32[4,8,4,8,1024]{4,3,2,1,0:T(8,128)} collective-permute-done((f32[4,8,4,8,1024]{4,3,2,1,0:T(8,128)}, f32[4,8,4,8,1024]{4,3,2,1,0:T(8,128)}, u32[]{:S(2)}, u32[]{:S(2)}) %collective-permute-start) | collective-permute-done | bytes 4194336 | tf_op jit(solution)/shard_map/ppermute | solution.py:43
  238.7 4.4 %bitcast_add_fusion = f32[4,8,4,8,1024]{4,3,2,1,0:T(8,128)S(1)} fusion(f32[4,8,4,8,1024]{4,3,2,1,0:T(8,128)} %collective-permute-done, f32[4,8,4,2,8,1024]{5,4,3,2,1,0:T(8,128)} %copy-done.1, s32[]{:T(128)S(6)} %select_n.137), kind=kLoop, calls=%fused_computation.9 | loop fusion | flops 1048576 | bytes 12582916 | tf_op jit(solution)/shard_map/add | solution.py:43
  243.1 1.9 copy-done.2
  246.8 8.1 %scatter_custom_fusion = s32[4096]{0:T(1024)S(1)} fusion(s32[2048]{0:T(1024)S(1)} %bitcast.159, s32[2048]{0:T(1024)S(1)} %bitcast.161, s32[]{:T(128)} %constant.177.clone.1), kind=kCustom, calls=%fused_computation.120 | custom fusion | bytes 16388
  255.7 8.3 %all-to-all-start = ((s32[4,64,16]{2,0,1:T(4,128)}), s32[4,64,16]{2,0,1:T(4,128)S(1)}, u32[]{:S(2)}, u32[]{:S(2)}) async-start(s32[4,64,16]{2,0,1:T(4,128)} %copy.116), calls=%async_computation | async-start | bytes 262144 | tf_op jit(solution)/shard_map/all_to_all | solution.py:144
  267.8 7.2 %all-to-all-done = s32[4,64,16]{2,0,1:T(4,128)S(1)} async-done(((s32[4,64,16]{2,0,1:T(4,128)}), s32[4,64,16]{2,0,1:T(4,128)S(1)}, u32[]{:S(2)}, u32[]{:S(2)}) %all-to-all-start) | async-done | bytes 16416 | tf_op jit(solution)/shard_map/all_to_all | solution.py:144
  275.0 5.6 %all-to-all-start.1 = ((bf16[4,64,16,256]{3,2,0,1:T(8,128)(2,1)}), bf16[4,64,16,256]{3,2,0,1:T(8,128)(2,1)}, u32[]{:S(2)}, u32[]{:S(2)}) async-start(bf16[4,64,16,256]{3,2,0,1:T(8,128)(2,1)} %copy.118), calls=%async_computation.1 | async-start | bytes 4194304 | tf_op jit(solution)/shard_map/all_to_all | solution.py:137
  284.0 44.3 %collective-permute-done.2 = f32[4,8,8,1024]{3,2,1,0:T(8,128)} collective-permute-done((f32[4,8,8,1024]{3,2,1,0:T(8,128)S(1)}, f32[4,8,8,1024]{3,2,1,0:T(8,128)}, u32[]{:S(2)}, u32[]{:S(2)}) %collective-permute-start.2) | collective-permute-done | bytes 1048608 | tf_op jit(solution)/shard_map/ppermute | solution.py:43
  330.1 25.7 %collective-permute-done.3 = f32[4,8,8,1024]{3,2,1,0:T(8,128)} collective-permute-done((f32[4,8,8,1024]{3,2,1,0:T(8,128)S(1)}, f32[4,8,8,1024]{3,2,1,0:T(8,128)}, u32[]{:S(2)}, u32[]{:S(2)}) %collective-permute-start.3) | collective-permute-done | bytes 1048608 | tf_op jit(solution)/shard_map/ppermute | solution.py:43
  360.0 4.8 %collective-permute-done.4 = f32[4,8,1024]{2,1,0:T(8,128)} collective-permute-done((f32[4,8,1024]{2,1,0:T(8,128)}, f32[4,8,1024]{2,1,0:T(8,128)}, u32[]{:S(2)}, u32[]{:S(2)}) %collective-permute-start.4) | collective-permute-done | bytes 131104 | tf_op jit(solution)/shard_map/ppermute | solution.py:43
  366.9 2.9 copy.121
  372.0 3.2 copy.119
  378.9 8.5 %all-to-all-start.8 = ((f32[64,3,1024]{2,1,0:T(4,128)}), f32[64,3,1024]{2,1,0:T(4,128)}, u32[]{:S(2)}, u32[]{:S(2)}) async-start(f32[64,3,1024]{2,1,0:T(4,128)} %broadcast_in_dim.20), calls=%async_computation.8 | async-start | bytes 2097152 | tf_op jit(solution)/shard_map/all_to_all | solution.py:26
  389.9 4.5 %multiply_reduce_fusion = (f32[4,512]{1,0:T(4,128)S(1)}, f32[4,512,256]{1,2,0:T(8,128)S(1)}) fusion(bf16[4,1024,256]{2,1,0:T(8,128)(2,1)} %bitcast.142, s32[4,1024]{1,0:T(4,128)} %eq.127), kind=kOutput, calls=%fused_computation.23 | convolution fusion | flops 1076885504 | bytes 4218880 | tf_op jit(solution)/shard_map/wjc,wjl->wcl/dot_general | solution.py:152
  394.4 21.8 %collective-permute-done.7 = f32[4,8,1024]{2,1,0:T(8,128)S(1)} collective-permute-done((f32[4,8,1024]{2,1,0:T(8,128)S(1)}, f32[4,8,1024]{2,1,0:T(8,128)S(1)}, u32[]{:S(2)}, u32[]{:S(2)}) %collective-permute-start.7) | collective-permute-done | bytes 131104 | tf_op jit(solution)/shard_map/ppermute | solution.py:43
  416.9 5.7 %collective-permute-done.8 = f32[4,8,1024]{2,1,0:T(8,128)S(1)} collective-permute-done((f32[4,8,1024]{2,1,0:T(8,128)S(1)}, f32[4,8,1024]{2,1,0:T(8,128)S(1)}, u32[]{:S(2)}, u32[]{:S(2)}) %collective-permute-start.8) | collective-permute-done | bytes 131104 | tf_op jit(solution)/shard_map/ppermute | solution.py:43
  422.7 1.8 divide_subtract_fusion
  424.5 2.9 copy.138
  427.4 2.0 reduce_sum.119
  430.5 3.1 fusion.20
  433.6 3.0 collective-permute-done.10
  (145 shorter events, 48.7 us)
Async XLA Ops:
  0.6 264.0 %copy-start = (bf16[4,512,256]{2,1,0:T(8,128)(2,1)S(1)}, bf16[4,512,256]{2,1,0:T(8,128)(2,1)}, u32[]{:S(2)}) copy-start(bf16[4,512,256]{2,1,0:T(8,128)(2,1)} %param.15) | copy-start | bytes 3145732
  0.6 3.6 copy-start.28
  0.7 3.7 copy-start.27
  0.7 2.9 copy-start.16
  0.7 3.9 copy-start.20
  41.1 56.8 %all-to-all-start.3 = ((bf16[4,64,16,256]{3,2,0,1:T(8,128)(2,1)}), bf16[4,64,16,256]{3,2,0,1:T(8,128)(2,1)}, u32[]{:S(2)}, u32[]{:S(2)}) async-start(bf16[4,64,16,256]{3,2,0,1:T(8,128)(2,1)} %copy.128), calls=%async_computation.3 | async-start | bytes 4194304 | tf_op jit(solution)/shard_map/all_to_all | solution.py:179
  46.6 0.8 copy-start.25
  102.0 7.8 %copy-start.21 = (f32[2,1024]{1,0:T(2,128)S(1)}, f32[2,1024]{1,0:T(2,128)}, u32[]{:S(2)}) copy-start(f32[2,1024]{1,0:T(2,128)} %param.24) | copy-start | bytes 24580
  104.8 11.5 %all-to-all-start.4 = ((f32[4,64,512]{2,1,0:T(8,128)}), f32[4,64,512]{2,1,0:T(8,128)S(1)}, u32[]{:S(2)}, u32[]{:S(2)}) async-start(f32[4,64,512]{2,1,0:T(8,128)} %fusion.38), calls=%async_computation.4 | async-start | bytes 1048576 | tf_op jit(solution)/shard_map/all_to_all | solution.py:20
  116.4 14.6 %copy-start.13 = (bf16[2,512,1024]{2,1,0:T(8,128)(2,1)S(1)}, bf16[2,512,1024]{2,1,0:T(8,128)(2,1)}, u32[]{:S(2)}) copy-start(bf16[2,512,1024]{2,1,0:T(8,128)(2,1)} %param.23) | copy-start | bytes 6291460
  128.2 4.0 copy-start.8
  131.0 25.8 %copy-start.6 = (bf16[256,1024]{1,0:T(8,128)(2,1)}, bf16[256,1024]{1,0:T(8,128)(2,1)S(1)}, u32[]{:S(2)}) copy-start(bf16[256,1024]{1,0:T(8,128)(2,1)S(1)} %get-tuple-element.72) | copy-start | bytes 1572868
  131.0 6.8 %copy-start.14 = (f32[1024]{0:T(1024)S(1)}, f32[1024]{0:T(1024)}, u32[]{:S(2)}) copy-start(f32[1024]{0:T(1024)} %param.25) | copy-start | bytes 12292
  132.3 12.8 %all-to-all-start.5 = ((f32[4,64,512]{2,1,0:T(8,128)}), f32[4,64,512]{2,1,0:T(8,128)S(1)}, u32[]{:S(2)}, u32[]{:S(2)}) async-start(f32[4,64,512]{2,1,0:T(8,128)} %fusion.32), calls=%async_computation.5 | async-start | bytes 1048576 | tf_op jit(solution)/shard_map/all_to_all | solution.py:20
  145.1 23.8 %copy-start.26 = (s32[256]{0:T(256)S(1)}, s32[256]{0:T(256)}, u32[]{:S(2)}) copy-start(s32[256]{0:T(256)} %param.21) | copy-start | bytes 3076
  169.0 25.9 %copy-start.17 = (f32[256]{0:T(256)}, f32[256]{0:T(256)S(1)}, u32[]{:S(2)}) copy-start(f32[256]{0:T(256)S(1)} %fusion.72) | copy-start | bytes 3076
  170.0 2.2 copy-start.11
  194.9 2.5 copy-start.5
  199.4 21.0 %all-to-all-start.7 = ((f32[4,256,512]{2,1,0:T(8,128)}), f32[4,256,512]{2,1,0:T(8,128)}, u32[]{:S(2)}, u32[]{:S(2)}) async-start(f32[4,256,512]{2,1,0:T(8,128)} %broadcast_in_dim.19), calls=%async_computation.7 | async-start | bytes 4194304 | tf_op jit(solution)/shard_map/all_to_all | solution.py:26
  206.1 3.0 copy-start.7
  206.2 3.0 copy-start.12
  209.2 1.8 copy-start.9
  222.5 1.6 copy-start.4
  226.7 4.5 %copy-start.1 = (f32[4,8,4,2,8,1024]{5,4,3,2,1,0:T(8,128)}, f32[4,8,4,2,8,1024]{5,4,3,2,1,0:T(8,128)S(1)}, u32[]{:S(2)}) copy-start(f32[4,8,4,2,8,1024]{5,4,3,2,1,0:T(8,128)S(1)} %pad_maximum_fusion) | copy-start | bytes 25165828
  231.2 7.5 %collective-permute-start = (f32[4,8,4,8,1024]{4,3,2,1,0:T(8,128)}, f32[4,8,4,8,1024]{4,3,2,1,0:T(8,128)}, u32[]{:S(2)}, u32[]{:S(2)}) collective-permute-start(f32[4,8,4,8,1024]{4,3,2,1,0:T(8,128)} %dynamic-slice_bitcast_fusion), channel_id=1, source_target_pairs={{0,4},{4,0},{8,12},{12,8},{16,20},{20,16},{24,28},{28,24},{32,36},... | collective-permute-start | bytes 12582920 | tf_op jit(solution)/shard_map/ppermute | solution.py:43
  243.1 1.9 copy-start.2
  245.0 1.8 copy-start.22
  245.1 35.5 %collective-permute-start.1 = (f32[4,8,8,1024]{3,2,1,0:T(8,128)S(1)}, f32[4,8,8,1024]{3,2,1,0:T(8,128)}, u32[]{:S(2)}, u32[]{:S(2)}) collective-permute-start(f32[4,8,8,1024]{3,2,1,0:T(8,128)S(1)} %dynamic-slice_bitcast_fusion.1), channel_id=1, source_target_pairs={{0,8},{4,12},{8,16},{12,20},{16,24},{20,28},{24,0},{28,4},{32,40},... | collective-permute-start | bytes 3145736 | tf_op jit(solution)/shard_map/ppermute | solution.py:43
  255.7 19.3 %all-to-all-start = ((s32[4,64,16]{2,0,1:T(4,128)}), s32[4,64,16]{2,0,1:T(4,128)S(1)}, u32[]{:S(2)}, u32[]{:S(2)}) async-start(s32[4,64,16]{2,0,1:T(4,128)} %copy.116), calls=%async_computation | async-start | bytes 262144 | tf_op jit(solution)/shard_map/all_to_all | solution.py:144
  275.0 97.0 %all-to-all-start.1 = ((bf16[4,64,16,256]{3,2,0,1:T(8,128)(2,1)}), bf16[4,64,16,256]{3,2,0,1:T(8,128)(2,1)}, u32[]{:S(2)}, u32[]{:S(2)}) async-start(bf16[4,64,16,256]{3,2,0,1:T(8,128)(2,1)} %copy.118), calls=%async_computation.1 | async-start | bytes 4194304 | tf_op jit(solution)/shard_map/all_to_all | solution.py:137
  282.3 46.0 %collective-permute-start.2 = (f32[4,8,8,1024]{3,2,1,0:T(8,128)S(1)}, f32[4,8,8,1024]{3,2,1,0:T(8,128)}, u32[]{:S(2)}, u32[]{:S(2)}) collective-permute-start(f32[4,8,8,1024]{3,2,1,0:T(8,128)S(1)} %bitcast_add_fusion.3), channel_id=1, source_target_pairs={{0,8},{4,12},{8,16},{12,20},{16,24},{20,28},{24,0},{28,4},{32,40},... | collective-permute-start | bytes 3145736 | tf_op jit(solution)/shard_map/ppermute | solution.py:43
  330.0 25.8 %collective-permute-start.3 = (f32[4,8,8,1024]{3,2,1,0:T(8,128)S(1)}, f32[4,8,8,1024]{3,2,1,0:T(8,128)}, u32[]{:S(2)}, u32[]{:S(2)}) collective-permute-start(f32[4,8,8,1024]{3,2,1,0:T(8,128)S(1)} %bitcast_add_fusion.2), channel_id=1, source_target_pairs={{0,8},{4,12},{8,16},{12,20},{16,24},{20,28},{24,0},{28,4},{32,40},... | collective-permute-start | bytes 3145736 | tf_op jit(solution)/shard_map/ppermute | solution.py:43
  358.2 6.6 %collective-permute-start.4 = (f32[4,8,1024]{2,1,0:T(8,128)}, f32[4,8,1024]{2,1,0:T(8,128)}, u32[]{:S(2)}, u32[]{:S(2)}) collective-permute-start(f32[4,8,1024]{2,1,0:T(8,128)} %dynamic-slice_bitcast_fusion.2), channel_id=1, source_target_pairs={{0,32},{4,36},{8,40},{12,44},{16,48},{20,52},{24,56},{28,60},{32,6... | collective-permute-start | bytes 393224 | tf_op jit(solution)/shard_map/ppermute | solution.py:43
  366.4 8.9 %collective-permute-start.5 = (f32[4,8,1024]{2,1,0:T(8,128)}, f32[4,8,1024]{2,1,0:T(8,128)}, u32[]{:S(2)}, u32[]{:S(2)}) collective-permute-start(f32[4,8,1024]{2,1,0:T(8,128)} %bitcast_add_fusion.10), channel_id=1, source_target_pairs={{0,32},{4,36},{8,40},{12,44},{16,48},{20,52},{24,56},{28,60},{32,6... | collective-permute-start | bytes 393224 | tf_op jit(solution)/shard_map/ppermute | solution.py:43
  372.0 5.4 %copy-start.18 = (f32[256]{0:T(256)S(1)}, f32[256]{0:T(256)}, u32[]{:S(2)}) copy-start(f32[256]{0:T(256)} %copy-done.17) | copy-start | bytes 3076
  372.0 5.6 %copy-start.19 = (f32[4,256]{1,0:T(4,128)S(1)}, f32[4,256]{1,0:T(4,128)}, u32[]{:S(2)}) copy-start(f32[4,256]{1,0:T(4,128)} %get-tuple-element.58) | copy-start | bytes 12292
  372.0 5.6 %copy-start.24 = (f32[1024]{0:T(1024)S(1)}, f32[1024]{0:T(1024)}, u32[]{:S(2)}) copy-start(f32[1024]{0:T(1024)} %get-tuple-element.75) | copy-start | bytes 12292
  372.0 5.4 %copy-start.10 = (bf16[256,1024]{1,0:T(8,128)(2,1)S(1)}, bf16[256,1024]{1,0:T(8,128)(2,1)}, u32[]{:S(2)}) copy-start(bf16[256,1024]{1,0:T(8,128)(2,1)} %get-tuple-element.53) | copy-start | bytes 1572868
  376.1 11.2 %collective-permute-start.6 = (f32[4,8,1024]{2,1,0:T(8,128)S(1)}, f32[4,8,1024]{2,1,0:T(8,128)}, u32[]{:S(2)}, u32[]{:S(2)}) collective-permute-start(f32[4,8,1024]{2,1,0:T(8,128)S(1)} %bitcast_add_fusion.9), channel_id=1, source_target_pairs={{0,32},{4,36},{8,40},{12,44},{16,48},{20,52},{24,56},{28,60},{32,6... | collective-permute-start | bytes 393224 | tf_op jit(solution)/shard_map/ppermute | solution.py:43
  378.9 48.5 %all-to-all-start.8 = ((f32[64,3,1024]{2,1,0:T(4,128)}), f32[64,3,1024]{2,1,0:T(4,128)}, u32[]{:S(2)}, u32[]{:S(2)}) async-start(f32[64,3,1024]{2,1,0:T(4,128)} %broadcast_in_dim.20), calls=%async_computation.8 | async-start | bytes 2097152 | tf_op jit(solution)/shard_map/all_to_all | solution.py:26
  388.3 27.8 %collective-permute-start.7 = (f32[4,8,1024]{2,1,0:T(8,128)S(1)}, f32[4,8,1024]{2,1,0:T(8,128)S(1)}, u32[]{:S(2)}, u32[]{:S(2)}) collective-permute-start(f32[4,8,1024]{2,1,0:T(8,128)S(1)} %bitcast_add_fusion.8), channel_id=1, source_target_pairs={{0,32},{4,36},{8,40},{12,44},{16,48},{20,52},{24,56},{28,60},{32,6... | collective-permute-start | bytes 393224 | tf_op jit(solution)/shard_map/ppermute | solution.py:43
  389.9 26.4 %copy-start.23 = (f32[4,512]{1,0:T(4,128)S(1)}, f32[4,512]{1,0:T(4,128)}, u32[]{:S(2)}) copy-start(f32[4,512]{1,0:T(4,128)} %param.14) | copy-start | bytes 24580
  389.9 32.8 %copy-start.3 = (f32[4,512,256]{1,2,0:T(8,128)S(1)}, f32[4,512,256]{1,2,0:T(8,128)}, u32[]{:S(2)}) copy-start(f32[4,512,256]{1,2,0:T(8,128)} %copy.121) | copy-start | bytes 6291460
  416.2 6.4 %collective-permute-start.8 = (f32[4,8,1024]{2,1,0:T(8,128)S(1)}, f32[4,8,1024]{2,1,0:T(8,128)S(1)}, u32[]{:S(2)}, u32[]{:S(2)}) collective-permute-start(f32[4,8,1024]{2,1,0:T(8,128)S(1)} %bitcast_add_fusion.7), channel_id=1, source_target_pairs={{0,32},{4,36},{8,40},{12,44},{16,48},{20,52},{24,56},{28,60},{32,6... | collective-permute-start | bytes 393224 | tf_op jit(solution)/shard_map/ppermute | solution.py:43
  422.6 6.9 %collective-permute-start.9 = (f32[4,8,1024]{2,1,0:T(8,128)S(1)}, f32[4,8,1024]{2,1,0:T(8,128)}, u32[]{:S(2)}, u32[]{:S(2)}) collective-permute-start(f32[4,8,1024]{2,1,0:T(8,128)S(1)} %bitcast_add_fusion.6), channel_id=1, source_target_pairs={{0,32},{4,36},{8,40},{12,44},{16,48},{20,52},{24,56},{28,60},{32,6... | collective-permute-start | bytes 393224 | tf_op jit(solution)/shard_map/ppermute | solution.py:43
  424.5 5.9 %copy-start.15 = (f32[1024]{0:T(1024)S(1)}, f32[1024]{0:T(1024)}, u32[]{:S(2)}) copy-start(f32[1024]{0:T(1024)} %param.25) | copy-start | bytes 12292
  430.4 6.3 %collective-permute-start.10 = (f32[4,8,1024]{2,1,0:T(8,128)S(1)}, f32[4,8,1024]{2,1,0:T(8,128)S(1)}, u32[]{:S(2)}, u32[]{:S(2)}) collective-permute-start(f32[4,8,1024]{2,1,0:T(8,128)S(1)} %bitcast_add_fusion.5), channel_id=1, source_target_pairs={{0,32},{4,36},{8,40},{12,44},{16,48},{20,52},{24,56},{28,60},{32,6... | collective-permute-start | bytes 393224 | tf_op jit(solution)/shard_map/ppermute | solution.py:43

commit v8 on v7

--- a/solution.py
+++ b/solution.py
@@ -30,7 +30,7 @@
     return copy_for_each(array, axis).sum(axis=0)
 
 
-def ring_sum_scatter(blocks, axis, stride):
+def ring_sum_scatter(blocks, axis, stride, wire):
     size = blocks.shape[0]
     peers = lax.axis_size(axis)
     pos = (lax.axis_index(axis) // stride) % size
@@ -40,18 +40,28 @@
     ]
     carry = blocks[(pos + size - 1) % size]
     for step in range(size - 1):
-        carry = lax.ppermute(carry, axis, ahead) + blocks[(pos + 2 * size - step - 2) % size]
+        arrived = lax.ppermute(carry.astype(wire), axis, ahead).astype(carry.dtype)
+        carry = arrived + blocks[(pos + 2 * size - step - 2) % size]
     return carry
 
-def tree_sum_scatter(array, axis, dim, splits):
+def tree_sum_scatter(array, axis, dim, splits, wires):
     lead = array.shape[:dim]
     parts = array.reshape(*lead, *splits, array.shape[dim] // np.prod(splits), *array.shape[dim + 1:])
     stride = 1
     for level in reversed(range(len(splits))):
         parts = jnp.moveaxis(parts, dim + level, 0)
-        parts = ring_sum_scatter(parts, axis, stride)
+        parts = ring_sum_scatter(parts, axis, stride, wires[level])
         stride *= splits[level]
     return parts
+
+def butterfly_sum(array, axis):
+    peers = lax.axis_size(axis)
+    step = 1
+    while step < peers:
+        array = array + lax.ppermute(array, axis, [(i, i ^ step) for i in range(peers)])
+        step *= 2
+    return array
+
 
 def side_by_side(arrays, axis, dim, along):
     widths = [a.shape[along] for a in arrays]
@@ -232,8 +242,9 @@
         grads_u[layer] = grad_u_layer
         grads_v[layer] = down_factor_gradient
     both = jnp.concatenate((jnp.stack(grads_u), jnp.stack(grads_v)), axis=0)
-    grad_u, grad_v = jnp.split(tree_sum_scatter(both, "dp", 1, splits), 2, axis=0)
-    grad_small = over_copies(jnp.stack(bias_grads + [head_grad]), "dp")
+    wires = [jnp.float32] + [jnp.bfloat16] * (len(splits) - 1)
+    grad_u, grad_v = jnp.split(tree_sum_scatter(both, "dp", 1, splits, wires), 2, axis=0)
+    grad_small = butterfly_sum(jnp.stack(bias_grads + [head_grad]), "dp")
     grad_pooled = (upstream + to_start).astype(jnp.bfloat16)
     return (new_table, new_accum, grad_u, grad_v, grad_small, grad_pooled)
 

time: 440 us -> 392 us (0.89)
  waiting for transfers between devices: 192 us -> 149 us
    ppermute x11 -> x17, waiting for transfers between devices: 113 us -> 72.3 us  [the longest x11 71.8 us: ring_sum_scatter(): arrived = lax.ppermute(carry.astype(wire), axis, ahead).astype(carry.dtype)]
    ppermute x11 -> x17, starting transfers between devices: 8.86 us -> 17.9 us  [the longest x11 9.16 us: ring_sum_scatter(): arrived = lax.ppermute(carry.astype(wire), axis, ahead).astype(carry.dtype)]
    all_to_all x2 -> x1, starting transfers between devices: 14.3 us -> 5.87 us  [copy_for_each(): return lax.all_to_all(copies, axis, split_axis=0, concat_axis=0, tiled=True)]
    add x11 -> x15, other arithmetic: 13.8 us -> 10.4 us  [the longest x9 7.64 us: ring_sum_scatter(): carry = arrived + blocks[(pos + 2 * size - step - 2) % size]]
    unnamed x70 -> x64, local copies, waits for them, and re-layouts: 29.3 us -> 29.8 us
  transfers between devices with their start and end apart: 18 -> 23, of which waited for: 12 -> 14; matrix products, arithmetic and copies ran while one was open for 12% -> 14% of each run, Pallas kernels for 0% -> 0%
where the time goes in v8:
time: 392 us; the launch traced here: 389 us
  waiting for transfers between devices  149 us (38%)
  blocking collectives  75.5 us (19%)
  starting transfers between devices  53.4 us (14%)
  local copies, waits for them, and re-layouts  47.8 us (12%)
  matrix products  36.1 us (9%)
  other arithmetic  26.1 us (7%)
    ppermute x11, waiting for transfers between devices, ring_sum_scatter(): arrived = lax.ppermute(carry.astype(wire), axis, ahead).astype(carry.dtype)  71.8 us
    all_to_all x1, waiting for transfers between devices, local(): lax.all_to_all(served.reshape(local_feats, peers, look_cap, width), 'dp',...  50.3 us
    unnamed x64, local copies, waits for them, and re-layouts  29.8 us
    all_gather x2, blocking collectives, cross_down(): return lax.all_gather(share.astype(jnp.bfloat16), 'mp', axis=0, tiled=True)  23.4 us
    all_to_all x1, blocking collectives, local(): lax.all_to_all(wanted.reshape(local_feats, peers, look_cap), 'dp', split_...  22.8 us
    all_to_all x1, blocking collectives, copy_for_each(): return lax.all_to_all(copies, axis, split_axis=0, concat_axis=0, tiled=True)  20 us
    all_to_all x2, waiting for transfers between devices, sum_at_owner(): lax.all_to_all(parts, axis, split_axis=0, concat_axis=0, tiled=True)  13.7 us
    all_to_all x2, starting transfers between devices, sum_at_owner(): lax.all_to_all(parts, axis, split_axis=0, concat_axis=0, tiled=True)  10.4 us
  transfers between devices with their start and end apart: 23, of which 14 were waited for; matrix products, arithmetic and copies ran while one was open for 14% of the time, Pallas kernels for 0%

profile of v8, /device:TPU:8, one launch (start us, length us, event | category | flops | bytes accessed | tf_op | source)
XLA Modules:
  0.0 389.2 jit_solution(252968513132994903)
XLA Ops:
  4.0 8.1 %scatter_custom_fusion.1 = s32[4096]{0:T(1024)S(1)} fusion(s32[2048]{0:T(1024)S(1)} %bitcast.171, s32[2048]{0:T(1024)S(1)} %bitcast.173, s32[]{:T(128)} %constant.180.clone.1), kind=kCustom, calls=%fused_computation.122 | custom fusion | bytes 16388
  12.3 22.8 %all_to_all.40 = s32[4,64,16]{2,0,1:T(4,128)S(1)} all-to-all(s32[4,64,16]{2,0,1:T(4,128)S(1)} %copy.92), channel_id=1, replica_groups=mesh['dp'=64,'mp'=4] {'dp'}, dimensions={1} | all-to-all | bytes 32768 | tf_op jit(solution)/shard_map/all_to_all | solution.py:179
  35.2 3.7 fusion.15
  40.5 5.6 %all-to-all-start.3 = ((bf16[4,64,16,256]{3,2,0,1:T(8,128)(2,1)}), bf16[4,64,16,256]{3,2,0,1:T(8,128)(2,1)}, u32[]{:S(2)}, u32[]{:S(2)}) async-start(bf16[4,64,16,256]{3,2,0,1:T(8,128)(2,1)} %copy.94), calls=%async_computation.3 | async-start | bytes 4194304 | tf_op jit(solution)/shard_map/all_to_all | solution.py:189
  46.9 50.3 %all-to-all-done.3 = bf16[4,64,16,256]{3,2,0,1:T(8,128)(2,1)} async-done(((bf16[4,64,16,256]{3,2,0,1:T(8,128)(2,1)}), bf16[4,64,16,256]{3,2,0,1:T(8,128)(2,1)}, u32[]{:S(2)}, u32[]{:S(2)}) %all-to-all-start.3) | async-done | bytes 2097184 | tf_op jit(solution)/shard_map/all_to_all | solution.py:189
  99.0 2.1 fusion.18
  101.8 2.5 fusion.41
  104.3 4.9 %all-to-all-start.4 = ((f32[4,64,512]{2,1,0:T(8,128)}), f32[4,64,512]{2,1,0:T(8,128)S(1)}, u32[]{:S(2)}, u32[]{:S(2)}) async-start(f32[4,64,512]{2,1,0:T(8,128)} %fusion.41), calls=%async_computation.4 | async-start | bytes 1048576 | tf_op jit(solution)/shard_map/all_to_all | solution.py:20
  109.4 6.4 %all-to-all-done.4 = f32[4,64,512]{2,1,0:T(8,128)S(1)} async-done(((f32[4,64,512]{2,1,0:T(8,128)}), f32[4,64,512]{2,1,0:T(8,128)S(1)}, u32[]{:S(2)}, u32[]{:S(2)}) %all-to-all-start.4) | async-done | bytes 524320 | tf_op jit(solution)/shard_map/all_to_all | solution.py:20
  115.9 11.8 %all_gather.6 = bf16[256,512]{1,0:T(8,128)(2,1)S(1)} all-gather(bf16[64,512]{1,0:T(8,128)(2,1)S(1)} %reduce_sum.102), channel_id=1, replica_groups=mesh['dp'=64,'mp'=4] {'mp'}, dimensions={0}, use_global_device_ids=true | all-gather | bytes 327680 | tf_op jit(solution)/shard_map/all_gather | solution.py:100
  127.6 2.8 fusion.27
  131.7 5.5 %all-to-all-start.5 = ((f32[4,64,512]{2,1,0:T(8,128)}), f32[4,64,512]{2,1,0:T(8,128)S(1)}, u32[]{:S(2)}, u32[]{:S(2)}) async-start(f32[4,64,512]{2,1,0:T(8,128)} %fusion.35), calls=%async_computation.5 | async-start | bytes 1048576 | tf_op jit(solution)/shard_map/all_to_all | solution.py:20
  137.2 7.3 %all-to-all-done.5 = f32[4,64,512]{2,1,0:T(8,128)S(1)} async-done(((f32[4,64,512]{2,1,0:T(8,128)}), f32[4,64,512]{2,1,0:T(8,128)S(1)}, u32[]{:S(2)}, u32[]{:S(2)}) %all-to-all-start.5) | async-done | bytes 524320 | tf_op jit(solution)/shard_map/all_to_all | solution.py:20
  144.6 11.6 %all_gather.7 = bf16[256,512]{1,0:T(8,128)(2,1)S(1)} all-gather(bf16[64,512]{1,0:T(8,128)(2,1)S(1)} %reduce_sum.103), channel_id=1, replica_groups=mesh['dp'=64,'mp'=4] {'mp'}, dimensions={0}, use_global_device_ids=true | all-gather | bytes 327680 | tf_op jit(solution)/shard_map/all_gather | solution.py:100
  156.2 2.9 fusion.24
  159.0 9.3 %psum.7 = f32[256]{0:T(256)S(1)} all-reduce(f32[256]{0:T(256)S(1)} %get-tuple-element.40), channel_id=1, replica_groups=mesh['dp'=64,'mp'=4] {'mp'}, use_global_device_ids=true, to_apply=%region_8.0 | all-reduce | flops 256 | bytes 2048 | tf_op jit(solution)/shard_map/psum | solution.py:221
  171.6 20.0 %all_to_all.41 = f32[4,256,512]{2,1,0:T(8,128)} all-to-all(f32[4,256,512]{2,1,0:T(8,128)S(1)} %broadcast_in_dim.16), channel_id=1, replica_groups=mesh['dp'=64,'mp'=4] {'mp'}, dimensions={0} | all-to-all | bytes 4194304 | tf_op jit(solution)/shard_map/all_to_all | solution.py:26
  191.5 2.6 reduce_sum.105
  194.1 1.9 fusion.61
  198.2 5.9 %all-to-all-start.7 = ((f32[4,256,512]{2,1,0:T(8,128)}), f32[4,256,512]{2,1,0:T(8,128)}, u32[]{:S(2)}, u32[]{:S(2)}) async-start(f32[4,256,512]{2,1,0:T(8,128)} %broadcast_in_dim.17), calls=%async_computation.7 | async-start | bytes 4194304 | tf_op jit(solution)/shard_map/all_to_all | solution.py:26
  204.9 3.0 convolution_bitcast_fusion.1
  211.5 7.7 %all-to-all-done.7 = f32[4,256,512]{2,1,0:T(8,128)} async-done(((f32[4,256,512]{2,1,0:T(8,128)}), f32[4,256,512]{2,1,0:T(8,128)}, u32[]{:S(2)}, u32[]{:S(2)}) %all-to-all-start.7) | async-done | bytes 2097184 | tf_op jit(solution)/shard_map/all_to_all | solution.py:26
  222.8 2.6 pad_maximum_fusion
  225.4 3.2 copy-done.1
  230.3 8.1 %scatter_custom_fusion = s32[4096]{0:T(1024)S(1)} fusion(s32[2048]{0:T(1024)S(1)} %bitcast.170, s32[2048]{0:T(1024)S(1)} %bitcast.172, s32[]{:T(128)} %constant.177.clone.1), kind=kCustom, calls=%fused_computation.124 | custom fusion | bytes 16388
  239.2 8.0 %all-to-all-start = ((s32[4,64,16]{2,0,1:T(4,128)}), s32[4,64,16]{2,0,1:T(4,128)S(1)}, u32[]{:S(2)}, u32[]{:S(2)}) async-start(s32[4,64,16]{2,0,1:T(4,128)} %copy.82), calls=%async_computation | async-start | bytes 262144 | tf_op jit(solution)/shard_map/all_to_all | solution.py:154
  247.2 2.8 fusion.16
  250.0 3.3 copy.84
  253.3 4.9 %all-to-all-done = s32[4,64,16]{2,0,1:T(4,128)S(1)} async-done(((s32[4,64,16]{2,0,1:T(4,128)}), s32[4,64,16]{2,0,1:T(4,128)S(1)}, u32[]{:S(2)}, u32[]{:S(2)}) %all-to-all-start) | async-done | bytes 16416 | tf_op jit(solution)/shard_map/all_to_all | solution.py:154
  258.2 5.6 %all-to-all-start.1 = ((bf16[4,64,16,256]{3,2,0,1:T(8,128)(2,1)}), bf16[4,64,16,256]{3,2,0,1:T(8,128)(2,1)}, u32[]{:S(2)}, u32[]{:S(2)}) async-start(bf16[4,64,16,256]{3,2,0,1:T(8,128)(2,1)} %copy.84), calls=%async_computation.1 | async-start | bytes 4194304 | tf_op jit(solution)/shard_map/all_to_all | solution.py:147
  263.9 3.6 bitcast_add_fusion
  267.5 1.9 copy-done.2
  271.1 22.1 %collective-permute-done.1 = bf16[4,8,8,1024]{3,2,1,0:T(8,128)(2,1)S(1)} collective-permute-done((bf16[4,8,8,1024]{3,2,1,0:T(8,128)(2,1)S(1)}, bf16[4,8,8,1024]{3,2,1,0:T(8,128)(2,1)S(1)}, u32[]{:S(2)}, u32[]{:S(2)}) %collective-permute-start.1) | collective-permute-done | bytes 524320 | tf_op jit(solution)/shard_map/ppermute | solution.py:43
  294.6 2.3 collective-permute-start.2
  296.9 19.0 %collective-permute-done.2 = bf16[4,8,8,1024]{3,2,1,0:T(8,128)(2,1)S(1)} collective-permute-done((bf16[4,8,8,1024]{3,2,1,0:T(8,128)(2,1)S(1)}, bf16[4,8,8,1024]{3,2,1,0:T(8,128)(2,1)S(1)}, u32[]{:S(2)}, u32[]{:S(2)}) %collective-permute-start.2) | collective-permute-done | bytes 524320 | tf_op jit(solution)/shard_map/ppermute | solution.py:43
  317.5 14.3 %collective-permute-done.3 = bf16[4,8,8,1024]{3,2,1,0:T(8,128)(2,1)} collective-permute-done((bf16[4,8,8,1024]{3,2,1,0:T(8,128)(2,1)S(1)}, bf16[4,8,8,1024]{3,2,1,0:T(8,128)(2,1)}, u32[]{:S(2)}, u32[]{:S(2)}) %collective-permute-start.3) | collective-permute-done | bytes 524320 | tf_op jit(solution)/shard_map/ppermute | solution.py:43
  333.3 2.1 collective-permute-start.4
  336.8 4.0 %collective-permute-done.4 = f32[4,8,1024]{2,1,0:T(8,128)S(1)} collective-permute-done((f32[4,8,1024]{2,1,0:T(8,128)S(1)}, f32[4,8,1024]{2,1,0:T(8,128)S(1)}, u32[]{:S(2)}, u32[]{:S(2)}) %collective-permute-start.4) | collective-permute-done | bytes 131104 | tf_op jit(solution)/shard_map/ppermute | solution.py:43
  341.0 6.0 %collective-permute-done.5 = f32[4,8,1024]{2,1,0:T(8,128)S(1)} collective-permute-done((f32[4,8,1024]{2,1,0:T(8,128)S(1)}, f32[4,8,1024]{2,1,0:T(8,128)S(1)}, u32[]{:S(2)}, u32[]{:S(2)}) %collective-permute-start.5) | collective-permute-done | bytes 131104 | tf_op jit(solution)/shard_map/ppermute | solution.py:43
  348.6 2.9 copy.87
  356.6 2.1 collective-permute-start.7
  358.7 2.9 multiply_reduce_fusion
  361.6 4.7 %collective-permute-start.15 = (f32[3,1024]{1,0:T(4,128)S(1)}, f32[3,1024]{1,0:T(4,128)S(1)}, u32[]{:S(2)}, u32[]{:S(2)}) collective-permute-start(f32[3,1024]{1,0:T(4,128)S(1)} %add.355), channel_id=1, source_target_pairs={{0,64},{4,68},{8,72},{12,76},{16,80},{20,84},{24,88},{28,92},{32,9... | collective-permute-start | bytes 36872 | tf_op jit(solution)/shard_map/ppermute | solution.py:61
  368.0 3.8 collective-permute-start.16
  371.8 2.0 collective-permute-done.8
  375.7 2.9 copy.103
  382.4 3.2 fusion.21
  385.5 3.0 collective-permute-done.10
  (153 shorter events, 48.0 us)
Async XLA Ops:
  0.6 246.6 %copy-start = (bf16[4,512,256]{2,1,0:T(8,128)(2,1)S(1)}, bf16[4,512,256]{2,1,0:T(8,128)(2,1)}, u32[]{:S(2)}) copy-start(bf16[4,512,256]{2,1,0:T(8,128)(2,1)} %param.15) | copy-start | bytes 3145732
  0.6 3.0 copy-start.25
  0.7 3.1 copy-start.24
  0.7 2.9 copy-start.15
  0.7 3.3 copy-start.18
  40.5 56.8 %all-to-all-start.3 = ((bf16[4,64,16,256]{3,2,0,1:T(8,128)(2,1)}), bf16[4,64,16,256]{3,2,0,1:T(8,128)(2,1)}, u32[]{:S(2)}, u32[]{:S(2)}) async-start(bf16[4,64,16,256]{3,2,0,1:T(8,128)(2,1)} %copy.94), calls=%async_computation.3 | async-start | bytes 4194304 | tf_op jit(solution)/shard_map/all_to_all | solution.py:189
  101.4 7.8 %copy-start.19 = (f32[2,1024]{1,0:T(2,128)S(1)}, f32[2,1024]{1,0:T(2,128)}, u32[]{:S(2)}) copy-start(f32[2,1024]{1,0:T(2,128)} %param.24) | copy-start | bytes 24580
  104.3 11.5 %all-to-all-start.4 = ((f32[4,64,512]{2,1,0:T(8,128)}), f32[4,64,512]{2,1,0:T(8,128)S(1)}, u32[]{:S(2)}, u32[]{:S(2)}) async-start(f32[4,64,512]{2,1,0:T(8,128)} %fusion.41), calls=%async_computation.4 | async-start | bytes 1048576 | tf_op jit(solution)/shard_map/all_to_all | solution.py:20
  115.8 14.6 %copy-start.12 = (bf16[2,512,1024]{2,1,0:T(8,128)(2,1)S(1)}, bf16[2,512,1024]{2,1,0:T(8,128)(2,1)}, u32[]{:S(2)}) copy-start(bf16[2,512,1024]{2,1,0:T(8,128)(2,1)} %param.23) | copy-start | bytes 6291460
  127.6 4.1 %copy-start.8 = (bf16[256,512]{1,0:T(8,128)(2,1)}, bf16[256,512]{1,0:T(8,128)(2,1)S(1)}, u32[]{:S(2)}) copy-start(bf16[256,512]{1,0:T(8,128)(2,1)S(1)} %all_gather.6) | copy-start | bytes 786436
  130.4 25.8 %copy-start.6 = (bf16[256,1024]{1,0:T(8,128)(2,1)}, bf16[256,1024]{1,0:T(8,128)(2,1)S(1)}, u32[]{:S(2)}) copy-start(bf16[256,1024]{1,0:T(8,128)(2,1)S(1)} %get-tuple-element.60) | copy-start | bytes 1572868
  130.4 6.8 %copy-start.14 = (f32[1024]{0:T(1024)S(1)}, f32[1024]{0:T(1024)}, u32[]{:S(2)}) copy-start(f32[1024]{0:T(1024)} %param.25) | copy-start | bytes 12292
  131.7 12.8 %all-to-all-start.5 = ((f32[4,64,512]{2,1,0:T(8,128)}), f32[4,64,512]{2,1,0:T(8,128)S(1)}, u32[]{:S(2)}, u32[]{:S(2)}) async-start(f32[4,64,512]{2,1,0:T(8,128)} %fusion.35), calls=%async_computation.5 | async-start | bytes 1048576 | tf_op jit(solution)/shard_map/all_to_all | solution.py:20
  144.6 23.8 %copy-start.23 = (s32[256]{0:T(256)S(1)}, s32[256]{0:T(256)}, u32[]{:S(2)}) copy-start(s32[256]{0:T(256)} %param.21) | copy-start | bytes 3076
  168.4 167.0 %copy-start.16 = (f32[256]{0:T(256)}, f32[256]{0:T(256)S(1)}, u32[]{:S(2)}) copy-start(f32[256]{0:T(256)S(1)} %fusion.76) | copy-start | bytes 3076
  169.4 2.2 copy-start.10
  194.1 2.0 copy-start.5
  196.1 144.8 %copy-start.13 = (f32[1024]{0:T(1024)}, f32[1024]{0:T(1024)S(1)}, u32[]{:S(2)}) copy-start(f32[1024]{0:T(1024)S(1)} %get-tuple-element.63) | copy-start | bytes 12292
  198.2 21.0 %all-to-all-start.7 = ((f32[4,256,512]{2,1,0:T(8,128)}), f32[4,256,512]{2,1,0:T(8,128)}, u32[]{:S(2)}, u32[]{:S(2)}) async-start(f32[4,256,512]{2,1,0:T(8,128)} %broadcast_in_dim.17), calls=%async_computation.7 | async-start | bytes 4194304 | tf_op jit(solution)/shard_map/all_to_all | solution.py:26
  204.9 3.0 copy-start.7
  204.9 3.0 copy-start.11
  207.9 1.8 copy-start.9
  221.2 1.6 copy-start.4
  225.4 3.2 copy-start.1
  228.7 1.6 copy-start.20
  230.3 33.6 %collective-permute-start = (bf16[4,8,4,8,1024]{4,3,2,1,0:T(8,128)(2,1)}, bf16[4,8,4,8,1024]{4,3,2,1,0:T(8,128)(2,1)}, u32[]{:S(2)}, u32[]{:S(2)}) collective-permute-start(bf16[4,8,4,8,1024]{4,3,2,1,0:T(8,128)(2,1)} %fusion.12), channel_id=1, source_target_pairs={{0,4},{4,0},{8,12},{12,8},{16,20},{20,16},{24,28},{28,24},{32,36},... | collective-permute-start | bytes 6291464 | tf_op jit(solution)/shard_map/ppermute | solution.py:43
  239.2 19.0 %all-to-all-start = ((s32[4,64,16]{2,0,1:T(4,128)}), s32[4,64,16]{2,0,1:T(4,128)S(1)}, u32[]{:S(2)}, u32[]{:S(2)}) async-start(s32[4,64,16]{2,0,1:T(4,128)} %copy.82), calls=%async_computation | async-start | bytes 262144 | tf_op jit(solution)/shard_map/all_to_all | solution.py:154
  258.2 94.9 %all-to-all-start.1 = ((bf16[4,64,16,256]{3,2,0,1:T(8,128)(2,1)}), bf16[4,64,16,256]{3,2,0,1:T(8,128)(2,1)}, u32[]{:S(2)}, u32[]{:S(2)}) async-start(bf16[4,64,16,256]{3,2,0,1:T(8,128)(2,1)} %copy.84), calls=%async_computation.1 | async-start | bytes 4194304 | tf_op jit(solution)/shard_map/all_to_all | solution.py:147
  267.5 2.0 copy-start.2
  269.5 23.7 %collective-permute-start.1 = (bf16[4,8,8,1024]{3,2,1,0:T(8,128)(2,1)S(1)}, bf16[4,8,8,1024]{3,2,1,0:T(8,128)(2,1)S(1)}, u32[]{:S(2)}, u32[]{:S(2)}) collective-permute-start(bf16[4,8,8,1024]{3,2,1,0:T(8,128)(2,1)S(1)} %fusion.63), channel_id=1, source_target_pairs={{0,8},{4,12},{8,16},{12,20},{16,24},{20,28},{24,0},{28,4},{32,40},... | collective-permute-start | bytes 1572872 | tf_op jit(solution)/shard_map/ppermute | solution.py:43
  294.6 21.3 %collective-permute-start.2 = (bf16[4,8,8,1024]{3,2,1,0:T(8,128)(2,1)S(1)}, bf16[4,8,8,1024]{3,2,1,0:T(8,128)(2,1)S(1)}, u32[]{:S(2)}, u32[]{:S(2)}) collective-permute-start(bf16[4,8,8,1024]{3,2,1,0:T(8,128)(2,1)S(1)} %fusion.31), channel_id=1, source_target_pairs={{0,8},{4,12},{8,16},{12,20},{16,24},{20,28},{24,0},{28,4},{32,40},... | collective-permute-start | bytes 1572872 | tf_op jit(solution)/shard_map/ppermute | solution.py:43
  317.3 19.3 %copy-start.17 = (f32[4,256]{1,0:T(4,128)S(1)}, f32[4,256]{1,0:T(4,128)}, u32[]{:S(2)}) copy-start(f32[4,256]{1,0:T(4,128)} %get-tuple-element.46) | copy-start | bytes 12292
  317.3 14.4 %collective-permute-start.3 = (bf16[4,8,8,1024]{3,2,1,0:T(8,128)(2,1)S(1)}, bf16[4,8,8,1024]{3,2,1,0:T(8,128)(2,1)}, u32[]{:S(2)}, u32[]{:S(2)}) collective-permute-start(bf16[4,8,8,1024]{3,2,1,0:T(8,128)(2,1)S(1)} %fusion.30), channel_id=1, source_target_pairs={{0,8},{4,12},{8,16},{12,20},{16,24},{20,28},{24,0},{28,4},{32,40},... | collective-permute-start | bytes 1572872 | tf_op jit(solution)/shard_map/ppermute | solution.py:43
  333.3 7.5 %collective-permute-start.4 = (f32[4,8,1024]{2,1,0:T(8,128)S(1)}, f32[4,8,1024]{2,1,0:T(8,128)S(1)}, u32[]{:S(2)}, u32[]{:S(2)}) collective-permute-start(f32[4,8,1024]{2,1,0:T(8,128)S(1)} %dynamic-slice_bitcast_fusion), channel_id=1, source_target_pairs={{0,32},{4,36},{8,40},{12,44},{16,48},{20,52},{24,56},{28,60},{32,6... | collective-permute-start | bytes 393224 | tf_op jit(solution)/shard_map/ppermute | solution.py:43
  336.7 4.2 %collective-permute-start.11 = (f32[3,1024]{1,0:T(4,128)S(1)}, f32[3,1024]{1,0:T(4,128)S(1)}, u32[]{:S(2)}, u32[]{:S(2)}) collective-permute-start(f32[3,1024]{1,0:T(4,128)S(1)} %pad_maximum_fusion.1), channel_id=1, source_target_pairs={{0,4},{4,0},{8,12},{12,8},{16,20},{20,16},{24,28},{28,24},{32,36},... | collective-permute-start | bytes 36872 | tf_op jit(solution)/shard_map/ppermute | solution.py:61
  340.8 6.3 %collective-permute-start.5 = (f32[4,8,1024]{2,1,0:T(8,128)S(1)}, f32[4,8,1024]{2,1,0:T(8,128)S(1)}, u32[]{:S(2)}, u32[]{:S(2)}) collective-permute-start(f32[4,8,1024]{2,1,0:T(8,128)S(1)} %bitcast_add_fusion.10), channel_id=1, source_target_pairs={{0,32},{4,36},{8,40},{12,44},{16,48},{20,52},{24,56},{28,60},{32,6... | collective-permute-start | bytes 393224 | tf_op jit(solution)/shard_map/ppermute | solution.py:43
  340.9 6.8 %collective-permute-start.12 = (f32[3,1024]{1,0:T(4,128)S(1)}, f32[3,1024]{1,0:T(4,128)S(1)}, u32[]{:S(2)}, u32[]{:S(2)}) collective-permute-start(f32[3,1024]{1,0:T(4,128)S(1)} %fusion.78), channel_id=1, source_target_pairs={{0,8},{4,12},{8,0},{12,4},{16,24},{20,28},{24,16},{28,20},{32,40},... | collective-permute-start | bytes 36872 | tf_op jit(solution)/shard_map/ppermute | solution.py:61
  347.7 8.0 %collective-permute-start.6 = (f32[4,8,1024]{2,1,0:T(8,128)}, f32[4,8,1024]{2,1,0:T(8,128)}, u32[]{:S(2)}, u32[]{:S(2)}) collective-permute-start(f32[4,8,1024]{2,1,0:T(8,128)} %bitcast_add_fusion.9), channel_id=1, source_target_pairs={{0,32},{4,36},{8,40},{12,44},{16,48},{20,52},{24,56},{28,60},{32,6... | collective-permute-start | bytes 393224 | tf_op jit(solution)/shard_map/ppermute | solution.py:43
  348.4 6.5 %collective-permute-start.13 = (f32[3,1024]{1,0:T(4,128)S(1)}, f32[3,1024]{1,0:T(4,128)}, u32[]{:S(2)}, u32[]{:S(2)}) collective-permute-start(f32[3,1024]{1,0:T(4,128)S(1)} %fusion.105), channel_id=1, source_target_pairs={{0,16},{4,20},{8,24},{12,28},{16,0},{20,4},{24,8},{28,12},{32,48},... | collective-permute-start | bytes 36872 | tf_op jit(solution)/shard_map/ppermute | solution.py:61
  355.7 5.9 %collective-permute-start.14 = (f32[3,1024]{1,0:T(4,128)S(1)}, f32[3,1024]{1,0:T(4,128)S(1)}, u32[]{:S(2)}, u32[]{:S(2)}) collective-permute-start(f32[3,1024]{1,0:T(4,128)S(1)} %add.354), channel_id=1, source_target_pairs={{0,32},{4,36},{8,40},{12,44},{16,48},{20,52},{24,56},{28,60},{32,0... | collective-permute-start | bytes 36872 | tf_op jit(solution)/shard_map/ppermute | solution.py:61
  356.6 9.7 %collective-permute-start.7 = (f32[4,8,1024]{2,1,0:T(8,128)S(1)}, f32[4,8,1024]{2,1,0:T(8,128)S(1)}, u32[]{:S(2)}, u32[]{:S(2)}) collective-permute-start(f32[4,8,1024]{2,1,0:T(8,128)S(1)} %bitcast_add_fusion.8), channel_id=1, source_target_pairs={{0,32},{4,36},{8,40},{12,44},{16,48},{20,52},{24,56},{28,60},{32,6... | collective-permute-start | bytes 393224 | tf_op jit(solution)/shard_map/ppermute | solution.py:43
  358.7 8.3 %copy-start.21 = (f32[4,512]{1,0:T(4,128)S(1)}, f32[4,512]{1,0:T(4,128)}, u32[]{:S(2)}) copy-start(f32[4,512]{1,0:T(4,128)} %param.14) | copy-start | bytes 24580
  358.7 15.2 %copy-start.3 = (f32[4,512,256]{1,2,0:T(8,128)S(1)}, f32[4,512,256]{1,2,0:T(8,128)}, u32[]{:S(2)}) copy-start(f32[4,512,256]{1,2,0:T(8,128)} %copy.87) | copy-start | bytes 6291460
  361.6 6.4 %collective-permute-start.15 = (f32[3,1024]{1,0:T(4,128)S(1)}, f32[3,1024]{1,0:T(4,128)S(1)}, u32[]{:S(2)}, u32[]{:S(2)}) collective-permute-start(f32[3,1024]{1,0:T(4,128)S(1)} %add.355), channel_id=1, source_target_pairs={{0,64},{4,68},{8,72},{12,76},{16,80},{20,84},{24,88},{28,92},{32,9... | collective-permute-start | bytes 36872 | tf_op jit(solution)/shard_map/ppermute | solution.py:61
  366.3 7.4 %collective-permute-start.8 = (f32[4,8,1024]{2,1,0:T(8,128)S(1)}, f32[4,8,1024]{2,1,0:T(8,128)S(1)}, u32[]{:S(2)}, u32[]{:S(2)}) collective-permute-start(f32[4,8,1024]{2,1,0:T(8,128)S(1)} %bitcast_add_fusion.7), channel_id=1, source_target_pairs={{0,32},{4,36},{8,40},{12,44},{16,48},{20,52},{24,56},{28,60},{32,6... | collective-permute-start | bytes 393224 | tf_op jit(solution)/shard_map/ppermute | solution.py:43
  368.0 10.6 %collective-permute-start.16 = (f32[3,1024]{1,0:T(4,128)S(1)}, f32[3,1024]{1,0:T(4,128)}, u32[]{:S(2)}, u32[]{:S(2)}) collective-permute-start(f32[3,1024]{1,0:T(4,128)S(1)} %add.356), channel_id=1, source_target_pairs={{0,128},{4,132},{8,136},{12,140},{16,144},{20,148},{24,152},{28,15... | collective-permute-start | bytes 36872 | tf_op jit(solution)/shard_map/ppermute | solution.py:61
  373.8 7.6 %collective-permute-start.9 = (f32[4,8,1024]{2,1,0:T(8,128)S(1)}, f32[4,8,1024]{2,1,0:T(8,128)}, u32[]{:S(2)}, u32[]{:S(2)}) collective-permute-start(f32[4,8,1024]{2,1,0:T(8,128)S(1)} %bitcast_add_fusion.6), channel_id=1, source_target_pairs={{0,32},{4,36},{8,40},{12,44},{16,48},{20,52},{24,56},{28,60},{32,6... | collective-permute-start | bytes 393224 | tf_op jit(solution)/shard_map/ppermute | solution.py:43
  382.3 6.3 %collective-permute-start.10 = (f32[4,8,1024]{2,1,0:T(8,128)S(1)}, f32[4,8,1024]{2,1,0:T(8,128)S(1)}, u32[]{:S(2)}, u32[]{:S(2)}) collective-permute-start(f32[4,8,1024]{2,1,0:T(8,128)S(1)} %bitcast_add_fusion.5), channel_id=1, source_target_pairs={{0,32},{4,36},{8,40},{12,44},{16,48},{20,52},{24,56},{28,60},{32,6... | collective-permute-start | bytes 393224 | tf_op jit(solution)/shard_map/ppermute | solution.py:43
  (1 other events, 0.8 us)

commit v9 on v8

--- a/solution.py
+++ b/solution.py
@@ -44,15 +44,31 @@
         carry = arrived + blocks[(pos + 2 * size - step - 2) % size]
     return carry
 
+def direct_sum_scatter(blocks, axis, stride, wire):
+    size = blocks.shape[0]
+    peers = lax.axis_size(axis)
+    pos = (lax.axis_index(axis) // stride) % size
+    total = blocks[pos]
+    for offset in range(1, size):
+        toward = [
+            (i, i + (((i // stride) % size + offset) % size - (i // stride) % size) * stride)
+            for i in range(peers)
+        ]
+        sent = blocks[(pos + offset) % size].astype(wire)
+        total = total + lax.ppermute(sent, axis, toward).astype(total.dtype)
+    return total
+
+
 def tree_sum_scatter(array, axis, dim, splits, wires):
     lead = array.shape[:dim]
     parts = array.reshape(*lead, *splits, array.shape[dim] // np.prod(splits), *array.shape[dim + 1:])
     stride = 1
     for level in reversed(range(len(splits))):
         parts = jnp.moveaxis(parts, dim + level, 0)
-        parts = ring_sum_scatter(parts, axis, stride, wires[level])
+        parts = direct_sum_scatter(parts, axis, stride, wires[level])
         stride *= splits[level]
     return parts
+
 
 def butterfly_sum(array, axis):
     peers = lax.axis_size(axis)

time: 392 us -> 379 us (0.967)
  blocking collectives: 75.5 us -> 55.4 us
  starting transfers between devices: 53.4 us -> 67.6 us
  other arithmetic: 26.1 us -> 18.3 us
    ppermute x11, waiting for transfers between devices: 71.8 us -> 25.7 us  [direct_sum_scatter(): total = total + lax.ppermute(sent, axis, toward).astype(total.dtype)]
    all_to_all x1 -> x2, waiting for transfers between devices: 7.67 us -> 28.6 us  [copy_for_each(): return lax.all_to_all(copies, axis, split_axis=0, concat_axis=0, tiled=True)]
    all_to_all x1 -> x0, blocking collectives: 20 us -> none  [copy_for_each(): return lax.all_to_all(copies, axis, split_axis=0, concat_axis=0, tiled=True)]
    all_to_all x1, waiting for transfers between devices: 0.01 us -> 18.5 us  [local(): lax.all_to_all(send_grads.reshape(local_feats, peers, grad_cap, width), '...]
    ppermute x11, starting transfers between devices: 9.16 us -> 19.6 us  [direct_sum_scatter(): total = total + lax.ppermute(sent, axis, toward).astype(total.dtype)]
    ppermute x6, waiting for transfers between devices: 0.49 us -> 9.95 us  [butterfly_sum(): lax.ppermute(array, axis, [(i, i ^ step) for i in range(peers)])]
    all_to_all x1 -> x2, starting transfers between devices: 5.87 us -> 12.1 us  [copy_for_each(): return lax.all_to_all(copies, axis, split_axis=0, concat_axis=0, tiled=True)]
    unnamed x64 -> x72, local copies, waits for them, and re-layouts: 29.8 us -> 28.1 us
  transfers between devices with their start and end apart: 23 -> 24, of which waited for: 14 -> 14; matrix products, arithmetic and copies ran while one was open for 14% -> 15% of each run, Pallas kernels for 0% -> 0%
where the time goes in v9:
time: 379 us; the launch traced here: 376 us
  waiting for transfers between devices  152 us (40%)
  starting transfers between devices  67.6 us (18%)
  blocking collectives  55.4 us (15%)
  local copies, waits for them, and re-layouts  46.4 us (12%)
  matrix products  35 us (9%)
  other arithmetic  18.3 us (5%)
    all_to_all x1, waiting for transfers between devices, local(): lax.all_to_all(served.reshape(local_feats, peers, look_cap, width), 'dp',...  50.3 us
    all_to_all x2, waiting for transfers between devices, copy_for_each(): return lax.all_to_all(copies, axis, split_axis=0, concat_axis=0, tiled=True)  28.6 us
    unnamed x72, local copies, waits for them, and re-layouts  28.1 us
    ppermute x11, waiting for transfers between devices, direct_sum_scatter(): total = total + lax.ppermute(sent, axis, toward).astype(total.dtype)  25.7 us
    all_gather x2, blocking collectives, cross_down(): return lax.all_gather(share.astype(jnp.bfloat16), 'mp', axis=0, tiled=True)  23.4 us
    all_to_all x1, blocking collectives, local(): lax.all_to_all(wanted.reshape(local_feats, peers, look_cap), 'dp', split_...  22.8 us
    ppermute x11, starting transfers between devices, direct_sum_scatter(): total = total + lax.ppermute(sent, axis, toward).astype(total.dtype)  19.6 us
    all_to_all x1, waiting for transfers between devices, local(): lax.all_to_all(send_grads.reshape(local_feats, peers, grad_cap, width), '...  18.5 us
  transfers between devices with their start and end apart: 24, of which 14 were waited for; matrix products, arithmetic and copies ran while one was open for 15% of the time, Pallas kernels for 0%

profile of v9, /device:TPU:8, one launch (start us, length us, event | category | flops | bytes accessed | tf_op | source)
XLA Modules:
  0.0 375.9 jit_solution(12657290858116445533)
XLA Ops:
  4.0 8.1 %scatter_custom_fusion.1 = s32[4096]{0:T(1024)S(1)} fusion(s32[2048]{0:T(1024)S(1)} %bitcast.191, s32[2048]{0:T(1024)S(1)} %bitcast.193, s32[]{:T(128)} %constant.128.clone.1), kind=kCustom, calls=%fused_computation.130 | custom fusion | bytes 16388
  12.3 22.8 %all_to_all.40 = s32[4,64,16]{2,0,1:T(4,128)S(1)} all-to-all(s32[4,64,16]{2,0,1:T(4,128)S(1)} %copy.100), channel_id=1, replica_groups=mesh['dp'=64,'mp'=4] {'dp'}, dimensions={1} | all-to-all | bytes 32768 | tf_op jit(solution)/shard_map/all_to_all | solution.py:195
  35.2 3.7 fusion.15
  40.5 5.6 %all-to-all-start.3 = ((bf16[4,64,16,256]{3,2,0,1:T(8,128)(2,1)}), bf16[4,64,16,256]{3,2,0,1:T(8,128)(2,1)}, u32[]{:S(2)}, u32[]{:S(2)}) async-start(bf16[4,64,16,256]{3,2,0,1:T(8,128)(2,1)} %copy.102), calls=%async_computation.3 | async-start | bytes 4194304 | tf_op jit(solution)/shard_map/all_to_all | solution.py:205
  46.9 50.3 %all-to-all-done.3 = bf16[4,64,16,256]{3,2,0,1:T(8,128)(2,1)} async-done(((bf16[4,64,16,256]{3,2,0,1:T(8,128)(2,1)}), bf16[4,64,16,256]{3,2,0,1:T(8,128)(2,1)}, u32[]{:S(2)}, u32[]{:S(2)}) %all-to-all-start.3) | async-done | bytes 2097184 | tf_op jit(solution)/shard_map/all_to_all | solution.py:205
  99.0 2.1 fusion.18
  101.8 2.5 fusion.41
  104.3 4.9 %all-to-all-start.4 = ((f32[4,64,512]{2,1,0:T(8,128)}), f32[4,64,512]{2,1,0:T(8,128)S(1)}, u32[]{:S(2)}, u32[]{:S(2)}) async-start(f32[4,64,512]{2,1,0:T(8,128)} %fusion.41), calls=%async_computation.4 | async-start | bytes 1048576 | tf_op jit(solution)/shard_map/all_to_all | solution.py:20
  109.4 6.4 %all-to-all-done.4 = f32[4,64,512]{2,1,0:T(8,128)S(1)} async-done(((f32[4,64,512]{2,1,0:T(8,128)}), f32[4,64,512]{2,1,0:T(8,128)S(1)}, u32[]{:S(2)}, u32[]{:S(2)}) %all-to-all-start.4) | async-done | bytes 524320 | tf_op jit(solution)/shard_map/all_to_all | solution.py:20
  115.9 11.8 %all_gather.6 = bf16[256,512]{1,0:T(8,128)(2,1)S(1)} all-gather(bf16[64,512]{1,0:T(8,128)(2,1)S(1)} %reduce_sum.102), channel_id=1, replica_groups=mesh['dp'=64,'mp'=4] {'mp'}, dimensions={0}, use_global_device_ids=true | all-gather | bytes 327680 | tf_op jit(solution)/shard_map/all_gather | solution.py:116
  127.6 2.8 fusion.27
  131.7 5.5 %all-to-all-start.5 = ((f32[4,64,512]{2,1,0:T(8,128)}), f32[4,64,512]{2,1,0:T(8,128)S(1)}, u32[]{:S(2)}, u32[]{:S(2)}) async-start(f32[4,64,512]{2,1,0:T(8,128)} %fusion.35), calls=%async_computation.5 | async-start | bytes 1048576 | tf_op jit(solution)/shard_map/all_to_all | solution.py:20
  137.2 7.3 %all-to-all-done.5 = f32[4,64,512]{2,1,0:T(8,128)S(1)} async-done(((f32[4,64,512]{2,1,0:T(8,128)}), f32[4,64,512]{2,1,0:T(8,128)S(1)}, u32[]{:S(2)}, u32[]{:S(2)}) %all-to-all-start.5) | async-done | bytes 524320 | tf_op jit(solution)/shard_map/all_to_all | solution.py:20
  144.6 11.6 %all_gather.7 = bf16[256,512]{1,0:T(8,128)(2,1)S(1)} all-gather(bf16[64,512]{1,0:T(8,128)(2,1)S(1)} %reduce_sum.103), channel_id=1, replica_groups=mesh['dp'=64,'mp'=4] {'mp'}, dimensions={0}, use_global_device_ids=true | all-gather | bytes 327680 | tf_op jit(solution)/shard_map/all_gather | solution.py:116
  156.2 2.9 fusion.24
  159.1 9.2 %psum.7 = f32[256]{0:T(256)S(1)} all-reduce(f32[256]{0:T(256)S(1)} %get-tuple-element.40), channel_id=1, replica_groups=mesh['dp'=64,'mp'=4] {'mp'}, use_global_device_ids=true, to_apply=%region_8.0 | all-reduce | flops 256 | bytes 2048 | tf_op jit(solution)/shard_map/psum | solution.py:237
  172.8 6.2 %all-to-all-start.6 = ((f32[4,256,512]{2,1,0:T(8,128)}), f32[4,256,512]{2,1,0:T(8,128)}, u32[]{:S(2)}, u32[]{:S(2)}) async-start(f32[4,256,512]{2,1,0:T(8,128)} %broadcast_in_dim.16), calls=%async_computation.6 | async-start | bytes 4194304 | tf_op jit(solution)/shard_map/all_to_all | solution.py:26
  179.1 8.1 %scatter_custom_fusion = s32[4096]{0:T(1024)S(1)} fusion(s32[2048]{0:T(1024)S(1)} %bitcast.190, s32[2048]{0:T(1024)S(1)} %bitcast.192, s32[]{:T(128)} %constant.125.clone.1), kind=kCustom, calls=%fused_computation.132 | custom fusion | bytes 16388
  188.0 6.2 %all-to-all-done.6 = f32[4,256,512]{2,1,0:T(8,128)} async-done(((f32[4,256,512]{2,1,0:T(8,128)}), f32[4,256,512]{2,1,0:T(8,128)}, u32[]{:S(2)}, u32[]{:S(2)}) %all-to-all-start.6) | async-done | bytes 2097184 | tf_op jit(solution)/shard_map/all_to_all | solution.py:26
  194.2 7.4 %all-to-all-start = ((s32[4,64,16]{2,0,1:T(4,128)}), s32[4,64,16]{2,0,1:T(4,128)S(1)}, u32[]{:S(2)}, u32[]{:S(2)}) async-start(s32[4,64,16]{2,0,1:T(4,128)} %copy.90), calls=%async_computation | async-start | bytes 262144 | tf_op jit(solution)/shard_map/all_to_all | solution.py:170
  201.7 2.6 reduce_sum.105
  207.6 5.2 %all-to-all-done = s32[4,64,16]{2,0,1:T(4,128)S(1)} async-done(((s32[4,64,16]{2,0,1:T(4,128)}), s32[4,64,16]{2,0,1:T(4,128)S(1)}, u32[]{:S(2)}, u32[]{:S(2)}) %all-to-all-start) | async-done | bytes 16416 | tf_op jit(solution)/shard_map/all_to_all | solution.py:170
  212.7 2.6 broadcast_in_dim.17
  215.3 5.9 %all-to-all-start.7 = ((f32[4,256,512]{2,1,0:T(8,128)}), f32[4,256,512]{2,1,0:T(8,128)}, u32[]{:S(2)}, u32[]{:S(2)}) async-start(f32[4,256,512]{2,1,0:T(8,128)} %broadcast_in_dim.17), calls=%async_computation.7 | async-start | bytes 4194304 | tf_op jit(solution)/shard_map/all_to_all | solution.py:26
  224.4 22.4 %all-to-all-done.7 = f32[4,256,512]{2,1,0:T(8,128)} async-done(((f32[4,256,512]{2,1,0:T(8,128)}), f32[4,256,512]{2,1,0:T(8,128)}, u32[]{:S(2)}, u32[]{:S(2)}) %all-to-all-start.7) | async-done | bytes 2097184 | tf_op jit(solution)/shard_map/all_to_all | solution.py:26
  246.8 5.6 %all-to-all-start.1 = ((bf16[4,64,16,256]{3,2,0,1:T(8,128)(2,1)}), bf16[4,64,16,256]{3,2,0,1:T(8,128)(2,1)}, u32[]{:S(2)}, u32[]{:S(2)}) async-start(bf16[4,64,16,256]{3,2,0,1:T(8,128)(2,1)} %copy.92), calls=%async_computation.1 | async-start | bytes 4194304 | tf_op jit(solution)/shard_map/all_to_all | solution.py:163
  253.2 2.8 convolution_bitcast_fusion.1
  263.2 2.6 pad_maximum_fusion
  265.8 3.3 copy-done.2
  271.6 3.4 collective-permute-done.11
  276.4 2.6 collective-permute-done.12
  279.0 3.0 collective-permute-start.13
  282.0 2.9 copy.95
  285.0 18.5 %all-to-all-done.1 = bf16[4,64,16,256]{3,2,0,1:T(8,128)(2,1)} async-done(((bf16[4,64,16,256]{3,2,0,1:T(8,128)(2,1)}), bf16[4,64,16,256]{3,2,0,1:T(8,128)(2,1)}, u32[]{:S(2)}, u32[]{:S(2)}) %all-to-all-start.1) | async-done | bytes 2097184 | tf_op jit(solution)/shard_map/all_to_all | solution.py:163
  306.0 3.5 bitcast_add_fusion
  311.3 2.7 collective-permute-start.2
  315.5 2.9 multiply_reduce_fusion
  319.1 4.0 %collective-permute-done.15 = f32[3,1024]{1,0:T(4,128)S(1)} collective-permute-done((f32[3,1024]{1,0:T(4,128)S(1)}, f32[3,1024]{1,0:T(4,128)S(1)}, u32[]{:S(2)}, u32[]{:S(2)}) %collective-permute-start.15) | collective-permute-done | bytes 12320 | tf_op jit(solution)/shard_map/ppermute | solution.py:77
  325.1 11.5 %collective-permute-done.2 = bf16[4,8,8,1024]{3,2,1,0:T(8,128)(2,1)S(1)} collective-permute-done((bf16[4,8,8,1024]{3,2,1,0:T(8,128)(2,1)S(1)}, bf16[4,8,8,1024]{3,2,1,0:T(8,128)(2,1)S(1)}, u32[]{:S(2)}, u32[]{:S(2)}) %collective-permute-start.2) | collective-permute-done | bytes 524320 | tf_op jit(solution)/shard_map/ppermute | solution.py:58
  338.0 2.3 collective-permute-start.10
  342.1 3.0 copy.113
  346.5 2.7 collective-permute-start.6
  349.2 3.7 collective-permute-start.7
  352.9 2.7 collective-permute-start.8
  355.6 2.5 collective-permute-start.9
  358.0 2.9 fusion.21
  360.9 7.7 %collective-permute-done.6 = f32[4,8,1024]{2,1,0:T(8,128)S(1)} collective-permute-done((f32[4,8,1024]{2,1,0:T(8,128)}, f32[4,8,1024]{2,1,0:T(8,128)S(1)}, u32[]{:S(2)}, u32[]{:S(2)}) %collective-permute-start.6) | collective-permute-done | bytes 131104 | tf_op jit(solution)/shard_map/ppermute | solution.py:58
  368.7 5.5 %collective-permute-done.9 = f32[4,8,1024]{2,1,0:T(8,128)S(1)} collective-permute-done((f32[4,8,1024]{2,1,0:T(8,128)S(1)}, f32[4,8,1024]{2,1,0:T(8,128)S(1)}, u32[]{:S(2)}, u32[]{:S(2)}) %collective-permute-start.9) | collective-permute-done | bytes 131104 | tf_op jit(solution)/shard_map/ppermute | solution.py:58
  (154 shorter events, 48.6 us)
Async XLA Ops:
  0.6 220.6 %copy-start = (bf16[4,512,256]{2,1,0:T(8,128)(2,1)S(1)}, bf16[4,512,256]{2,1,0:T(8,128)(2,1)}, u32[]{:S(2)}) copy-start(bf16[4,512,256]{2,1,0:T(8,128)(2,1)} %param.15) | copy-start | bytes 3145732
  0.6 3.0 copy-start.29
  0.7 3.1 copy-start.28
  0.7 2.9 copy-start.18
  0.7 3.3 copy-start.22
  40.5 56.8 %all-to-all-start.3 = ((bf16[4,64,16,256]{3,2,0,1:T(8,128)(2,1)}), bf16[4,64,16,256]{3,2,0,1:T(8,128)(2,1)}, u32[]{:S(2)}, u32[]{:S(2)}) async-start(bf16[4,64,16,256]{3,2,0,1:T(8,128)(2,1)} %copy.102), calls=%async_computation.3 | async-start | bytes 4194304 | tf_op jit(solution)/shard_map/all_to_all | solution.py:205
  101.4 7.8 %copy-start.23 = (f32[2,1024]{1,0:T(2,128)S(1)}, f32[2,1024]{1,0:T(2,128)}, u32[]{:S(2)}) copy-start(f32[2,1024]{1,0:T(2,128)} %param.24) | copy-start | bytes 24580
  104.3 11.5 %all-to-all-start.4 = ((f32[4,64,512]{2,1,0:T(8,128)}), f32[4,64,512]{2,1,0:T(8,128)S(1)}, u32[]{:S(2)}, u32[]{:S(2)}) async-start(f32[4,64,512]{2,1,0:T(8,128)} %fusion.41), calls=%async_computation.4 | async-start | bytes 1048576 | tf_op jit(solution)/shard_map/all_to_all | solution.py:20
  115.8 14.6 %copy-start.16 = (bf16[2,512,1024]{2,1,0:T(8,128)(2,1)S(1)}, bf16[2,512,1024]{2,1,0:T(8,128)(2,1)}, u32[]{:S(2)}) copy-start(bf16[2,512,1024]{2,1,0:T(8,128)(2,1)} %param.23) | copy-start | bytes 6291460
  127.6 4.1 %copy-start.10 = (bf16[256,512]{1,0:T(8,128)(2,1)}, bf16[256,512]{1,0:T(8,128)(2,1)S(1)}, u32[]{:S(2)}) copy-start(bf16[256,512]{1,0:T(8,128)(2,1)S(1)} %all_gather.6) | copy-start | bytes 786436
  130.4 25.8 %copy-start.6 = (bf16[256,1024]{1,0:T(8,128)(2,1)}, bf16[256,1024]{1,0:T(8,128)(2,1)S(1)}, u32[]{:S(2)}) copy-start(bf16[256,1024]{1,0:T(8,128)(2,1)S(1)} %get-tuple-element.70) | copy-start | bytes 1572868
  130.4 6.8 %copy-start.17 = (f32[1024]{0:T(1024)S(1)}, f32[1024]{0:T(1024)}, u32[]{:S(2)}) copy-start(f32[1024]{0:T(1024)} %param.25) | copy-start | bytes 12292
  131.7 12.8 %all-to-all-start.5 = ((f32[4,64,512]{2,1,0:T(8,128)}), f32[4,64,512]{2,1,0:T(8,128)S(1)}, u32[]{:S(2)}, u32[]{:S(2)}) async-start(f32[4,64,512]{2,1,0:T(8,128)} %fusion.35), calls=%async_computation.5 | async-start | bytes 1048576 | tf_op jit(solution)/shard_map/all_to_all | solution.py:20
  144.6 23.7 %copy-start.27 = (s32[256]{0:T(256)S(1)}, s32[256]{0:T(256)}, u32[]{:S(2)}) copy-start(s32[256]{0:T(256)} %param.21) | copy-start | bytes 3076
  168.3 4.5 %copy-start.19 = (f32[256]{0:T(256)}, f32[256]{0:T(256)S(1)}, u32[]{:S(2)}) copy-start(f32[256]{0:T(256)S(1)} %fusion.84) | copy-start | bytes 3076
  169.3 3.5 copy-start.13
  172.8 6.3 %copy-start.24 = (s32[4,512]{1,0:T(4,128)S(1)}, s32[4,512]{1,0:T(4,128)}, u32[]{:S(2)}) copy-start(s32[4,512]{1,0:T(4,128)} %param.17) | copy-start | bytes 24580
  172.8 21.4 %all-to-all-start.6 = ((f32[4,256,512]{2,1,0:T(8,128)}), f32[4,256,512]{2,1,0:T(8,128)}, u32[]{:S(2)}, u32[]{:S(2)}) async-start(f32[4,256,512]{2,1,0:T(8,128)} %broadcast_in_dim.16), calls=%async_computation.6 | async-start | bytes 4194304 | tf_op jit(solution)/shard_map/all_to_all | solution.py:26
  194.2 18.5 %all-to-all-start = ((s32[4,64,16]{2,0,1:T(4,128)}), s32[4,64,16]{2,0,1:T(4,128)S(1)}, u32[]{:S(2)}, u32[]{:S(2)}) async-start(s32[4,64,16]{2,0,1:T(4,128)} %copy.90), calls=%async_computation | async-start | bytes 262144 | tf_op jit(solution)/shard_map/all_to_all | solution.py:170
  204.3 2.0 copy-start.5
  215.3 31.4 %all-to-all-start.7 = ((f32[4,256,512]{2,1,0:T(8,128)}), f32[4,256,512]{2,1,0:T(8,128)}, u32[]{:S(2)}, u32[]{:S(2)}) async-start(f32[4,256,512]{2,1,0:T(8,128)} %broadcast_in_dim.17), calls=%async_computation.7 | async-start | bytes 4194304 | tf_op jit(solution)/shard_map/all_to_all | solution.py:26
  224.4 28.9 %copy-start.14 = (bf16[256,4,256]{0,2,1:T(8,128)(2,1)S(1)}, bf16[256,4,256]{0,2,1:T(8,128)(2,1)}, u32[]{:S(2)}) copy-start(bf16[256,4,256]{0,2,1:T(8,128)(2,1)} %copy-done.13) | copy-start | bytes 1572868
  246.8 56.8 %all-to-all-start.1 = ((bf16[4,64,16,256]{3,2,0,1:T(8,128)(2,1)}), bf16[4,64,16,256]{3,2,0,1:T(8,128)(2,1)}, u32[]{:S(2)}, u32[]{:S(2)}) async-start(bf16[4,64,16,256]{3,2,0,1:T(8,128)(2,1)} %copy.92), calls=%async_computation.1 | async-start | bytes 4194304 | tf_op jit(solution)/shard_map/all_to_all | solution.py:163
  252.3 3.7 copy-start.7
  253.2 2.8 copy-start.15
  265.8 3.3 copy-start.2
  270.7 35.3 %collective-permute-start = (bf16[4,8,4,8,1024]{4,3,2,1,0:T(8,128)(2,1)}, bf16[4,8,4,8,1024]{4,3,2,1,0:T(8,128)(2,1)}, u32[]{:S(2)}, u32[]{:S(2)}) collective-permute-start(bf16[4,8,4,8,1024]{4,3,2,1,0:T(8,128)(2,1)} %fusion.12), channel_id=1, source_target_pairs={{0,4},{4,0},{8,12},{12,8},{16,20},{20,16},{24,28},{28,24},{32,36},... | collective-permute-start | bytes 6291464 | tf_op jit(solution)/shard_map/ppermute | solution.py:58
  271.0 3.9 %collective-permute-start.11 = (f32[3,1024]{1,0:T(4,128)S(1)}, f32[3,1024]{1,0:T(4,128)S(1)}, u32[]{:S(2)}, u32[]{:S(2)}) collective-permute-start(f32[3,1024]{1,0:T(4,128)S(1)} %pad_maximum_fusion.1), channel_id=1, source_target_pairs={{0,4},{4,0},{8,12},{12,8},{16,20},{20,16},{24,28},{28,24},{32,36},... | collective-permute-start | bytes 36872 | tf_op jit(solution)/shard_map/ppermute | solution.py:77
  274.9 4.1 %collective-permute-start.12 = (f32[3,1024]{1,0:T(4,128)S(1)}, f32[3,1024]{1,0:T(4,128)S(1)}, u32[]{:S(2)}, u32[]{:S(2)}) collective-permute-start(f32[3,1024]{1,0:T(4,128)S(1)} %fusion.86), channel_id=1, source_target_pairs={{0,8},{4,12},{8,0},{12,4},{16,24},{20,28},{24,16},{28,20},{32,40},... | collective-permute-start | bytes 36872 | tf_op jit(solution)/shard_map/ppermute | solution.py:77
  279.0 26.3 %collective-permute-start.13 = (f32[3,1024]{1,0:T(4,128)S(1)}, f32[3,1024]{1,0:T(4,128)S(1)}, u32[]{:S(2)}, u32[]{:S(2)}) collective-permute-start(f32[3,1024]{1,0:T(4,128)S(1)} %fusion.113), channel_id=1, source_target_pairs={{0,16},{4,20},{8,24},{12,28},{16,0},{20,4},{24,8},{28,12},{32,48},... | collective-permute-start | bytes 36872 | tf_op jit(solution)/shard_map/ppermute | solution.py:77
  305.3 13.1 %collective-permute-start.14 = (f32[3,1024]{1,0:T(4,128)S(1)}, f32[3,1024]{1,0:T(4,128)S(1)}, u32[]{:S(2)}, u32[]{:S(2)}) collective-permute-start(f32[3,1024]{1,0:T(4,128)S(1)} %add.312), channel_id=1, source_target_pairs={{0,32},{4,36},{8,40},{12,44},{16,48},{20,52},{24,56},{28,60},{32,0... | collective-permute-start | bytes 36872 | tf_op jit(solution)/shard_map/ppermute | solution.py:77
  309.8 15.3 %collective-permute-start.1 = (bf16[4,8,8,1024]{3,2,1,0:T(8,128)(2,1)S(1)}, bf16[4,8,8,1024]{3,2,1,0:T(8,128)(2,1)S(1)}, u32[]{:S(2)}, u32[]{:S(2)}) collective-permute-start(bf16[4,8,8,1024]{3,2,1,0:T(8,128)(2,1)S(1)} %get-tuple-element.46), channel_id=1, source_target_pairs={{0,8},{4,12},{8,16},{12,20},{16,24},{20,28},{24,0},{28,4},{32,40},... | collective-permute-start | bytes 1572872 | tf_op jit(solution)/shard_map/ppermute | solution.py:58
  311.3 25.3 %collective-permute-start.2 = (bf16[4,8,8,1024]{3,2,1,0:T(8,128)(2,1)S(1)}, bf16[4,8,8,1024]{3,2,1,0:T(8,128)(2,1)S(1)}, u32[]{:S(2)}, u32[]{:S(2)}) collective-permute-start(bf16[4,8,8,1024]{3,2,1,0:T(8,128)(2,1)S(1)} %get-tuple-element.48), channel_id=1, source_target_pairs={{0,16},{4,20},{8,24},{12,28},{16,0},{20,4},{24,8},{28,12},{32,48},... | collective-permute-start | bytes 1572872 | tf_op jit(solution)/shard_map/ppermute | solution.py:58
  314.0 22.6 %collective-permute-start.3 = (bf16[4,8,8,1024]{3,2,1,0:T(8,128)(2,1)S(1)}, bf16[4,8,8,1024]{3,2,1,0:T(8,128)(2,1)S(1)}, u32[]{:S(2)}, u32[]{:S(2)}) collective-permute-start(bf16[4,8,8,1024]{3,2,1,0:T(8,128)(2,1)S(1)} %get-tuple-element.47), channel_id=1, source_target_pairs={{0,24},{4,28},{8,0},{12,4},{16,8},{20,12},{24,16},{28,20},{32,56},... | collective-permute-start | bytes 1572872 | tf_op jit(solution)/shard_map/ppermute | solution.py:58
  315.5 3.0 copy-start.25
  318.4 4.7 %collective-permute-start.15 = (f32[3,1024]{1,0:T(4,128)S(1)}, f32[3,1024]{1,0:T(4,128)S(1)}, u32[]{:S(2)}, u32[]{:S(2)}) collective-permute-start(f32[3,1024]{1,0:T(4,128)S(1)} %add.313), channel_id=1, source_target_pairs={{0,64},{4,68},{8,72},{12,76},{16,80},{20,84},{24,88},{28,92},{32,9... | collective-permute-start | bytes 36872 | tf_op jit(solution)/shard_map/ppermute | solution.py:77
  323.1 17.1 %copy-start.3 = (f32[4,512,256]{1,2,0:T(8,128)S(1)}, f32[4,512,256]{1,2,0:T(8,128)}, u32[]{:S(2)}) copy-start(f32[4,512,256]{1,2,0:T(8,128)} %copy.95) | copy-start | bytes 6291460
  323.1 21.9 %collective-permute-start.16 = (f32[3,1024]{1,0:T(4,128)S(1)}, f32[3,1024]{1,0:T(4,128)}, u32[]{:S(2)}, u32[]{:S(2)}) collective-permute-start(f32[3,1024]{1,0:T(4,128)S(1)} %add.314), channel_id=1, source_target_pairs={{0,128},{4,132},{8,136},{12,140},{16,144},{20,148},{24,152},{28,15... | collective-permute-start | bytes 36872 | tf_op jit(solution)/shard_map/ppermute | solution.py:77
  337.0 5.1 %copy-start.9 = (f32[4,8,8,1024]{3,2,1,0:T(8,128)}, f32[4,8,8,1024]{3,2,1,0:T(8,128)S(1)}, u32[]{:S(2)}) copy-start(f32[4,8,8,1024]{3,2,1,0:T(8,128)S(1)} %fusion.31) | copy-start | bytes 3145732
  338.0 14.9 %collective-permute-start.10 = (f32[4,8,1024]{2,1,0:T(8,128)}, f32[4,8,1024]{2,1,0:T(8,128)}, u32[]{:S(2)}, u32[]{:S(2)}) collective-permute-start(f32[4,8,1024]{2,1,0:T(8,128)} %get-tuple-element.50), channel_id=1, source_target_pairs={{0,224},{4,228},{8,232},{12,236},{16,240},{20,244},{24,248},{28,25... | collective-permute-start | bytes 393224 | tf_op jit(solution)/shard_map/ppermute | solution.py:58
  340.3 15.3 %collective-permute-start.4 = (f32[4,8,1024]{2,1,0:T(8,128)}, f32[4,8,1024]{2,1,0:T(8,128)}, u32[]{:S(2)}, u32[]{:S(2)}) collective-permute-start(f32[4,8,1024]{2,1,0:T(8,128)} %get-tuple-element.49), channel_id=1, source_target_pairs={{0,32},{4,36},{8,40},{12,44},{16,48},{20,52},{24,56},{28,60},{32,6... | collective-permute-start | bytes 393224 | tf_op jit(solution)/shard_map/ppermute | solution.py:58
  342.1 15.9 %copy-start.8 = (f32[256,1024]{1,0:T(8,128)S(1)}, f32[256,1024]{1,0:T(8,128)}, u32[]{:S(2)}) copy-start(f32[256,1024]{1,0:T(8,128)} %get-tuple-element.72) | copy-start | bytes 3145732
  346.4 14.5 %collective-permute-start.5 = (f32[4,8,1024]{2,1,0:T(8,128)}, f32[4,8,1024]{2,1,0:T(8,128)S(1)}, u32[]{:S(2)}, u32[]{:S(2)}) collective-permute-start(f32[4,8,1024]{2,1,0:T(8,128)} %get-tuple-element.55), channel_id=1, source_target_pairs={{0,64},{4,68},{8,72},{12,76},{16,80},{20,84},{24,88},{28,92},{32,9... | collective-permute-start | bytes 393224 | tf_op jit(solution)/shard_map/ppermute | solution.py:58
  346.5 22.2 %collective-permute-start.6 = (f32[4,8,1024]{2,1,0:T(8,128)}, f32[4,8,1024]{2,1,0:T(8,128)S(1)}, u32[]{:S(2)}, u32[]{:S(2)}) collective-permute-start(f32[4,8,1024]{2,1,0:T(8,128)} %get-tuple-element.54), channel_id=1, source_target_pairs={{0,96},{4,100},{8,104},{12,108},{16,112},{20,116},{24,120},{28,124... | collective-permute-start | bytes 393224 | tf_op jit(solution)/shard_map/ppermute | solution.py:58
  349.2 19.5 %collective-permute-start.7 = (f32[4,8,1024]{2,1,0:T(8,128)}, f32[4,8,1024]{2,1,0:T(8,128)S(1)}, u32[]{:S(2)}, u32[]{:S(2)}) collective-permute-start(f32[4,8,1024]{2,1,0:T(8,128)} %get-tuple-element.53), channel_id=1, source_target_pairs={{0,128},{4,132},{8,136},{12,140},{16,144},{20,148},{24,152},{28,15... | collective-permute-start | bytes 393224 | tf_op jit(solution)/shard_map/ppermute | solution.py:58
  352.9 15.8 %collective-permute-start.8 = (f32[4,8,1024]{2,1,0:T(8,128)}, f32[4,8,1024]{2,1,0:T(8,128)S(1)}, u32[]{:S(2)}, u32[]{:S(2)}) collective-permute-start(f32[4,8,1024]{2,1,0:T(8,128)} %get-tuple-element.52), channel_id=1, source_target_pairs={{0,160},{4,164},{8,168},{12,172},{16,176},{20,180},{24,184},{28,18... | collective-permute-start | bytes 393224 | tf_op jit(solution)/shard_map/ppermute | solution.py:58
  355.6 18.6 %collective-permute-start.9 = (f32[4,8,1024]{2,1,0:T(8,128)S(1)}, f32[4,8,1024]{2,1,0:T(8,128)S(1)}, u32[]{:S(2)}, u32[]{:S(2)}) collective-permute-start(f32[4,8,1024]{2,1,0:T(8,128)S(1)} %get-tuple-element.51), channel_id=1, source_target_pairs={{0,192},{4,196},{8,200},{12,204},{16,208},{20,212},{24,216},{28,22... | collective-permute-start | bytes 393224 | tf_op jit(solution)/shard_map/ppermute | solution.py:58
  358.0 17.9 %copy-start.1 = (bf16[4,512,256]{2,1,0:T(8,128)(2,1)S(1)}, bf16[4,512,256]{2,1,0:T(8,128)(2,1)}, u32[]{:S(2)}) copy-start(bf16[4,512,256]{2,1,0:T(8,128)(2,1)} %param.15) | copy-start | bytes 3145732
  (6 other events, 9.2 us)

commit v10 on v9

--- a/solution.py
+++ b/solution.py
@@ -258,7 +258,7 @@
         grads_u[layer] = grad_u_layer
         grads_v[layer] = down_factor_gradient
     both = jnp.concatenate((jnp.stack(grads_u), jnp.stack(grads_v)), axis=0)
-    wires = [jnp.float32] + [jnp.bfloat16] * (len(splits) - 1)
+    wires = [jnp.bfloat16] * len(splits)
     grad_u, grad_v = jnp.split(tree_sum_scatter(both, "dp", 1, splits, wires), 2, axis=0)
     grad_small = butterfly_sum(jnp.stack(bias_grads + [head_grad]), "dp")
     grad_pooled = (upstream + to_start).astype(jnp.bfloat16)

time: 379 us -> 369 us (0.974)
  waiting for transfers between devices: 152 us -> 143 us
    ppermute x11, waiting for transfers between devices: 25.7 us -> 16.2 us  [direct_sum_scatter(): total = total + lax.ppermute(sent, axis, toward).astype(total.dtype)]
where the time goes in v10:
time: 369 us; the launch traced here: 366 us
  waiting for transfers between devices  143 us (39%)
  starting transfers between devices  67.6 us (18%)
  blocking collectives  55.4 us (15%)
  local copies, waits for them, and re-layouts  46.2 us (13%)
  matrix products  35 us (9%)
  other arithmetic  18.2 us (5%)
    all_to_all x1, waiting for transfers between devices, local(): lax.all_to_all(served.reshape(local_feats, peers, look_cap, width), 'dp',...  50.3 us
    all_to_all x2, waiting for transfers between devices, copy_for_each(): return lax.all_to_all(copies, axis, split_axis=0, concat_axis=0, tiled=True)  28.6 us
    unnamed x72, local copies, waits for them, and re-layouts  28 us
    all_gather x2, blocking collectives, cross_down(): return lax.all_gather(share.astype(jnp.bfloat16), 'mp', axis=0, tiled=True)  23.4 us
    all_to_all x1, blocking collectives, local(): lax.all_to_all(wanted.reshape(local_feats, peers, look_cap), 'dp', split_...  22.8 us
    ppermute x11, starting transfers between devices, direct_sum_scatter(): total = total + lax.ppermute(sent, axis, toward).astype(total.dtype)  19.6 us
    all_to_all x1, waiting for transfers between devices, local(): lax.all_to_all(send_grads.reshape(local_feats, peers, grad_cap, width), '...  18.5 us
    ppermute x11, waiting for transfers between devices, direct_sum_scatter(): total = total + lax.ppermute(sent, axis, toward).astype(total.dtype)  16.2 us
  transfers between devices with their start and end apart: 24, of which 14 were waited for; matrix products, arithmetic and copies ran while one was open for 15% of the time, Pallas kernels for 0%

profile of v10, /device:TPU:8, one launch (start us, length us, event | category | flops | bytes accessed | tf_op | source)
XLA Modules:
  0.0 366.2 jit_solution(539168714883712135)
XLA Ops:
  4.0 8.1 %scatter_custom_fusion.1 = s32[4096]{0:T(1024)S(1)} fusion(s32[2048]{0:T(1024)S(1)} %bitcast.215, s32[2048]{0:T(1024)S(1)} %bitcast.217, s32[]{:T(128)} %constant.128.clone.1), kind=kCustom, calls=%fused_computation.137 | custom fusion | bytes 16388
  12.3 22.8 %all_to_all.40 = s32[4,64,16]{2,0,1:T(4,128)S(1)} all-to-all(s32[4,64,16]{2,0,1:T(4,128)S(1)} %copy.124), channel_id=1, replica_groups=mesh['dp'=64,'mp'=4] {'dp'}, dimensions={1} | all-to-all | bytes 32768 | tf_op jit(solution)/shard_map/all_to_all | solution.py:195
  35.2 3.7 %fusion.15 = bf16[4,1024,256]{2,1,0:T(8,128)(2,1)S(1)} fusion(s32[4,1024]{1,0:T(4,128)S(1)} %eq.144, f32[4,512,256]{2,1,0:T(8,128)} %param.13), kind=kOutput, calls=%fused_computation.25 | convolution fusion | flops 1077411840 | bytes 4210688 | tf_op jit(solution)/shard_map/adv,avm->adm/dot_general | solution.py:199
  40.5 5.6 %all-to-all-start.3 = ((bf16[4,64,16,256]{3,2,0,1:T(8,128)(2,1)}), bf16[4,64,16,256]{3,2,0,1:T(8,128)(2,1)}, u32[]{:S(2)}, u32[]{:S(2)}) async-start(bf16[4,64,16,256]{3,2,0,1:T(8,128)(2,1)} %copy.126), calls=%async_computation.3 | async-start | bytes 4194304 | tf_op jit(solution)/shard_map/all_to_all | solution.py:205
  46.9 50.3 %all-to-all-done.3 = bf16[4,64,16,256]{3,2,0,1:T(8,128)(2,1)} async-done(((bf16[4,64,16,256]{3,2,0,1:T(8,128)(2,1)}), bf16[4,64,16,256]{3,2,0,1:T(8,128)(2,1)}, u32[]{:S(2)}, u32[]{:S(2)}) %all-to-all-start.3) | async-done | bytes 2097184 | tf_op jit(solution)/shard_map/all_to_all | solution.py:205
  99.0 2.1 fusion.18
  101.8 2.5 fusion.41
  104.3 4.9 %all-to-all-start.4 = ((f32[4,64,512]{2,1,0:T(8,128)}), f32[4,64,512]{2,1,0:T(8,128)S(1)}, u32[]{:S(2)}, u32[]{:S(2)}) async-start(f32[4,64,512]{2,1,0:T(8,128)} %fusion.41), calls=%async_computation.4 | async-start | bytes 1048576 | tf_op jit(solution)/shard_map/all_to_all | solution.py:20
  109.4 6.4 %all-to-all-done.4 = f32[4,64,512]{2,1,0:T(8,128)S(1)} async-done(((f32[4,64,512]{2,1,0:T(8,128)}), f32[4,64,512]{2,1,0:T(8,128)S(1)}, u32[]{:S(2)}, u32[]{:S(2)}) %all-to-all-start.4) | async-done | bytes 524320 | tf_op jit(solution)/shard_map/all_to_all | solution.py:20
  115.9 11.8 %all_gather.6 = bf16[256,512]{1,0:T(8,128)(2,1)S(1)} all-gather(bf16[64,512]{1,0:T(8,128)(2,1)S(1)} %reduce_sum.102), channel_id=1, replica_groups=mesh['dp'=64,'mp'=4] {'mp'}, dimensions={0}, use_global_device_ids=true | all-gather | bytes 327680 | tf_op jit(solution)/shard_map/all_gather | solution.py:116
  127.6 2.8 fusion.27
  131.7 5.5 %all-to-all-start.5 = ((f32[4,64,512]{2,1,0:T(8,128)}), f32[4,64,512]{2,1,0:T(8,128)S(1)}, u32[]{:S(2)}, u32[]{:S(2)}) async-start(f32[4,64,512]{2,1,0:T(8,128)} %fusion.35), calls=%async_computation.5 | async-start | bytes 1048576 | tf_op jit(solution)/shard_map/all_to_all | solution.py:20
  137.3 7.3 %all-to-all-done.5 = f32[4,64,512]{2,1,0:T(8,128)S(1)} async-done(((f32[4,64,512]{2,1,0:T(8,128)}), f32[4,64,512]{2,1,0:T(8,128)S(1)}, u32[]{:S(2)}, u32[]{:S(2)}) %all-to-all-start.5) | async-done | bytes 524320 | tf_op jit(solution)/shard_map/all_to_all | solution.py:20
  144.6 11.6 %all_gather.7 = bf16[256,512]{1,0:T(8,128)(2,1)S(1)} all-gather(bf16[64,512]{1,0:T(8,128)(2,1)S(1)} %reduce_sum.103), channel_id=1, replica_groups=mesh['dp'=64,'mp'=4] {'mp'}, dimensions={0}, use_global_device_ids=true | all-gather | bytes 327680 | tf_op jit(solution)/shard_map/all_gather | solution.py:116
  156.2 2.9 fusion.24
  159.1 9.2 %psum.7 = f32[256]{0:T(256)S(1)} all-reduce(f32[256]{0:T(256)S(1)} %get-tuple-element.40), channel_id=1, replica_groups=mesh['dp'=64,'mp'=4] {'mp'}, use_global_device_ids=true, to_apply=%region_8.0 | all-reduce | flops 256 | bytes 2048 | tf_op jit(solution)/shard_map/psum | solution.py:237
  172.8 6.3 %all-to-all-start.6 = ((f32[4,256,512]{2,1,0:T(8,128)}), f32[4,256,512]{2,1,0:T(8,128)}, u32[]{:S(2)}, u32[]{:S(2)}) async-start(f32[4,256,512]{2,1,0:T(8,128)} %broadcast_in_dim.16), calls=%async_computation.6 | async-start | bytes 4194304 | tf_op jit(solution)/shard_map/all_to_all | solution.py:26
  179.1 8.1 %scatter_custom_fusion = s32[4096]{0:T(1024)S(1)} fusion(s32[2048]{0:T(1024)S(1)} %bitcast.214, s32[2048]{0:T(1024)S(1)} %bitcast.216, s32[]{:T(128)} %constant.125.clone.1), kind=kCustom, calls=%fused_computation.139 | custom fusion | bytes 16388
  188.0 6.2 %all-to-all-done.6 = f32[4,256,512]{2,1,0:T(8,128)} async-done(((f32[4,256,512]{2,1,0:T(8,128)}), f32[4,256,512]{2,1,0:T(8,128)}, u32[]{:S(2)}, u32[]{:S(2)}) %all-to-all-start.6) | async-done | bytes 2097184 | tf_op jit(solution)/shard_map/all_to_all | solution.py:26
  194.2 7.4 %all-to-all-start = ((s32[4,64,16]{2,0,1:T(4,128)}), s32[4,64,16]{2,0,1:T(4,128)S(1)}, u32[]{:S(2)}, u32[]{:S(2)}) async-start(s32[4,64,16]{2,0,1:T(4,128)} %copy.114), calls=%async_computation | async-start | bytes 262144 | tf_op jit(solution)/shard_map/all_to_all | solution.py:170
  201.7 2.6 reduce_sum.105
  204.3 1.9 fusion.61
  207.5 5.2 %all-to-all-done = s32[4,64,16]{2,0,1:T(4,128)S(1)} async-done(((s32[4,64,16]{2,0,1:T(4,128)}), s32[4,64,16]{2,0,1:T(4,128)S(1)}, u32[]{:S(2)}, u32[]{:S(2)}) %all-to-all-start) | async-done | bytes 16416 | tf_op jit(solution)/shard_map/all_to_all | solution.py:170
  212.7 2.6 broadcast_in_dim.17
  215.3 5.9 %all-to-all-start.7 = ((f32[4,256,512]{2,1,0:T(8,128)}), f32[4,256,512]{2,1,0:T(8,128)}, u32[]{:S(2)}, u32[]{:S(2)}) async-start(f32[4,256,512]{2,1,0:T(8,128)} %broadcast_in_dim.17), calls=%async_computation.7 | async-start | bytes 4194304 | tf_op jit(solution)/shard_map/all_to_all | solution.py:26
  224.3 22.4 %all-to-all-done.7 = f32[4,256,512]{2,1,0:T(8,128)} async-done(((f32[4,256,512]{2,1,0:T(8,128)}), f32[4,256,512]{2,1,0:T(8,128)}, u32[]{:S(2)}, u32[]{:S(2)}) %all-to-all-start.7) | async-done | bytes 2097184 | tf_op jit(solution)/shard_map/all_to_all | solution.py:26
  246.7 5.6 %all-to-all-start.1 = ((bf16[4,64,16,256]{3,2,0,1:T(8,128)(2,1)}), bf16[4,64,16,256]{3,2,0,1:T(8,128)(2,1)}, u32[]{:S(2)}, u32[]{:S(2)}) async-start(bf16[4,64,16,256]{3,2,0,1:T(8,128)(2,1)} %copy.116), calls=%async_computation.1 | async-start | bytes 4194304 | tf_op jit(solution)/shard_map/all_to_all | solution.py:163
  253.2 2.8 convolution_bitcast_fusion.1
  263.2 2.6 pad_maximum_fusion
  265.8 3.3 copy-done.2
  271.6 3.4 collective-permute-done.11
  276.4 2.6 collective-permute-done.12
  279.0 3.0 collective-permute-start.13
  282.0 2.9 copy.119
  285.0 18.5 %all-to-all-done.1 = bf16[4,64,16,256]{3,2,0,1:T(8,128)(2,1)} async-done(((bf16[4,64,16,256]{3,2,0,1:T(8,128)(2,1)}), bf16[4,64,16,256]{3,2,0,1:T(8,128)(2,1)}, u32[]{:S(2)}, u32[]{:S(2)}) %all-to-all-start.1) | async-done | bytes 2097184 | tf_op jit(solution)/shard_map/all_to_all | solution.py:163
  306.0 3.5 bitcast_add_fusion
  311.3 2.7 collective-permute-start.2
  315.5 2.9 multiply_reduce_fusion
  319.1 4.0 %collective-permute-done.15 = f32[3,1024]{1,0:T(4,128)S(1)} collective-permute-done((f32[3,1024]{1,0:T(4,128)S(1)}, f32[3,1024]{1,0:T(4,128)S(1)}, u32[]{:S(2)}, u32[]{:S(2)}) %collective-permute-start.15) | collective-permute-done | bytes 12320 | tf_op jit(solution)/shard_map/ppermute | solution.py:77
  325.1 11.5 %collective-permute-done.2 = bf16[4,8,8,1024]{3,2,1,0:T(8,128)(2,1)S(1)} collective-permute-done((bf16[4,8,8,1024]{3,2,1,0:T(8,128)(2,1)S(1)}, bf16[4,8,8,1024]{3,2,1,0:T(8,128)(2,1)S(1)}, u32[]{:S(2)}, u32[]{:S(2)}) %collective-permute-start.2) | collective-permute-done | bytes 524320 | tf_op jit(solution)/shard_map/ppermute | solution.py:58
  337.8 2.3 collective-permute-start.10
  342.0 3.0 copy.143
  346.3 2.7 collective-permute-start.6
  349.0 3.7 %collective-permute-start.7 = (bf16[4,8,1024]{2,1,0:T(8,128)(2,1)}, bf16[4,8,1024]{2,1,0:T(8,128)(2,1)S(1)}, u32[]{:S(2)}, u32[]{:S(2)}) collective-permute-start(bf16[4,8,1024]{2,1,0:T(8,128)(2,1)} %get-tuple-element.51), channel_id=1, source_target_pairs={{0,128},{4,132},{8,136},{12,140},{16,144},{20,148},{24,152},{28,15... | collective-permute-start | bytes 196616 | tf_op jit(solution)/shard_map/ppermute | solution.py:58
  352.8 2.7 collective-permute-start.8
  355.5 2.5 collective-permute-start.9
  357.9 2.9 fusion.21
  361.8 2.7 collective-permute-done.9
  (154 shorter events, 47.3 us)
Async XLA Ops:
  0.6 220.6 %copy-start = (bf16[4,512,256]{2,1,0:T(8,128)(2,1)S(1)}, bf16[4,512,256]{2,1,0:T(8,128)(2,1)}, u32[]{:S(2)}) copy-start(bf16[4,512,256]{2,1,0:T(8,128)(2,1)} %param.15) | copy-start | bytes 3145732
  0.6 3.0 copy-start.29
  0.7 3.1 copy-start.28
  0.7 2.9 copy-start.18
  0.7 3.3 copy-start.22
  40.5 56.8 %all-to-all-start.3 = ((bf16[4,64,16,256]{3,2,0,1:T(8,128)(2,1)}), bf16[4,64,16,256]{3,2,0,1:T(8,128)(2,1)}, u32[]{:S(2)}, u32[]{:S(2)}) async-start(bf16[4,64,16,256]{3,2,0,1:T(8,128)(2,1)} %copy.126), calls=%async_computation.3 | async-start | bytes 4194304 | tf_op jit(solution)/shard_map/all_to_all | solution.py:205
  101.4 7.8 %copy-start.23 = (f32[2,1024]{1,0:T(2,128)S(1)}, f32[2,1024]{1,0:T(2,128)}, u32[]{:S(2)}) copy-start(f32[2,1024]{1,0:T(2,128)} %param.24) | copy-start | bytes 24580
  104.3 11.5 %all-to-all-start.4 = ((f32[4,64,512]{2,1,0:T(8,128)}), f32[4,64,512]{2,1,0:T(8,128)S(1)}, u32[]{:S(2)}, u32[]{:S(2)}) async-start(f32[4,64,512]{2,1,0:T(8,128)} %fusion.41), calls=%async_computation.4 | async-start | bytes 1048576 | tf_op jit(solution)/shard_map/all_to_all | solution.py:20
  115.8 14.6 %copy-start.16 = (bf16[2,512,1024]{2,1,0:T(8,128)(2,1)S(1)}, bf16[2,512,1024]{2,1,0:T(8,128)(2,1)}, u32[]{:S(2)}) copy-start(bf16[2,512,1024]{2,1,0:T(8,128)(2,1)} %param.23) | copy-start | bytes 6291460
  127.6 4.1 %copy-start.10 = (bf16[256,512]{1,0:T(8,128)(2,1)}, bf16[256,512]{1,0:T(8,128)(2,1)S(1)}, u32[]{:S(2)}) copy-start(bf16[256,512]{1,0:T(8,128)(2,1)S(1)} %all_gather.6) | copy-start | bytes 786436
  130.4 25.8 %copy-start.6 = (bf16[256,1024]{1,0:T(8,128)(2,1)}, bf16[256,1024]{1,0:T(8,128)(2,1)S(1)}, u32[]{:S(2)}) copy-start(bf16[256,1024]{1,0:T(8,128)(2,1)S(1)} %get-tuple-element.70) | copy-start | bytes 1572868
  130.4 6.8 %copy-start.17 = (f32[1024]{0:T(1024)S(1)}, f32[1024]{0:T(1024)}, u32[]{:S(2)}) copy-start(f32[1024]{0:T(1024)} %param.25) | copy-start | bytes 12292
  131.7 12.8 %all-to-all-start.5 = ((f32[4,64,512]{2,1,0:T(8,128)}), f32[4,64,512]{2,1,0:T(8,128)S(1)}, u32[]{:S(2)}, u32[]{:S(2)}) async-start(f32[4,64,512]{2,1,0:T(8,128)} %fusion.35), calls=%async_computation.5 | async-start | bytes 1048576 | tf_op jit(solution)/shard_map/all_to_all | solution.py:20
  144.6 23.7 %copy-start.27 = (s32[256]{0:T(256)S(1)}, s32[256]{0:T(256)}, u32[]{:S(2)}) copy-start(s32[256]{0:T(256)} %param.21) | copy-start | bytes 3076
  168.3 4.5 %copy-start.19 = (f32[256]{0:T(256)}, f32[256]{0:T(256)S(1)}, u32[]{:S(2)}) copy-start(f32[256]{0:T(256)S(1)} %fusion.91) | copy-start | bytes 3076
  169.3 3.5 copy-start.13
  172.8 6.3 %copy-start.24 = (s32[4,512]{1,0:T(4,128)S(1)}, s32[4,512]{1,0:T(4,128)}, u32[]{:S(2)}) copy-start(s32[4,512]{1,0:T(4,128)} %param.17) | copy-start | bytes 24580
  172.8 21.4 %all-to-all-start.6 = ((f32[4,256,512]{2,1,0:T(8,128)}), f32[4,256,512]{2,1,0:T(8,128)}, u32[]{:S(2)}, u32[]{:S(2)}) async-start(f32[4,256,512]{2,1,0:T(8,128)} %broadcast_in_dim.16), calls=%async_computation.6 | async-start | bytes 4194304 | tf_op jit(solution)/shard_map/all_to_all | solution.py:26
  194.2 18.5 %all-to-all-start = ((s32[4,64,16]{2,0,1:T(4,128)}), s32[4,64,16]{2,0,1:T(4,128)S(1)}, u32[]{:S(2)}, u32[]{:S(2)}) async-start(s32[4,64,16]{2,0,1:T(4,128)} %copy.114), calls=%async_computation | async-start | bytes 262144 | tf_op jit(solution)/shard_map/all_to_all | solution.py:170
  204.3 2.0 copy-start.5
  215.3 31.4 %all-to-all-start.7 = ((f32[4,256,512]{2,1,0:T(8,128)}), f32[4,256,512]{2,1,0:T(8,128)}, u32[]{:S(2)}, u32[]{:S(2)}) async-start(f32[4,256,512]{2,1,0:T(8,128)} %broadcast_in_dim.17), calls=%async_computation.7 | async-start | bytes 4194304 | tf_op jit(solution)/shard_map/all_to_all | solution.py:26
  224.3 28.9 %copy-start.14 = (bf16[256,4,256]{0,2,1:T(8,128)(2,1)S(1)}, bf16[256,4,256]{0,2,1:T(8,128)(2,1)}, u32[]{:S(2)}) copy-start(bf16[256,4,256]{0,2,1:T(8,128)(2,1)} %copy-done.13) | copy-start | bytes 1572868
  246.7 56.8 %all-to-all-start.1 = ((bf16[4,64,16,256]{3,2,0,1:T(8,128)(2,1)}), bf16[4,64,16,256]{3,2,0,1:T(8,128)(2,1)}, u32[]{:S(2)}, u32[]{:S(2)}) async-start(bf16[4,64,16,256]{3,2,0,1:T(8,128)(2,1)} %copy.116), calls=%async_computation.1 | async-start | bytes 4194304 | tf_op jit(solution)/shard_map/all_to_all | solution.py:163
  252.3 3.7 copy-start.7
  253.2 2.8 copy-start.15
  265.8 3.3 copy-start.2
  270.7 35.3 %collective-permute-start = (bf16[4,8,4,8,1024]{4,3,2,1,0:T(8,128)(2,1)}, bf16[4,8,4,8,1024]{4,3,2,1,0:T(8,128)(2,1)}, u32[]{:S(2)}, u32[]{:S(2)}) collective-permute-start(bf16[4,8,4,8,1024]{4,3,2,1,0:T(8,128)(2,1)} %fusion.12), channel_id=1, source_target_pairs={{0,4},{4,0},{8,12},{12,8},{16,20},{20,16},{24,28},{28,24},{32,36},... | collective-permute-start | bytes 6291464 | tf_op jit(solution)/shard_map/ppermute | solution.py:58
  271.0 3.9 %collective-permute-start.11 = (f32[3,1024]{1,0:T(4,128)S(1)}, f32[3,1024]{1,0:T(4,128)S(1)}, u32[]{:S(2)}, u32[]{:S(2)}) collective-permute-start(f32[3,1024]{1,0:T(4,128)S(1)} %pad_maximum_fusion.1), channel_id=1, source_target_pairs={{0,4},{4,0},{8,12},{12,8},{16,20},{20,16},{24,28},{28,24},{32,36},... | collective-permute-start | bytes 36872 | tf_op jit(solution)/shard_map/ppermute | solution.py:77
  274.9 4.1 %collective-permute-start.12 = (f32[3,1024]{1,0:T(4,128)S(1)}, f32[3,1024]{1,0:T(4,128)S(1)}, u32[]{:S(2)}, u32[]{:S(2)}) collective-permute-start(f32[3,1024]{1,0:T(4,128)S(1)} %fusion.93), channel_id=1, source_target_pairs={{0,8},{4,12},{8,0},{12,4},{16,24},{20,28},{24,16},{28,20},{32,40},... | collective-permute-start | bytes 36872 | tf_op jit(solution)/shard_map/ppermute | solution.py:77
  279.0 26.3 %collective-permute-start.13 = (f32[3,1024]{1,0:T(4,128)S(1)}, f32[3,1024]{1,0:T(4,128)S(1)}, u32[]{:S(2)}, u32[]{:S(2)}) collective-permute-start(f32[3,1024]{1,0:T(4,128)S(1)} %fusion.120), channel_id=1, source_target_pairs={{0,16},{4,20},{8,24},{12,28},{16,0},{20,4},{24,8},{28,12},{32,48},... | collective-permute-start | bytes 36872 | tf_op jit(solution)/shard_map/ppermute | solution.py:77
  305.3 13.1 %collective-permute-start.14 = (f32[3,1024]{1,0:T(4,128)S(1)}, f32[3,1024]{1,0:T(4,128)S(1)}, u32[]{:S(2)}, u32[]{:S(2)}) collective-permute-start(f32[3,1024]{1,0:T(4,128)S(1)} %add.312), channel_id=1, source_target_pairs={{0,32},{4,36},{8,40},{12,44},{16,48},{20,52},{24,56},{28,60},{32,0... | collective-permute-start | bytes 36872 | tf_op jit(solution)/shard_map/ppermute | solution.py:77
  309.8 15.3 %collective-permute-start.1 = (bf16[4,8,8,1024]{3,2,1,0:T(8,128)(2,1)S(1)}, bf16[4,8,8,1024]{3,2,1,0:T(8,128)(2,1)S(1)}, u32[]{:S(2)}, u32[]{:S(2)}) collective-permute-start(bf16[4,8,8,1024]{3,2,1,0:T(8,128)(2,1)S(1)} %get-tuple-element.46), channel_id=1, source_target_pairs={{0,8},{4,12},{8,16},{12,20},{16,24},{20,28},{24,0},{28,4},{32,40},... | collective-permute-start | bytes 1572872 | tf_op jit(solution)/shard_map/ppermute | solution.py:58
  311.3 25.3 %collective-permute-start.2 = (bf16[4,8,8,1024]{3,2,1,0:T(8,128)(2,1)S(1)}, bf16[4,8,8,1024]{3,2,1,0:T(8,128)(2,1)S(1)}, u32[]{:S(2)}, u32[]{:S(2)}) collective-permute-start(bf16[4,8,8,1024]{3,2,1,0:T(8,128)(2,1)S(1)} %get-tuple-element.48), channel_id=1, source_target_pairs={{0,16},{4,20},{8,24},{12,28},{16,0},{20,4},{24,8},{28,12},{32,48},... | collective-permute-start | bytes 1572872 | tf_op jit(solution)/shard_map/ppermute | solution.py:58
  314.0 22.6 %collective-permute-start.3 = (bf16[4,8,8,1024]{3,2,1,0:T(8,128)(2,1)S(1)}, bf16[4,8,8,1024]{3,2,1,0:T(8,128)(2,1)S(1)}, u32[]{:S(2)}, u32[]{:S(2)}) collective-permute-start(bf16[4,8,8,1024]{3,2,1,0:T(8,128)(2,1)S(1)} %get-tuple-element.47), channel_id=1, source_target_pairs={{0,24},{4,28},{8,0},{12,4},{16,8},{20,12},{24,16},{28,20},{32,56},... | collective-permute-start | bytes 1572872 | tf_op jit(solution)/shard_map/ppermute | solution.py:58
  315.5 3.0 copy-start.25
  318.4 4.7 %collective-permute-start.15 = (f32[3,1024]{1,0:T(4,128)S(1)}, f32[3,1024]{1,0:T(4,128)S(1)}, u32[]{:S(2)}, u32[]{:S(2)}) collective-permute-start(f32[3,1024]{1,0:T(4,128)S(1)} %add.313), channel_id=1, source_target_pairs={{0,64},{4,68},{8,72},{12,76},{16,80},{20,84},{24,88},{28,92},{32,9... | collective-permute-start | bytes 36872 | tf_op jit(solution)/shard_map/ppermute | solution.py:77
  323.1 17.0 %copy-start.3 = (f32[4,512,256]{1,2,0:T(8,128)S(1)}, f32[4,512,256]{1,2,0:T(8,128)}, u32[]{:S(2)}) copy-start(f32[4,512,256]{1,2,0:T(8,128)} %copy.119) | copy-start | bytes 6291460
  323.1 21.8 %collective-permute-start.16 = (f32[3,1024]{1,0:T(4,128)S(1)}, f32[3,1024]{1,0:T(4,128)}, u32[]{:S(2)}, u32[]{:S(2)}) collective-permute-start(f32[3,1024]{1,0:T(4,128)S(1)} %add.314), channel_id=1, source_target_pairs={{0,128},{4,132},{8,136},{12,140},{16,144},{20,148},{24,152},{28,15... | collective-permute-start | bytes 36872 | tf_op jit(solution)/shard_map/ppermute | solution.py:77
  337.0 5.0 %copy-start.9 = (f32[4,8,8,1024]{3,2,1,0:T(8,128)}, f32[4,8,8,1024]{3,2,1,0:T(8,128)S(1)}, u32[]{:S(2)}) copy-start(f32[4,8,8,1024]{3,2,1,0:T(8,128)S(1)} %fusion.31) | copy-start | bytes 3145732
  337.8 14.9 %collective-permute-start.10 = (bf16[4,8,1024]{2,1,0:T(8,128)(2,1)}, bf16[4,8,1024]{2,1,0:T(8,128)(2,1)S(1)}, u32[]{:S(2)}, u32[]{:S(2)}) collective-permute-start(bf16[4,8,1024]{2,1,0:T(8,128)(2,1)} %get-tuple-element.54), channel_id=1, source_target_pairs={{0,224},{4,228},{8,232},{12,236},{16,240},{20,244},{24,248},{28,25... | collective-permute-start | bytes 196616 | tf_op jit(solution)/shard_map/ppermute | solution.py:58
  340.1 15.3 %collective-permute-start.4 = (bf16[4,8,1024]{2,1,0:T(8,128)(2,1)}, bf16[4,8,1024]{2,1,0:T(8,128)(2,1)S(1)}, u32[]{:S(2)}, u32[]{:S(2)}) collective-permute-start(bf16[4,8,1024]{2,1,0:T(8,128)(2,1)} %get-tuple-element.49), channel_id=1, source_target_pairs={{0,32},{4,36},{8,40},{12,44},{16,48},{20,52},{24,56},{28,60},{32,6... | collective-permute-start | bytes 196616 | tf_op jit(solution)/shard_map/ppermute | solution.py:58
  342.0 15.9 %copy-start.8 = (f32[256,1024]{1,0:T(8,128)S(1)}, f32[256,1024]{1,0:T(8,128)}, u32[]{:S(2)}) copy-start(f32[256,1024]{1,0:T(8,128)} %get-tuple-element.72) | copy-start | bytes 3145732
  346.3 14.5 %collective-permute-start.5 = (bf16[4,8,1024]{2,1,0:T(8,128)(2,1)}, bf16[4,8,1024]{2,1,0:T(8,128)(2,1)S(1)}, u32[]{:S(2)}, u32[]{:S(2)}) collective-permute-start(bf16[4,8,1024]{2,1,0:T(8,128)(2,1)} %get-tuple-element.53), channel_id=1, source_target_pairs={{0,64},{4,68},{8,72},{12,76},{16,80},{20,84},{24,88},{28,92},{32,9... | collective-permute-start | bytes 196616 | tf_op jit(solution)/shard_map/ppermute | solution.py:58
  346.3 14.5 %collective-permute-start.6 = (bf16[4,8,1024]{2,1,0:T(8,128)(2,1)}, bf16[4,8,1024]{2,1,0:T(8,128)(2,1)S(1)}, u32[]{:S(2)}, u32[]{:S(2)}) collective-permute-start(bf16[4,8,1024]{2,1,0:T(8,128)(2,1)} %get-tuple-element.52), channel_id=1, source_target_pairs={{0,96},{4,100},{8,104},{12,108},{16,112},{20,116},{24,120},{28,124... | collective-permute-start | bytes 196616 | tf_op jit(solution)/shard_map/ppermute | solution.py:58
  349.0 11.8 %collective-permute-start.7 = (bf16[4,8,1024]{2,1,0:T(8,128)(2,1)}, bf16[4,8,1024]{2,1,0:T(8,128)(2,1)S(1)}, u32[]{:S(2)}, u32[]{:S(2)}) collective-permute-start(bf16[4,8,1024]{2,1,0:T(8,128)(2,1)} %get-tuple-element.51), channel_id=1, source_target_pairs={{0,128},{4,132},{8,136},{12,140},{16,144},{20,148},{24,152},{28,15... | collective-permute-start | bytes 196616 | tf_op jit(solution)/shard_map/ppermute | solution.py:58
  352.8 9.0 %collective-permute-start.8 = (bf16[4,8,1024]{2,1,0:T(8,128)(2,1)}, bf16[4,8,1024]{2,1,0:T(8,128)(2,1)S(1)}, u32[]{:S(2)}, u32[]{:S(2)}) collective-permute-start(bf16[4,8,1024]{2,1,0:T(8,128)(2,1)} %get-tuple-element.50), channel_id=1, source_target_pairs={{0,160},{4,164},{8,168},{12,172},{16,176},{20,180},{24,184},{28,18... | collective-permute-start | bytes 196616 | tf_op jit(solution)/shard_map/ppermute | solution.py:58
  355.5 9.1 %collective-permute-start.9 = (bf16[4,8,1024]{2,1,0:T(8,128)(2,1)}, bf16[4,8,1024]{2,1,0:T(8,128)(2,1)S(1)}, u32[]{:S(2)}, u32[]{:S(2)}) collective-permute-start(bf16[4,8,1024]{2,1,0:T(8,128)(2,1)} %get-tuple-element.55), channel_id=1, source_target_pairs={{0,192},{4,196},{8,200},{12,204},{16,208},{20,212},{24,216},{28,22... | collective-permute-start | bytes 196616 | tf_op jit(solution)/shard_map/ppermute | solution.py:58
  357.9 8.2 %copy-start.1 = (bf16[4,512,256]{2,1,0:T(8,128)(2,1)S(1)}, bf16[4,512,256]{2,1,0:T(8,128)(2,1)}, u32[]{:S(2)}) copy-start(bf16[4,512,256]{2,1,0:T(8,128)(2,1)} %param.15) | copy-start | bytes 3145732
  (6 other events, 9.2 us)

commit v11 on v10

--- a/solution.py
+++ b/solution.py
@@ -97,6 +97,12 @@
 
 def selection_matrix(indices, length):
     return (indices[:, :, None] == jnp.arange(length)[None, None, :]).astype(jnp.bfloat16)
+
+
+def placed_ints(onehot, values):
+    digits = jnp.stack((values // 32, values % 32), axis=-1).astype(jnp.bfloat16)
+    moved = jnp.einsum("fns,fnk->fsk", onehot, digits, preferred_element_type=jnp.float32)
+    return moved[..., 0].astype(jnp.int32) * 32 + moved[..., 1].astype(jnp.int32)
 
 
 def contract_last(left, right):
@@ -155,11 +161,7 @@
     send_grads = jnp.einsum(
         "fns,fne->fse", place, stale_grad, preferred_element_type=jnp.float32
     ).astype(jnp.bfloat16)
-    send_rows = (
-        jnp.full((local_feats, grad_total), rows_per_shard, jnp.int32)
-        .at[which_feature, grad_slot]
-        .set(grad_row)
-    )
+    send_rows = placed_ints(place, grad_row + 1) - 1
     recv_grads = lax.all_to_all(
         send_grads.reshape(local_feats, peers, grad_cap, width),
         "dp",
@@ -189,9 +191,7 @@
     look_cap = max(2, 2 * look_dev // peers)
     look_total = peers * look_cap
     look_slot = bucket_slots(lookup_owner[:, :, 0], look_cap, peers)
-    wanted = (
-        jnp.zeros((local_feats, look_total), jnp.int32).at[which_feature, look_slot].set(lookup_row)
-    )
+    wanted = placed_ints(selection_matrix(look_slot, look_total), lookup_row)
     requested_ids = lax.all_to_all(
         wanted.reshape(local_feats, peers, look_cap), "dp", split_axis=1, concat_axis=1, tiled=True
     ).reshape(local_feats, look_total)

time: 369 us -> 361 us (0.978)
  local copies, waits for them, and re-layouts: 46.2 us -> 29.4 us
  waiting for transfers between devices: 143 us -> 148 us
  matrix products: 35 us -> 38.9 us
    unnamed x72 -> x59, local copies, waits for them, and re-layouts: 28 us -> 11.2 us
    all_to_all x2, waiting for transfers between devices: 28.6 us -> 33.9 us  [copy_for_each(): return lax.all_to_all(copies, axis, split_axis=0, concat_axis=0, tiled=True)]
  transfers between devices with their start and end apart: 24 -> 24, of which waited for: 14 -> 14; matrix products, arithmetic and copies ran while one was open for 15% -> 14% of each run, Pallas kernels for 0% -> 0%
where the time goes in v11:
time: 361 us; the launch traced here: 359 us
  waiting for transfers between devices  148 us (41%)
  starting transfers between devices  67.6 us (19%)
  blocking collectives  55.4 us (15%)
  matrix products  38.9 us (11%)
  local copies, waits for them, and re-layouts  29.4 us (8%)
  other arithmetic  18.2 us (5%)
    all_to_all x1, waiting for transfers between devices, local(): lax.all_to_all(served.reshape(local_feats, peers, look_cap, width), 'dp',...  50.3 us
    all_to_all x2, waiting for transfers between devices, copy_for_each(): return lax.all_to_all(copies, axis, split_axis=0, concat_axis=0, tiled=True)  33.9 us
    all_gather x2, blocking collectives, cross_down(): return lax.all_gather(share.astype(jnp.bfloat16), 'mp', axis=0, tiled=True)  23.4 us
    all_to_all x1, blocking collectives, local(): lax.all_to_all(wanted.reshape(local_feats, peers, look_cap), 'dp', split_...  22.8 us
    ppermute x11, starting transfers between devices, direct_sum_scatter(): total = total + lax.ppermute(sent, axis, toward).astype(total.dtype)  19.6 us
    all_to_all x1, waiting for transfers between devices, local(): lax.all_to_all(send_grads.reshape(local_feats, peers, grad_cap, width), '...  18.5 us
    ppermute x11, waiting for transfers between devices, direct_sum_scatter(): total = total + lax.ppermute(sent, axis, toward).astype(total.dtype)  16.2 us
    all_to_all x2, waiting for transfers between devices, sum_at_owner(): lax.all_to_all(parts, axis, split_axis=0, concat_axis=0, tiled=True)  13.7 us
  transfers between devices with their start and end apart: 24, of which 14 were waited for; matrix products, arithmetic and copies ran while one was open for 14% of the time, Pallas kernels for 0%

profile of v11, /device:TPU:8, one launch (start us, length us, event | category | flops | bytes accessed | tf_op | source)
XLA Modules:
  0.0 358.6 jit_solution(3054419487944814700)
XLA Ops:
  5.2 22.8 %all_to_all.40 = s32[4,64,16]{2,0,1:T(4,128)S(1)} all-to-all(s32[4,64,16]{2,0,1:T(4,128)S(1)} %copy.218), channel_id=1, replica_groups=mesh['dp'=64,'mp'=4] {'dp'}, dimensions={1} | all-to-all | bytes 32768 | tf_op jit(solution)/shard_map/all_to_all | solution.py:195
  28.1 3.7 %fusion.19 = bf16[4,1024,256]{2,1,0:T(8,128)(2,1)S(1)} fusion(s32[4,1024]{1,0:T(4,128)S(1)} %eq.166, f32[4,512,256]{2,1,0:T(8,128)} %param.13), kind=kOutput, calls=%fused_computation.28 | convolution fusion | flops 1077411840 | bytes 4210688 | tf_op jit(solution)/shard_map/adv,avm->adm/dot_general | solution.py:199
  33.4 5.6 %all-to-all-start.3 = ((bf16[4,64,16,256]{3,2,0,1:T(8,128)(2,1)}), bf16[4,64,16,256]{3,2,0,1:T(8,128)(2,1)}, u32[]{:S(2)}, u32[]{:S(2)}) async-start(bf16[4,64,16,256]{3,2,0,1:T(8,128)(2,1)} %copy.220), calls=%async_computation.3 | async-start | bytes 4194304 | tf_op jit(solution)/shard_map/all_to_all | solution.py:205
  39.9 50.3 %all-to-all-done.3 = bf16[4,64,16,256]{3,2,0,1:T(8,128)(2,1)} async-done(((bf16[4,64,16,256]{3,2,0,1:T(8,128)(2,1)}), bf16[4,64,16,256]{3,2,0,1:T(8,128)(2,1)}, u32[]{:S(2)}, u32[]{:S(2)}) %all-to-all-start.3) | async-done | bytes 2097184 | tf_op jit(solution)/shard_map/all_to_all | solution.py:205
  92.0 2.1 fusion.22
  94.7 2.5 fusion.45
  97.2 4.9 %all-to-all-start.4 = ((f32[4,64,512]{2,1,0:T(8,128)}), f32[4,64,512]{2,1,0:T(8,128)S(1)}, u32[]{:S(2)}, u32[]{:S(2)}) async-start(f32[4,64,512]{2,1,0:T(8,128)} %fusion.45), calls=%async_computation.4 | async-start | bytes 1048576 | tf_op jit(solution)/shard_map/all_to_all | solution.py:20
  102.4 6.4 %all-to-all-done.4 = f32[4,64,512]{2,1,0:T(8,128)S(1)} async-done(((f32[4,64,512]{2,1,0:T(8,128)}), f32[4,64,512]{2,1,0:T(8,128)S(1)}, u32[]{:S(2)}, u32[]{:S(2)}) %all-to-all-start.4) | async-done | bytes 524320 | tf_op jit(solution)/shard_map/all_to_all | solution.py:20
  108.8 11.8 %all_gather.6 = bf16[256,512]{1,0:T(8,128)(2,1)S(1)} all-gather(bf16[64,512]{1,0:T(8,128)(2,1)S(1)} %reduce_sum.102), channel_id=1, replica_groups=mesh['dp'=64,'mp'=4] {'mp'}, dimensions={0}, use_global_device_ids=true | all-gather | bytes 327680 | tf_op jit(solution)/shard_map/all_gather | solution.py:122
  120.6 2.8 fusion.31
  124.7 5.5 %all-to-all-start.5 = ((f32[4,64,512]{2,1,0:T(8,128)}), f32[4,64,512]{2,1,0:T(8,128)S(1)}, u32[]{:S(2)}, u32[]{:S(2)}) async-start(f32[4,64,512]{2,1,0:T(8,128)} %fusion.39), calls=%async_computation.5 | async-start | bytes 1048576 | tf_op jit(solution)/shard_map/all_to_all | solution.py:20
  130.2 7.3 %all-to-all-done.5 = f32[4,64,512]{2,1,0:T(8,128)S(1)} async-done(((f32[4,64,512]{2,1,0:T(8,128)}), f32[4,64,512]{2,1,0:T(8,128)S(1)}, u32[]{:S(2)}, u32[]{:S(2)}) %all-to-all-start.5) | async-done | bytes 524320 | tf_op jit(solution)/shard_map/all_to_all | solution.py:20
  137.6 11.6 %all_gather.7 = bf16[256,512]{1,0:T(8,128)(2,1)S(1)} all-gather(bf16[64,512]{1,0:T(8,128)(2,1)S(1)} %reduce_sum.103), channel_id=1, replica_groups=mesh['dp'=64,'mp'=4] {'mp'}, dimensions={0}, use_global_device_ids=true | all-gather | bytes 327680 | tf_op jit(solution)/shard_map/all_gather | solution.py:122
  149.1 2.9 fusion.28
  152.0 9.3 %psum.7 = f32[256]{0:T(256)S(1)} all-reduce(f32[256]{0:T(256)S(1)} %get-tuple-element.54), channel_id=1, replica_groups=mesh['dp'=64,'mp'=4] {'mp'}, use_global_device_ids=true, to_apply=%region_6.7 | all-reduce | flops 256 | bytes 2048 | tf_op jit(solution)/shard_map/psum | solution.py:237
  161.7 1.9 fusion.36
  165.2 6.2 %all-to-all-start.6 = ((f32[4,256,512]{2,1,0:T(8,128)}), f32[4,256,512]{2,1,0:T(8,128)}, u32[]{:S(2)}, u32[]{:S(2)}) async-start(f32[4,256,512]{2,1,0:T(8,128)} %broadcast_in_dim.4), calls=%async_computation.6 | async-start | bytes 4194304 | tf_op jit(solution)/shard_map/all_to_all | solution.py:26
  174.4 12.2 %all-to-all-done.6 = f32[4,256,512]{2,1,0:T(8,128)} async-done(((f32[4,256,512]{2,1,0:T(8,128)}), f32[4,256,512]{2,1,0:T(8,128)}, u32[]{:S(2)}, u32[]{:S(2)}) %all-to-all-start.6) | async-done | bytes 2097184 | tf_op jit(solution)/shard_map/all_to_all | solution.py:26
  186.6 7.4 %all-to-all-start = ((s32[4,64,16]{2,0,1:T(4,128)}), s32[4,64,16]{2,0,1:T(4,128)S(1)}, u32[]{:S(2)}, u32[]{:S(2)}) async-start(s32[4,64,16]{2,0,1:T(4,128)} %copy.206), calls=%async_computation | async-start | bytes 262144 | tf_op jit(solution)/shard_map/all_to_all | solution.py:172
  194.0 2.6 reduce_sum.105
  196.7 1.9 fusion.65
  199.9 5.2 %all-to-all-done = s32[4,64,16]{2,0,1:T(4,128)S(1)} async-done(((s32[4,64,16]{2,0,1:T(4,128)}), s32[4,64,16]{2,0,1:T(4,128)S(1)}, u32[]{:S(2)}, u32[]{:S(2)}) %all-to-all-start) | async-done | bytes 16416 | tf_op jit(solution)/shard_map/all_to_all | solution.py:172
  205.1 2.6 broadcast_in_dim.5
  207.7 5.9 %all-to-all-start.7 = ((f32[4,256,512]{2,1,0:T(8,128)}), f32[4,256,512]{2,1,0:T(8,128)}, u32[]{:S(2)}, u32[]{:S(2)}) async-start(f32[4,256,512]{2,1,0:T(8,128)} %broadcast_in_dim.5), calls=%async_computation.7 | async-start | bytes 4194304 | tf_op jit(solution)/shard_map/all_to_all | solution.py:26
  213.6 2.2 fusion.20
  217.5 21.7 %all-to-all-done.7 = f32[4,256,512]{2,1,0:T(8,128)} async-done(((f32[4,256,512]{2,1,0:T(8,128)}), f32[4,256,512]{2,1,0:T(8,128)}, u32[]{:S(2)}, u32[]{:S(2)}) %all-to-all-start.7) | async-done | bytes 2097184 | tf_op jit(solution)/shard_map/all_to_all | solution.py:26
  239.2 5.6 %all-to-all-start.1 = ((bf16[4,64,16,256]{3,2,0,1:T(8,128)(2,1)}), bf16[4,64,16,256]{3,2,0,1:T(8,128)(2,1)}, u32[]{:S(2)}, u32[]{:S(2)}) async-start(bf16[4,64,16,256]{3,2,0,1:T(8,128)(2,1)} %copy.208), calls=%async_computation.1 | async-start | bytes 4194304 | tf_op jit(solution)/shard_map/all_to_all | solution.py:165
  245.6 2.8 convolution_bitcast_fusion.1
  255.6 2.6 pad_maximum_fusion
  258.2 3.3 copy-done.2
  264.0 3.4 collective-permute-done.11
  268.8 2.6 collective-permute-done.12
  271.4 3.0 collective-permute-start.13
  274.4 2.9 copy.211
  277.4 18.5 %all-to-all-done.1 = bf16[4,64,16,256]{3,2,0,1:T(8,128)(2,1)} async-done(((bf16[4,64,16,256]{3,2,0,1:T(8,128)(2,1)}), bf16[4,64,16,256]{3,2,0,1:T(8,128)(2,1)}, u32[]{:S(2)}, u32[]{:S(2)}) %all-to-all-start.1) | async-done | bytes 2097184 | tf_op jit(solution)/shard_map/all_to_all | solution.py:165
  298.4 3.5 bitcast_add_fusion
  303.7 2.7 collective-permute-start.2
  307.9 2.9 multiply_reduce_fusion
  311.5 4.0 %collective-permute-done.15 = f32[3,1024]{1,0:T(4,128)S(1)} collective-permute-done((f32[3,1024]{1,0:T(4,128)S(1)}, f32[3,1024]{1,0:T(4,128)S(1)}, u32[]{:S(2)}, u32[]{:S(2)}) %collective-permute-start.15) | collective-permute-done | bytes 12320 | tf_op jit(solution)/shard_map/ppermute | solution.py:77
  317.5 11.5 %collective-permute-done.2 = bf16[4,8,8,1024]{3,2,1,0:T(8,128)(2,1)S(1)} collective-permute-done((bf16[4,8,8,1024]{3,2,1,0:T(8,128)(2,1)S(1)}, bf16[4,8,8,1024]{3,2,1,0:T(8,128)(2,1)S(1)}, u32[]{:S(2)}, u32[]{:S(2)}) %collective-permute-start.2) | collective-permute-done | bytes 524320 | tf_op jit(solution)/shard_map/ppermute | solution.py:58
  330.3 2.3 collective-permute-start.10
  334.4 3.0 copy.237
  338.8 2.7 collective-permute-start.6
  341.5 3.7 %collective-permute-start.7 = (bf16[4,8,1024]{2,1,0:T(8,128)(2,1)}, bf16[4,8,1024]{2,1,0:T(8,128)(2,1)S(1)}, u32[]{:S(2)}, u32[]{:S(2)}) collective-permute-start(bf16[4,8,1024]{2,1,0:T(8,128)(2,1)} %get-tuple-element.63), channel_id=1, source_target_pairs={{0,128},{4,132},{8,136},{12,140},{16,144},{20,148},{24,152},{28,15... | collective-permute-start | bytes 196616 | tf_op jit(solution)/shard_map/ppermute | solution.py:58
  345.2 2.7 collective-permute-start.8
  347.9 2.5 collective-permute-start.9
  350.4 2.9 fusion.25
  354.2 2.7 collective-permute-done.9
  (147 shorter events, 46.5 us)
Async XLA Ops:
  0.6 213.0 %copy-start = (bf16[4,512,256]{2,1,0:T(8,128)(2,1)S(1)}, bf16[4,512,256]{2,1,0:T(8,128)(2,1)}, u32[]{:S(2)}) copy-start(bf16[4,512,256]{2,1,0:T(8,128)(2,1)} %param.15) | copy-start | bytes 3145732
  33.4 56.8 %all-to-all-start.3 = ((bf16[4,64,16,256]{3,2,0,1:T(8,128)(2,1)}), bf16[4,64,16,256]{3,2,0,1:T(8,128)(2,1)}, u32[]{:S(2)}, u32[]{:S(2)}) async-start(bf16[4,64,16,256]{3,2,0,1:T(8,128)(2,1)} %copy.220), calls=%async_computation.3 | async-start | bytes 4194304 | tf_op jit(solution)/shard_map/all_to_all | solution.py:205
  94.3 7.8 %copy-start.20 = (f32[2,1024]{1,0:T(2,128)S(1)}, f32[2,1024]{1,0:T(2,128)}, u32[]{:S(2)}) copy-start(f32[2,1024]{1,0:T(2,128)} %param.24) | copy-start | bytes 24580
  97.2 11.5 %all-to-all-start.4 = ((f32[4,64,512]{2,1,0:T(8,128)}), f32[4,64,512]{2,1,0:T(8,128)S(1)}, u32[]{:S(2)}, u32[]{:S(2)}) async-start(f32[4,64,512]{2,1,0:T(8,128)} %fusion.45), calls=%async_computation.4 | async-start | bytes 1048576 | tf_op jit(solution)/shard_map/all_to_all | solution.py:20
  108.8 14.6 %copy-start.16 = (bf16[2,512,1024]{2,1,0:T(8,128)(2,1)S(1)}, bf16[2,512,1024]{2,1,0:T(8,128)(2,1)}, u32[]{:S(2)}) copy-start(bf16[2,512,1024]{2,1,0:T(8,128)(2,1)} %param.23) | copy-start | bytes 6291460
  120.6 4.1 %copy-start.10 = (bf16[256,512]{1,0:T(8,128)(2,1)}, bf16[256,512]{1,0:T(8,128)(2,1)S(1)}, u32[]{:S(2)}) copy-start(bf16[256,512]{1,0:T(8,128)(2,1)S(1)} %all_gather.6) | copy-start | bytes 786436
  123.4 25.8 %copy-start.6 = (bf16[256,1024]{1,0:T(8,128)(2,1)}, bf16[256,1024]{1,0:T(8,128)(2,1)S(1)}, u32[]{:S(2)}) copy-start(bf16[256,1024]{1,0:T(8,128)(2,1)S(1)} %get-tuple-element.86) | copy-start | bytes 1572868
  123.4 6.8 %copy-start.17 = (f32[1024]{0:T(1024)S(1)}, f32[1024]{0:T(1024)}, u32[]{:S(2)}) copy-start(f32[1024]{0:T(1024)} %param.25) | copy-start | bytes 12292
  124.7 12.8 %all-to-all-start.5 = ((f32[4,64,512]{2,1,0:T(8,128)}), f32[4,64,512]{2,1,0:T(8,128)S(1)}, u32[]{:S(2)}, u32[]{:S(2)}) async-start(f32[4,64,512]{2,1,0:T(8,128)} %fusion.39), calls=%async_computation.5 | async-start | bytes 1048576 | tf_op jit(solution)/shard_map/all_to_all | solution.py:20
  137.5 23.8 %copy-start.25 = (s32[256]{0:T(256)S(1)}, s32[256]{0:T(256)}, u32[]{:S(2)}) copy-start(s32[256]{0:T(256)} %param.21) | copy-start | bytes 3076
  161.3 101.8 %copy-start.19 = (f32[256]{0:T(256)}, f32[256]{0:T(256)S(1)}, u32[]{:S(2)}) copy-start(f32[256]{0:T(256)S(1)} %fusion.114) | copy-start | bytes 3076
  161.7 3.5 copy-start.13
  165.2 6.2 %copy-start.18 = (s32[4,512,1]{1,2,0:T(1,128)S(1)}, s32[4,512,1]{1,2,0:T(1,128)}, u32[]{:S(2)}) copy-start(s32[4,512,1]{1,2,0:T(1,128)} %param.16) | copy-start | bytes 24580
  165.2 6.6 %copy-start.21 = (s32[4,512]{1,0:T(4,128)S(1)}, s32[4,512]{1,0:T(4,128)}, u32[]{:S(2)}) copy-start(s32[4,512]{1,0:T(4,128)} %param.17) | copy-start | bytes 24580
  165.2 21.4 %all-to-all-start.6 = ((f32[4,256,512]{2,1,0:T(8,128)}), f32[4,256,512]{2,1,0:T(8,128)}, u32[]{:S(2)}, u32[]{:S(2)}) async-start(f32[4,256,512]{2,1,0:T(8,128)} %broadcast_in_dim.4), calls=%async_computation.6 | async-start | bytes 4194304 | tf_op jit(solution)/shard_map/all_to_all | solution.py:26
  171.8 14.8 %copy-start.22 = (s32[4,512,1]{1,0,2:T(4,128)}, s32[4,512,1]{1,0,2:T(4,128)S(1)}, u32[]{:S(2)}) copy-start(s32[4,512,1]{1,0,2:T(4,128)S(1)} %copy.264) | copy-start | bytes 24580
  186.6 18.5 %all-to-all-start = ((s32[4,64,16]{2,0,1:T(4,128)}), s32[4,64,16]{2,0,1:T(4,128)S(1)}, u32[]{:S(2)}, u32[]{:S(2)}) async-start(s32[4,64,16]{2,0,1:T(4,128)} %copy.206), calls=%async_computation | async-start | bytes 262144 | tf_op jit(solution)/shard_map/all_to_all | solution.py:172
  196.7 2.0 copy-start.5
  207.7 31.4 %all-to-all-start.7 = ((f32[4,256,512]{2,1,0:T(8,128)}), f32[4,256,512]{2,1,0:T(8,128)}, u32[]{:S(2)}, u32[]{:S(2)}) async-start(f32[4,256,512]{2,1,0:T(8,128)} %broadcast_in_dim.5), calls=%async_computation.7 | async-start | bytes 4194304 | tf_op jit(solution)/shard_map/all_to_all | solution.py:26
  217.5 28.2 %copy-start.14 = (bf16[256,4,256]{0,2,1:T(8,128)(2,1)S(1)}, bf16[256,4,256]{0,2,1:T(8,128)(2,1)}, u32[]{:S(2)}) copy-start(bf16[256,4,256]{0,2,1:T(8,128)(2,1)} %copy-done.13) | copy-start | bytes 1572868
  239.2 56.8 %all-to-all-start.1 = ((bf16[4,64,16,256]{3,2,0,1:T(8,128)(2,1)}), bf16[4,64,16,256]{3,2,0,1:T(8,128)(2,1)}, u32[]{:S(2)}, u32[]{:S(2)}) async-start(bf16[4,64,16,256]{3,2,0,1:T(8,128)(2,1)} %copy.208), calls=%async_computation.1 | async-start | bytes 4194304 | tf_op jit(solution)/shard_map/all_to_all | solution.py:165
  244.7 3.7 %copy-start.7 = (bf16[256,1024]{1,0:T(8,128)(2,1)S(1)}, bf16[256,1024]{1,0:T(8,128)(2,1)}, u32[]{:S(2)}) copy-start(bf16[256,1024]{1,0:T(8,128)(2,1)} %copy-done.6) | copy-start | bytes 1572868
  245.6 2.8 copy-start.15
  248.4 1.8 copy-start.11
  258.2 3.3 copy-start.2
  261.5 1.7 copy-start.12
  263.1 35.3 %collective-permute-start = (bf16[4,8,4,8,1024]{4,3,2,1,0:T(8,128)(2,1)}, bf16[4,8,4,8,1024]{4,3,2,1,0:T(8,128)(2,1)}, u32[]{:S(2)}, u32[]{:S(2)}) collective-permute-start(bf16[4,8,4,8,1024]{4,3,2,1,0:T(8,128)(2,1)} %fusion.16), channel_id=1, source_target_pairs={{0,4},{4,0},{8,12},{12,8},{16,20},{20,16},{24,28},{28,24},{32,36},... | collective-permute-start | bytes 6291464 | tf_op jit(solution)/shard_map/ppermute | solution.py:58
  263.4 3.9 %collective-permute-start.11 = (f32[3,1024]{1,0:T(4,128)S(1)}, f32[3,1024]{1,0:T(4,128)S(1)}, u32[]{:S(2)}, u32[]{:S(2)}) collective-permute-start(f32[3,1024]{1,0:T(4,128)S(1)} %pad_maximum_fusion.1), channel_id=1, source_target_pairs={{0,4},{4,0},{8,12},{12,8},{16,20},{20,16},{24,28},{28,24},{32,36},... | collective-permute-start | bytes 36872 | tf_op jit(solution)/shard_map/ppermute | solution.py:77
  267.4 4.1 %collective-permute-start.12 = (f32[3,1024]{1,0:T(4,128)S(1)}, f32[3,1024]{1,0:T(4,128)S(1)}, u32[]{:S(2)}, u32[]{:S(2)}) collective-permute-start(f32[3,1024]{1,0:T(4,128)S(1)} %fusion.118), channel_id=1, source_target_pairs={{0,8},{4,12},{8,0},{12,4},{16,24},{20,28},{24,16},{28,20},{32,40},... | collective-permute-start | bytes 36872 | tf_op jit(solution)/shard_map/ppermute | solution.py:77
  271.4 26.3 %collective-permute-start.13 = (f32[3,1024]{1,0:T(4,128)S(1)}, f32[3,1024]{1,0:T(4,128)S(1)}, u32[]{:S(2)}, u32[]{:S(2)}) collective-permute-start(f32[3,1024]{1,0:T(4,128)S(1)} %fusion.145), channel_id=1, source_target_pairs={{0,16},{4,20},{8,24},{12,28},{16,0},{20,4},{24,8},{28,12},{32,48},... | collective-permute-start | bytes 36872 | tf_op jit(solution)/shard_map/ppermute | solution.py:77
  297.7 13.1 %collective-permute-start.14 = (f32[3,1024]{1,0:T(4,128)S(1)}, f32[3,1024]{1,0:T(4,128)S(1)}, u32[]{:S(2)}, u32[]{:S(2)}) collective-permute-start(f32[3,1024]{1,0:T(4,128)S(1)} %add.339), channel_id=1, source_target_pairs={{0,32},{4,36},{8,40},{12,44},{16,48},{20,52},{24,56},{28,60},{32,0... | collective-permute-start | bytes 36872 | tf_op jit(solution)/shard_map/ppermute | solution.py:77
  302.2 15.3 %collective-permute-start.1 = (bf16[4,8,8,1024]{3,2,1,0:T(8,128)(2,1)S(1)}, bf16[4,8,8,1024]{3,2,1,0:T(8,128)(2,1)S(1)}, u32[]{:S(2)}, u32[]{:S(2)}) collective-permute-start(bf16[4,8,8,1024]{3,2,1,0:T(8,128)(2,1)S(1)} %get-tuple-element.58), channel_id=1, source_target_pairs={{0,8},{4,12},{8,16},{12,20},{16,24},{20,28},{24,0},{28,4},{32,40},... | collective-permute-start | bytes 1572872 | tf_op jit(solution)/shard_map/ppermute | solution.py:58
  303.7 25.3 %collective-permute-start.2 = (bf16[4,8,8,1024]{3,2,1,0:T(8,128)(2,1)S(1)}, bf16[4,8,8,1024]{3,2,1,0:T(8,128)(2,1)S(1)}, u32[]{:S(2)}, u32[]{:S(2)}) collective-permute-start(bf16[4,8,8,1024]{3,2,1,0:T(8,128)(2,1)S(1)} %get-tuple-element.60), channel_id=1, source_target_pairs={{0,16},{4,20},{8,24},{12,28},{16,0},{20,4},{24,8},{28,12},{32,48},... | collective-permute-start | bytes 1572872 | tf_op jit(solution)/shard_map/ppermute | solution.py:58
  306.4 22.6 %collective-permute-start.3 = (bf16[4,8,8,1024]{3,2,1,0:T(8,128)(2,1)S(1)}, bf16[4,8,8,1024]{3,2,1,0:T(8,128)(2,1)S(1)}, u32[]{:S(2)}, u32[]{:S(2)}) collective-permute-start(bf16[4,8,8,1024]{3,2,1,0:T(8,128)(2,1)S(1)} %get-tuple-element.59), channel_id=1, source_target_pairs={{0,24},{4,28},{8,0},{12,4},{16,8},{20,12},{24,16},{28,20},{32,56},... | collective-permute-start | bytes 1572872 | tf_op jit(solution)/shard_map/ppermute | solution.py:58
  307.9 3.0 copy-start.23
  310.8 4.7 %collective-permute-start.15 = (f32[3,1024]{1,0:T(4,128)S(1)}, f32[3,1024]{1,0:T(4,128)S(1)}, u32[]{:S(2)}, u32[]{:S(2)}) collective-permute-start(f32[3,1024]{1,0:T(4,128)S(1)} %add.340), channel_id=1, source_target_pairs={{0,64},{4,68},{8,72},{12,76},{16,80},{20,84},{24,88},{28,92},{32,9... | collective-permute-start | bytes 36872 | tf_op jit(solution)/shard_map/ppermute | solution.py:77
  315.5 17.0 %copy-start.3 = (f32[4,512,256]{1,2,0:T(8,128)S(1)}, f32[4,512,256]{1,2,0:T(8,128)}, u32[]{:S(2)}) copy-start(f32[4,512,256]{1,2,0:T(8,128)} %copy.211) | copy-start | bytes 6291460
  315.5 21.9 %collective-permute-start.16 = (f32[3,1024]{1,0:T(4,128)S(1)}, f32[3,1024]{1,0:T(4,128)}, u32[]{:S(2)}, u32[]{:S(2)}) collective-permute-start(f32[3,1024]{1,0:T(4,128)S(1)} %add.341), channel_id=1, source_target_pairs={{0,128},{4,132},{8,136},{12,140},{16,144},{20,148},{24,152},{28,15... | collective-permute-start | bytes 36872 | tf_op jit(solution)/shard_map/ppermute | solution.py:77
  329.4 5.0 %copy-start.9 = (f32[4,8,8,1024]{3,2,1,0:T(8,128)}, f32[4,8,8,1024]{3,2,1,0:T(8,128)S(1)}, u32[]{:S(2)}) copy-start(f32[4,8,8,1024]{3,2,1,0:T(8,128)S(1)} %fusion.35) | copy-start | bytes 3145732
  330.3 15.0 %collective-permute-start.10 = (bf16[4,8,1024]{2,1,0:T(8,128)(2,1)}, bf16[4,8,1024]{2,1,0:T(8,128)(2,1)S(1)}, u32[]{:S(2)}, u32[]{:S(2)}) collective-permute-start(bf16[4,8,1024]{2,1,0:T(8,128)(2,1)} %get-tuple-element.66), channel_id=1, source_target_pairs={{0,224},{4,228},{8,232},{12,236},{16,240},{20,244},{24,248},{28,25... | collective-permute-start | bytes 196616 | tf_op jit(solution)/shard_map/ppermute | solution.py:58
  332.5 15.3 %collective-permute-start.4 = (bf16[4,8,1024]{2,1,0:T(8,128)(2,1)}, bf16[4,8,1024]{2,1,0:T(8,128)(2,1)S(1)}, u32[]{:S(2)}, u32[]{:S(2)}) collective-permute-start(bf16[4,8,1024]{2,1,0:T(8,128)(2,1)} %get-tuple-element.61), channel_id=1, source_target_pairs={{0,32},{4,36},{8,40},{12,44},{16,48},{20,52},{24,56},{28,60},{32,6... | collective-permute-start | bytes 196616 | tf_op jit(solution)/shard_map/ppermute | solution.py:58
  334.4 15.9 %copy-start.8 = (f32[256,1024]{1,0:T(8,128)S(1)}, f32[256,1024]{1,0:T(8,128)}, u32[]{:S(2)}) copy-start(f32[256,1024]{1,0:T(8,128)} %get-tuple-element.88) | copy-start | bytes 3145732
  338.7 14.5 %collective-permute-start.5 = (bf16[4,8,1024]{2,1,0:T(8,128)(2,1)}, bf16[4,8,1024]{2,1,0:T(8,128)(2,1)S(1)}, u32[]{:S(2)}, u32[]{:S(2)}) collective-permute-start(bf16[4,8,1024]{2,1,0:T(8,128)(2,1)} %get-tuple-element.65), channel_id=1, source_target_pairs={{0,64},{4,68},{8,72},{12,76},{16,80},{20,84},{24,88},{28,92},{32,9... | collective-permute-start | bytes 196616 | tf_op jit(solution)/shard_map/ppermute | solution.py:58
  338.8 14.5 %collective-permute-start.6 = (bf16[4,8,1024]{2,1,0:T(8,128)(2,1)}, bf16[4,8,1024]{2,1,0:T(8,128)(2,1)S(1)}, u32[]{:S(2)}, u32[]{:S(2)}) collective-permute-start(bf16[4,8,1024]{2,1,0:T(8,128)(2,1)} %get-tuple-element.64), channel_id=1, source_target_pairs={{0,96},{4,100},{8,104},{12,108},{16,112},{20,116},{24,120},{28,124... | collective-permute-start | bytes 196616 | tf_op jit(solution)/shard_map/ppermute | solution.py:58
  341.5 11.8 %collective-permute-start.7 = (bf16[4,8,1024]{2,1,0:T(8,128)(2,1)}, bf16[4,8,1024]{2,1,0:T(8,128)(2,1)S(1)}, u32[]{:S(2)}, u32[]{:S(2)}) collective-permute-start(bf16[4,8,1024]{2,1,0:T(8,128)(2,1)} %get-tuple-element.63), channel_id=1, source_target_pairs={{0,128},{4,132},{8,136},{12,140},{16,144},{20,148},{24,152},{28,15... | collective-permute-start | bytes 196616 | tf_op jit(solution)/shard_map/ppermute | solution.py:58
  345.2 9.0 %collective-permute-start.8 = (bf16[4,8,1024]{2,1,0:T(8,128)(2,1)}, bf16[4,8,1024]{2,1,0:T(8,128)(2,1)S(1)}, u32[]{:S(2)}, u32[]{:S(2)}) collective-permute-start(bf16[4,8,1024]{2,1,0:T(8,128)(2,1)} %get-tuple-element.62), channel_id=1, source_target_pairs={{0,160},{4,164},{8,168},{12,172},{16,176},{20,180},{24,184},{28,18... | collective-permute-start | bytes 196616 | tf_op jit(solution)/shard_map/ppermute | solution.py:58
  347.9 9.1 %collective-permute-start.9 = (bf16[4,8,1024]{2,1,0:T(8,128)(2,1)}, bf16[4,8,1024]{2,1,0:T(8,128)(2,1)S(1)}, u32[]{:S(2)}, u32[]{:S(2)}) collective-permute-start(bf16[4,8,1024]{2,1,0:T(8,128)(2,1)} %get-tuple-element.67), channel_id=1, source_target_pairs={{0,192},{4,196},{8,200},{12,204},{16,208},{20,212},{24,216},{28,22... | collective-permute-start | bytes 196616 | tf_op jit(solution)/shard_map/ppermute | solution.py:58
  350.3 8.3 %copy-start.1 = (bf16[4,512,256]{2,1,0:T(8,128)(2,1)S(1)}, bf16[4,512,256]{2,1,0:T(8,128)(2,1)}, u32[]{:S(2)}) copy-start(bf16[4,512,256]{2,1,0:T(8,128)(2,1)} %param.15) | copy-start | bytes 3145732
  (2 other events, 2.4 us)
